TPU v7x, 512 devices: a whole 4x4x16 slice. The times are simulated.
512 devices in a mesh: pos: 64 (over z, y), mode: 8 (over x, core).
Axes of the slice: x: 4, y: 4, z: 16, core: 2. Of those that a mesh axis runs over, the one named last changes fastest.
Arguments:
- object_field: float32 [2, 8192, 512], P(None, 'pos'), may hold values from -6 to 6
- probe: float32 [2, 8, 256, 256], P(None, 'mode'), may hold values from -3 to 3
- measured: float32 [192, 256, 256], P('pos'), may hold values from 0 to 16
- row_offsets: int32 [192], P('pos'), may hold values from 0 to 127
- col_offsets: int32 [192], P('pos'), may hold values from 0 to 256
- tile_counts: int32 [64], P('pos'), may hold values from 1 to 3, 96 in all
Outputs:
- updated_object: float32 [2, 8192, 512], P(None, ('pos', 'mode'))
Inputs may be any that keep to these rules, and one draw needn't show every extreme that they name: Slots 0 to tile_counts[t] - 1 of tile t hold scan positions, the others are empty; the counts sum to 96 and the largest equals 3.
All inputs are finite; a program needn't handle non-finite values. No bound on the sum of `tile_counts` on one device may be relied on, other than what follows from the above.
Results may differ from a plain program's by a relative error of at most 0.0016.
Values sent between devices are 32-bit elements; how exact they have to be, the bound alone decides.
No kernel may reach another device: no remote copies, remote signals or barrier semaphores. Data moves between devices by JAX's collectives and lax.ppermute only.
A program may use at most 64 MiB of HBM per device.

v0:
```python
import math

import jax
import jax.numpy as jnp
from jax import lax
from jax.sharding import PartitionSpec as P


def extended_2(array, sides, width):
    for axis, dim in sides:
        size, length = (lax.axis_size(axis), array.shape[dim])
        up = [(i, (i + 1) % size) for i in range(size - 1)]
        down = [(j, i) for i, j in up]
        last = lax.slice_in_dim(array, length - width, length, axis=dim)
        first = lax.slice_in_dim(array, 0, width, axis=dim)
        before = lax.ppermute(last, axis, up)
        after = lax.ppermute(first, axis, down)
        array = jnp.concatenate([before, array, after], axis=dim)
    return array


def dft_tables(pattern):
    counter = jnp.arange(pattern, dtype=jnp.int32)
    phases = counter[:, None] * counter[None, :] % pattern
    angles = phases.astype(jnp.float32) * (2.0 * math.pi / pattern)
    factor = 1.0 / math.sqrt(pattern)
    return (
        (jnp.cos(angles) * factor).astype(jnp.bfloat16),
        (-jnp.sin(angles) * factor).astype(jnp.bfloat16),
    )


def left_product(table, stacked):
    return jnp.einsum("ua,kab->kub", table, stacked, preferred_element_type=jnp.float32)


def right_product(stacked, table):
    return jnp.einsum("kub,bv->kuv", stacked, table, preferred_element_type=jnp.float32)


def local(object_field, probe, measured, row_offsets, col_offsets, tile_counts):
    rows_tile = object_field.shape[1]
    columns = object_field.shape[2]
    pattern = probe.shape[2]
    slot_count = measured.shape[0]
    mode_count = lax.axis_size("mode")
    my_mode = lax.axis_index("mode")
    share_rows = rows_tile // mode_count
    real_table, imag_table = dft_tables(pattern)
    anchor = jnp.zeros((), jnp.int32)
    extended = extended_2(object_field, (("pos", 1),), rows_tile)
    probe_re = probe[0]
    probe_im = probe[1]
    top_rows = rows_tile + row_offsets - pattern // 2

    def forward(position):
        window = lax.dynamic_slice(
            extended, (anchor, top_rows[position], col_offsets[position]), (2, pattern, pattern)
        )
        exit_re = (probe_re * window[0] - probe_im * window[1]).astype(jnp.bfloat16)
        exit_im = (probe_re * window[1] + probe_im * window[0]).astype(jnp.bfloat16)
        half_re = (left_product(real_table, exit_re) - left_product(imag_table, exit_im)).astype(
            jnp.bfloat16
        )
        half_im = (left_product(real_table, exit_im) + left_product(imag_table, exit_re)).astype(
            jnp.bfloat16
        )
        wave_re = right_product(half_re, real_table) - right_product(half_im, imag_table)
        wave_im = right_product(half_re, imag_table) + right_product(half_im, real_table)
        return (exit_re, exit_im, wave_re, wave_im)

    exit_re, exit_im, wave_re, wave_im = lax.map(forward, jnp.arange(slot_count, dtype=jnp.int32))
    power_sum = jnp.sum(wave_re * wave_re + wave_im * wave_im, axis=1)
    model_power = lax.psum(power_sum, "mode")
    scaling = jnp.sqrt(measured) / jnp.maximum(jnp.sqrt(model_power), 1.0)
    probe_power = jnp.sum(probe_re * probe_re + probe_im * probe_im, axis=0)
    live_count = tile_counts[0]

    def backward(position, buffer):
        fixed_re = (scaling[position] * wave_re[position]).astype(jnp.bfloat16)
        fixed_im = (scaling[position] * wave_im[position]).astype(jnp.bfloat16)
        back_re = (left_product(real_table, fixed_re) + left_product(imag_table, fixed_im)).astype(
            jnp.bfloat16
        )
        back_im = (left_product(real_table, fixed_im) - left_product(imag_table, fixed_re)).astype(
            jnp.bfloat16
        )
        delta_re = (
            right_product(back_re, real_table)
            + right_product(back_im, imag_table)
            - exit_re[position].astype(jnp.float32)
        )
        delta_im = (
            right_product(back_im, real_table)
            - right_product(back_re, imag_table)
            - exit_im[position].astype(jnp.float32)
        )
        numer_re = jnp.sum(probe_re * delta_re + probe_im * delta_im, axis=0)
        numer_im = jnp.sum(probe_re * delta_im - probe_im * delta_re, axis=0)
        contrib = jnp.stack([numer_re, numer_im, probe_power])
        contrib = jnp.where(position < live_count, contrib, jnp.zeros_like(contrib))
        corner = (anchor, top_rows[position], col_offsets[position])
        current = lax.dynamic_slice(buffer, corner, (3, pattern, pattern))
        return lax.dynamic_update_slice(buffer, current + contrib, corner)

    buffer = lax.fori_loop(
        0, slot_count, backward, jnp.zeros((3, 3 * rows_tile, columns), jnp.float32)
    )
    outside = jnp.concatenate([buffer[:, :rows_tile], buffer[:, 2 * rows_tile :]], axis=1)
    framed_sum = extended_2(outside, (("pos", 1),), rows_tile)
    tile_sum = (
        buffer[:, rows_tile : 2 * rows_tile]
        + framed_sum[:, :rows_tile]
        + framed_sum[:, 3 * rows_tile :]
    )
    update_sum = lax.psum_scatter(tile_sum, "mode", scatter_dimension=1, tiled=True)
    own_rows = lax.dynamic_slice_in_dim(object_field, my_mode * share_rows, share_rows, 1)
    return own_rows + update_sum[:2] / (update_sum[2] + 1.0)


def solution(mesh):
    in_specs = (
        P(None, "pos", None),
        P(None, "mode", None, None),
        P("pos", None, None),
        P("pos"),
        P("pos"),
        P("pos"),
    )
    out_specs = P(None, ("pos", "mode"), None)
    return jax.shard_map(local, mesh=mesh, in_specs=in_specs, out_specs=out_specs, check_vma=False)
```

profile of v0, /device:TPU:16, one launch (start us, length us, event | category | flops | bytes accessed | tf_op | source)
XLA Modules:
  0.0 350.2 jit_solution(2317298614045170838)
XLA Ops:
  6.5 3.3 collective-permute-start
  9.9 2.7 collective-permute-start.1
  14.5 8.0 %collective-permute-done = f32[2,128,512]{2,1,0:T(8,128)S(1)} collective-permute-done((f32[2,128,512]{2,1,0:T(8,128)}, f32[2,128,512]{2,1,0:T(8,128)S(1)}, u32[]{:S(2)}, u32[]{:S(2)}) %collective-permute-start) | collective-permute-done | bytes 524320 | tf_op jit(solution)/shard_map/ppermute | solution.py:16
  22.4 2.9 collective-permute-done.1
  26.6 60.4 %while.33 = (s32[]{:T(128)}, bf16[3,1,256,256]{3,2,1,0:T(8,128)(2,1)}, bf16[3,1,256,256]{3,2,1,0:T(8,128)(2,1)}, f32[3,1,256,256]{3,2,1,0:T(8,128)}, f32[3,1,256...) while((s32[]{:T(128)}, ...), condition=%wide.region_1.2_spmd.clone.clone, body=%wide.region_0.1_spmd.clone.clone.sunk | while | flops 278003712 | bytes 5506879 | solution.py:72
  74.4 2.0 bitcast_dynamic-update-slice_fusion.3
  86.9 2.5 fusion.136
  89.6 83.3 %all-reduce.2.cloned.1.call-done = f32[3,256,256]{2,1,0:T(8,128)} async-done(((f32[3,256,256]{2,1,0:T(8,128)}), f32[3,256,256]{2,1,0:T(8,128)}) %all-reduce.2.cloned.1.call-update) | async-done | bytes 786448 | tf_op jit(solution)/shard_map/psum | solution.py:74
  172.9 2.5 maximum_divide_fusion
  175.7 98.4 %while.34 = (s32[]{:T(128)}, f32[3,384,512]{2,1,0:T(8,128)S(1)}, s32[3]{0:T(128)S(1)}, s32[3]{0:T(128)S(1)}, s32[]{:T(128)}, /*index=5*/f32[1,256,256]{2,1,0:T(8...) while((s32[]{:T(128)}, f32[3,384,512]{2,1,0:T(8,128)S(1)}, ...), condition=%wide.region_4.5_spmd.clone.clone, body=%wide.region_3.4_spmd.clone.clone.sunk | while | flops 279183360 | bytes 10223899 | solution.py:106
  182.6 2.1 fusion.216
  185.8 3.1 fusion.218
  196.3 13.3 %dynamic_update_slice.42 = f32[3,384,512]{2,1,0:T(8,128)S(1)} dynamic-update-slice(f32[3,384,512]{2,1,0:T(8,128)S(1)} %get-tuple-element.786, f32[3,256,256]{2,1,0:T(8,128)S(1)} %fusion.219, s32[]{:T(128)} %constant.88.clone.1..sunk.1, s32[]{:T(128)S(6)} %select_n.210, s32[]{:T(128)S(6)} %select_n.211) | dynamic-update-slice | bytes 1572868 | tf_op jit(solution)/shard_map/while/body/eval_jaxpr/dynamic_update_slice | solution.py:104
  216.5 2.1 fusion.216
  219.8 3.1 fusion.218
  230.3 11.5 %dynamic_update_slice.42 = f32[3,384,512]{2,1,0:T(8,128)S(1)} dynamic-update-slice(f32[3,384,512]{2,1,0:T(8,128)S(1)} %get-tuple-element.786, f32[3,256,256]{2,1,0:T(8,128)S(1)} %fusion.219, s32[]{:T(128)} %constant.88.clone.1..sunk.1, s32[]{:T(128)S(6)} %select_n.210, s32[]{:T(128)S(6)} %select_n.211) | dynamic-update-slice | bytes 1572868 | tf_op jit(solution)/shard_map/while/body/eval_jaxpr/dynamic_update_slice | solution.py:104
  248.7 2.1 fusion.216
  251.9 3.1 fusion.218
  262.4 11.7 %dynamic_update_slice.42 = f32[3,384,512]{2,1,0:T(8,128)S(1)} dynamic-update-slice(f32[3,384,512]{2,1,0:T(8,128)S(1)} %get-tuple-element.786, f32[3,256,256]{2,1,0:T(8,128)S(1)} %fusion.219, s32[]{:T(128)} %constant.88.clone.1..sunk.1, s32[]{:T(128)S(6)} %select_n.210, s32[]{:T(128)S(6)} %select_n.211) | dynamic-update-slice | bytes 1572868 | tf_op jit(solution)/shard_map/while/body/eval_jaxpr/dynamic_update_slice | solution.py:104
  274.3 2.8 collective-permute-start.2
  277.2 3.0 collective-permute-start.3
  280.2 13.3 %collective-permute-done.2 = f32[3,128,512]{2,1,0:T(8,128)S(1)} collective-permute-done((f32[3,128,512]{2,1,0:T(8,128)S(1)}, f32[3,128,512]{2,1,0:T(8,128)S(1)}, u32[]{:S(2)}, u32[]{:S(2)}) %collective-permute-start.2) | collective-permute-done | bytes 786464 | tf_op jit(solution)/shard_map/ppermute | solution.py:16
  293.5 2.5 collective-permute-done.3
  297.2 43.9 %reduce-scatter.2.cloned.1.call-done = f32[3,16,512]{2,1,0:T(8,128)} async-done(((f32[3,128,512]{2,1,0:T(8,128)}), f32[3,16,512]{2,1,0:T(8,128)}) %reduce-scatter.2.cloned.1.call-update) | async-done | bytes 98320 | tf_op jit(solution)/shard_map/reduce_scatter | solution.py:116
  (87 shorter events, 80.3 us)
Async XLA Ops:
  6.5 20.0 %copy-start.1 = (s32[3]{0:T(128)S(1)}, s32[3]{0:T(128)}, u32[]{:S(2)}) copy-start(s32[3]{0:T(128)} %param.13) | copy-start | bytes 40
  6.5 20.0 %copy-start.2 = (s32[3]{0:T(128)S(1)}, s32[3]{0:T(128)}, u32[]{:S(2)}) copy-start(s32[3]{0:T(128)} %param.14) | copy-start | bytes 40
  6.5 166.4 %all-reduce.2.cloned.1.call-start = ((), (), s32[]{:S(2)}) async-start(), calls=%async_computation.1 | async-start | bytes 1572864 | tf_op jit(solution)/shard_map/psum | solution.py:74
  6.5 15.9 %collective-permute-start = (f32[2,128,512]{2,1,0:T(8,128)}, f32[2,128,512]{2,1,0:T(8,128)S(1)}, u32[]{:S(2)}, u32[]{:S(2)}) collective-permute-start(f32[2,128,512]{2,1,0:T(8,128)} %param.10), channel_id=1, source_target_pairs={{0,8},{8,16},{16,24},{24,32},{32,40},{40,48},{48,56},{56,64},{64,7... | collective-permute-start | bytes 1572872 | tf_op jit(solution)/shard_map/ppermute | solution.py:16
  9.9 15.5 %collective-permute-start.1 = (f32[2,128,512]{2,1,0:T(8,128)}, f32[2,128,512]{2,1,0:T(8,128)S(1)}, u32[]{:S(2)}, u32[]{:S(2)}) collective-permute-start(f32[2,128,512]{2,1,0:T(8,128)} %param.10), channel_id=1, source_target_pairs={{8,0},{16,8},{24,16},{32,24},{40,32},{48,40},{56,48},{64,56},{72,6... | collective-permute-start | bytes 1572872 | tf_op jit(solution)/shard_map/ppermute | solution.py:17
  86.9 86.0 %copy-start = (f32[3,256,256]{2,1,0:T(8,128)S(1)}, f32[3,256,256]{2,1,0:T(8,128)}, u32[]{:S(2)}) copy-start(f32[3,256,256]{2,1,0:T(8,128)} %param.12) | copy-start | bytes 2359300
  89.4 251.7 %reduce-scatter.2.cloned.1.call-start = ((), (), s32[]{:S(2)}) async-start(), calls=%async_computation.2 | async-start | bytes 884736 | tf_op jit(solution)/shard_map/reduce_scatter | solution.py:116
  274.3 19.1 %collective-permute-start.2 = (f32[3,128,512]{2,1,0:T(8,128)S(1)}, f32[3,128,512]{2,1,0:T(8,128)S(1)}, u32[]{:S(2)}, u32[]{:S(2)}) collective-permute-start(f32[3,128,512]{2,1,0:T(8,128)S(1)} %get-tuple-element.550), channel_id=1, source_target_pairs={{0,8},{8,16},{16,24},{24,32},{32,40},{40,48},{48,56},{56,64},{64,7... | collective-permute-start | bytes 2359304 | tf_op jit(solution)/shard_map/ppermute | solution.py:16
  277.2 18.9 %collective-permute-start.3 = (f32[3,128,512]{2,1,0:T(8,128)S(1)}, f32[3,128,512]{2,1,0:T(8,128)S(1)}, u32[]{:S(2)}, u32[]{:S(2)}) collective-permute-start(f32[3,128,512]{2,1,0:T(8,128)S(1)} %get-tuple-element.551), channel_id=1, source_target_pairs={{8,0},{16,8},{24,16},{32,24},{40,32},{48,40},{56,48},{64,56},{72,6... | collective-permute-start | bytes 2359304 | tf_op jit(solution)/shard_map/ppermute | solution.py:17
Sparse Core Ops, SparseCore 0:
  89.5 83.3 all-reduce.1
  297.3 43.7 reduce-scatter.1
where the time goes:
time: 351 us; the launch traced here: 350 us
  waiting for transfers between devices  154 us (44%)
  matrix products  67.6 us (19%)
  local copies, waits for them, and re-layouts  46.6 us (13%)
  loops' own time  31.8 us (9%)
  other arithmetic  24.7 us (7%)
  between operations  13.5 us (4%)
  starting transfers between devices  12 us (3%)
    psum x1, waiting for transfers between devices, local(): model_power = lax.psum(power_sum, 'mode')  83.3 us
    reduce_scatter x1, waiting for transfers between devices, local(): lax.psum_scatter(tile_sum, 'mode', scatter_dimension=1, tiled=True)  43.9 us
    dot_general x24, matrix products, right_product(): jnp.einsum('kub,bv->kuv', stacked, table, preferred_element_type=jnp.floa...  40.3 us
    dynamic_update_slice x3, local copies, waits for them, and re-layouts, backward(): return lax.dynamic_update_slice(buffer, current + contrib, corner)  36.5 us
    dot_general x24, matrix products, left_product(): jnp.einsum('ua,kab->kub', table, stacked, preferred_element_type=jnp.floa...  27.3 us
    ppermute x2, waiting for transfers between devices, extended_2(): before = lax.ppermute(last, axis, up)  21.3 us
    another operation x1, loops' own time, local(): lax.map(forward, jnp.arange(slot_count, dtype=jnp.int32))  17.2 us
    another operation x1, loops' own time, local(): lax.fori_loop(0, slot_count, backward, jnp.zeros((3, 3 * rows_tile, colum...  14.6 us
  transfers between devices with their start and end apart: 6, of which 6 were waited for; matrix products, arithmetic and copies ran while one was open for 1% of the time, Pallas kernels for 0%

commit v1 on v0

v1 whole, which is shorter than its diff:
```python
import math

import jax
import jax.numpy as jnp
from jax import lax
from jax.experimental import pallas as pl
from jax.experimental.pallas import tpu as pltpu
from jax.sharding import PartitionSpec as P


def dft_tables(pattern):
    counter = jnp.arange(pattern, dtype=jnp.int32)
    phases = counter[:, None] * counter[None, :] % pattern
    angles = phases.astype(jnp.float32) * (2.0 * math.pi / pattern)
    factor = 1.0 / math.sqrt(pattern)
    return (
        (jnp.cos(angles) * factor).astype(jnp.bfloat16),
        (-jnp.sin(angles) * factor).astype(jnp.bfloat16),
    )


def neighbour_pairs(size, step):
    if step > 0:
        return [(i, i + 1) for i in range(size - 1)]
    return [(i + 1, i) for i in range(size - 1)]


def allreduce_mode(x):
    n = lax.axis_size("mode")
    d = 1
    while d < n:
        x = x + lax.ppermute(x, "mode", [(i, i ^ d) for i in range(n)])
        d *= 2
    return x


def reduce_scatter_mode(x):
    n = lax.axis_size("mode")
    k = n.bit_length() - 1
    m = lax.axis_index("mode")
    c, rows, w = x.shape
    x = x.reshape((c,) + (2,) * k + (rows // n, w))
    for i in range(k):
        d = 1 << i
        dim = k - i
        bit = (m // d) % 2
        keep = lax.dynamic_index_in_dim(x, bit, axis=dim, keepdims=False)
        send = lax.dynamic_index_in_dim(x, 1 - bit, axis=dim, keepdims=False)
        x = keep + lax.ppermute(send, "mode", [(j, j ^ d) for j in range(n)])
    return x.reshape(c, rows // n, w)


def _dot(a, b):
    return jnp.dot(a, b, preferred_element_type=jnp.float32)


def forward_kernel(roff, coff, cnt, ext_ref, probe_ref, fr_ref, fi_ref, exit_ref, wave_ref, power_ref):
    j = pl.program_id(0)
    pat = probe_ref.shape[1]
    width = ext_ref.shape[2]
    live = j < cnt[0]

    @pl.when(live)
    def _():
        r = roff[j]
        base = pl.multiple_of((r // 8) * 8, 8)
        span = pat + 8
        down = (span - (r - base)) % span
        shift = (width - coff[j]) % width

        def window(k):
            rows = pltpu.roll(ext_ref[k, pl.ds(base, span), :], down, 0)[:pat]
            return pltpu.roll(rows, shift, 1)[:, :pat]

        obj_re = window(0)
        obj_im = window(1)
        p_re = probe_ref[0]
        p_im = probe_ref[1]
        e_re = (p_re * obj_re - p_im * obj_im).astype(jnp.bfloat16)
        e_im = (p_re * obj_im + p_im * obj_re).astype(jnp.bfloat16)
        fr = fr_ref[...]
        fi = fi_ref[...]
        h_re = (_dot(fr, e_re) - _dot(fi, e_im)).astype(jnp.bfloat16)
        h_im = (_dot(fr, e_im) + _dot(fi, e_re)).astype(jnp.bfloat16)
        v_re = _dot(h_re, fr) - _dot(h_im, fi)
        v_im = _dot(h_re, fi) + _dot(h_im, fr)
        exit_ref[0, 0] = e_re
        exit_ref[0, 1] = e_im
        wave_ref[0, 0] = v_re
        wave_ref[0, 1] = v_im
        power_ref[0] = v_re * v_re + v_im * v_im

    @pl.when(jnp.logical_not(live))
    def _():
        power_ref[...] = jnp.zeros(power_ref.shape, jnp.float32)


def backward_kernel(roff, coff, cnt, exit_ref, wave_ref, model_ref, meas_ref, probe_ref, ppt_ref,
                    fr_ref, fi_ref, numer_ref, illum_ref):
    j = pl.program_id(0)
    pat = probe_ref.shape[1]
    width = numer_ref.shape[2]

    @pl.when(j == 0)
    def _():
        numer_ref[...] = jnp.zeros(numer_ref.shape, jnp.float32)
        illum_ref[...] = jnp.zeros(illum_ref.shape, jnp.float32)

    @pl.when(j < cnt[0])
    def _():
        r = roff[j]
        c = coff[j]
        base = pl.multiple_of((r // 8) * 8, 8)
        span = pat + 8
        v_re = wave_ref[0, 0]
        v_im = wave_ref[0, 1]
        scaling = jnp.sqrt(meas_ref[0]) / jnp.maximum(jnp.sqrt(model_ref[0]), 1.0)
        x_re = (scaling * v_re).astype(jnp.bfloat16)
        x_im = (scaling * v_im).astype(jnp.bfloat16)
        fr = fr_ref[...]
        fi = fi_ref[...]
        b_re = (_dot(fr, x_re) + _dot(fi, x_im)).astype(jnp.bfloat16)
        b_im = (_dot(fr, x_im) - _dot(fi, x_re)).astype(jnp.bfloat16)
        d_re = _dot(b_re, fr) + _dot(b_im, fi) - exit_ref[0, 0].astype(jnp.float32)
        d_im = _dot(b_im, fr) - _dot(b_re, fi) - exit_ref[0, 1].astype(jnp.float32)
        p_re = probe_ref[0]
        p_im = probe_ref[1]
        n_re = p_re * d_re + p_im * d_im
        n_im = p_re * d_im - p_im * d_re
        pad = jnp.zeros((pat, width - pat), jnp.float32)
        pad_rows = jnp.zeros((span - pat, width), jnp.float32)

        def place(a):
            wide = pltpu.roll(jnp.concatenate([a, pad], axis=1), c, 1)
            return pltpu.roll(jnp.concatenate([wide, pad_rows], axis=0), r - base, 0)

        numer_ref[0, pl.ds(base, span), :] += place(n_re)
        numer_ref[1, pl.ds(base, span), :] += place(n_im)
        illum_ref[pl.ds(base, span), :] += place(ppt_ref[...])


def run_forward(ext, probe2, fr, fi, roff, coff, cnt):
    slots = roff.shape[0]
    pat = probe2.shape[1]
    whole3 = lambda j, *_: (0, 0, 0)
    whole2 = lambda j, *_: (0, 0)
    per4 = lambda j, *_: (j, 0, 0, 0)
    per3 = lambda j, *_: (j, 0, 0)
    flops = slots * 8 * 2 * pat ** 3
    return pl.pallas_call(
        forward_kernel,
        grid_spec=pltpu.PrefetchScalarGridSpec(
            num_scalar_prefetch=3,
            grid=(slots,),
            in_specs=[
                pl.BlockSpec(ext.shape, whole3),
                pl.BlockSpec(probe2.shape, whole3),
                pl.BlockSpec(fr.shape, whole2),
                pl.BlockSpec(fi.shape, whole2),
            ],
            out_specs=[
                pl.BlockSpec((1, 2, pat, pat), per4),
                pl.BlockSpec((1, 2, pat, pat), per4),
                pl.BlockSpec((1, pat, pat), per3),
            ],
        ),
        out_shape=[
            jax.ShapeDtypeStruct((slots, 2, pat, pat), jnp.bfloat16),
            jax.ShapeDtypeStruct((slots, 2, pat, pat), jnp.float32),
            jax.ShapeDtypeStruct((slots, pat, pat), jnp.float32),
        ],
        compiler_params=pltpu.CompilerParams(dimension_semantics=("arbitrary",)),
        cost_estimate=pl.CostEstimate(flops=flops, transcendentals=0, bytes_accessed=8 * 1024 * 1024),
    )(roff, coff, cnt, ext, probe2, fr, fi)


def run_backward(exits, waves, model, measured, probe2, ppt, fr, fi, roff, coff, cnt, ext_rows, width):
    slots = roff.shape[0]
    pat = probe2.shape[1]
    whole3 = lambda j, *_: (0, 0, 0)
    whole2 = lambda j, *_: (0, 0)
    per4 = lambda j, *_: (j, 0, 0, 0)
    per3 = lambda j, *_: (j, 0, 0)
    flops = slots * 8 * 2 * pat ** 3
    return pl.pallas_call(
        backward_kernel,
        grid_spec=pltpu.PrefetchScalarGridSpec(
            num_scalar_prefetch=3,
            grid=(slots,),
            in_specs=[
                pl.BlockSpec((1, 2, pat, pat), per4),
                pl.BlockSpec((1, 2, pat, pat), per4),
                pl.BlockSpec((1, pat, pat), per3),
                pl.BlockSpec((1, pat, pat), per3),
                pl.BlockSpec(probe2.shape, whole3),
                pl.BlockSpec(ppt.shape, whole2),
                pl.BlockSpec(fr.shape, whole2),
                pl.BlockSpec(fi.shape, whole2),
            ],
            out_specs=[
                pl.BlockSpec((2, ext_rows, width), whole3),
                pl.BlockSpec((ext_rows, width), whole2),
            ],
        ),
        out_shape=[
            jax.ShapeDtypeStruct((2, ext_rows, width), jnp.float32),
            jax.ShapeDtypeStruct((ext_rows, width), jnp.float32),
        ],
        compiler_params=pltpu.CompilerParams(dimension_semantics=("arbitrary",)),
        cost_estimate=pl.CostEstimate(flops=flops, transcendentals=0, bytes_accessed=12 * 1024 * 1024),
    )(roff, coff, cnt, exits, waves, model, measured, probe2, ppt, fr, fi)


def local(object_field, probe, measured, row_offsets, col_offsets, tile_counts):
    rows_tile = object_field.shape[1]
    width = object_field.shape[2]
    pos_count = lax.axis_size("pos")
    mode_count = lax.axis_size("mode")
    my_mode = lax.axis_index("mode")
    share_rows = rows_tile // mode_count
    pattern = probe.shape[2]
    fr, fi = dft_tables(pattern)
    probe2 = probe[:, 0]

    probe_power = allreduce_mode(probe2[0] * probe2[0] + probe2[1] * probe2[1])

    before = lax.ppermute(object_field, "pos", neighbour_pairs(pos_count, 1))
    after = lax.ppermute(object_field, "pos", neighbour_pairs(pos_count, -1))
    ext = jnp.concatenate([before, object_field, after], axis=1)
    ext_rows = ext.shape[1]

    roff = row_offsets.astype(jnp.int32)
    coff = col_offsets.astype(jnp.int32)
    cnt = tile_counts.astype(jnp.int32)

    exits, waves, power = run_forward(ext, probe2, fr, fi, roff, coff, cnt)
    model = allreduce_mode(power)
    numer, illum = run_backward(
        exits, waves, model, measured, probe2, probe_power, fr, fi, roff, coff, cnt, ext_rows, width
    )

    top = numer[:, :rows_tile]
    mid = numer[:, rows_tile : 2 * rows_tile]
    bottom = numer[:, 2 * rows_tile :]
    tile_numer = (
        mid
        + lax.ppermute(bottom, "pos", neighbour_pairs(pos_count, 1))
        + lax.ppermute(top, "pos", neighbour_pairs(pos_count, -1))
    )
    numer_rows = reduce_scatter_mode(tile_numer)

    start = my_mode * share_rows
    illum_top = lax.dynamic_slice_in_dim(illum, start, share_rows, 0)
    illum_mid = lax.dynamic_slice_in_dim(illum, rows_tile + start, share_rows, 0)
    illum_bottom = lax.dynamic_slice_in_dim(illum, 2 * rows_tile + start, share_rows, 0)
    illum_rows = (
        illum_mid
        + lax.ppermute(illum_bottom, "pos", neighbour_pairs(pos_count, 1))
        + lax.ppermute(illum_top, "pos", neighbour_pairs(pos_count, -1))
    )

    own_rows = lax.dynamic_slice_in_dim(object_field, start, share_rows, 1)
    return own_rows + numer_rows / (illum_rows + 1.0)


def solution(mesh):
    in_specs = (
        P(None, "pos", None),
        P(None, "mode", None, None),
        P("pos", None, None),
        P("pos"),
        P("pos"),
        P("pos"),
    )
    out_specs = P(None, ("pos", "mode"), None)
    return jax.shard_map(local, mesh=mesh, in_specs=in_specs, out_specs=out_specs, check_vma=False)
```

time: 351 us -> 151 us (0.43)
  the two profiles are of different devices: /device:TPU:16 before, /device:TPU:256 now
where the time goes in v1:
time: 151 us; the launch traced here: 150 us
  waiting for transfers between devices  67.8 us (45%)
  starting transfers between devices  56.2 us (37%)
  Pallas kernels  12.2 us (8%)
  other arithmetic  10.7 us (7%)
  local copies, waits for them, and re-layouts  2.14 us (1%)
    ppermute x6, waiting for transfers between devices, allreduce_mode(): x = x + lax.ppermute(x, 'mode', [(i, i ^ d) for i in range(n)])  45 us
    ppermute x6, starting transfers between devices, allreduce_mode(): x = x + lax.ppermute(x, 'mode', [(i, i ^ d) for i in range(n)])  18.7 us
    ppermute x3, starting transfers between devices, reduce_scatter_mode(): x = keep + lax.ppermute(send, 'mode', [(j, j ^ d) for j in range(n)])  8.35 us
    ppermute x1, waiting for transfers between devices, local(): lax.ppermute(bottom, 'pos', neighbour_pairs(pos_count, 1))  7.59 us
    ppermute x1, waiting for transfers between devices, local(): before = lax.ppermute(object_field, 'pos', neighbour_pairs(pos_count, 1))  7.52 us
    ppermute x1, starting transfers between devices, local(): lax.ppermute(illum_top, 'pos', neighbour_pairs(pos_count, -1))  7.52 us
    ppermute x1, starting transfers between devices, local(): lax.ppermute(top, 'pos', neighbour_pairs(pos_count, -1))  7.44 us
    pallas_call x1, Pallas kernels, run_backward(): pl.pallas_call(backward_kernel, grid_spec=pltpu.PrefetchScalarGridSpec(nu...  6.77 us
  transfers between devices with their start and end apart: 15, of which 10 were waited for; matrix products, arithmetic and copies ran while one was open for 3% of the time, Pallas kernels for 0%

profile of v1, /device:TPU:256, one launch (start us, length us, event | category | flops | bytes accessed | tf_op | source)
XLA Modules:
  0.0 150.0 jit_solution(12026438116240571859)
XLA Ops:
  0.0 3.5 %collective-permute-start = (f32[2,128,512]{2,1,0:T(8,128)}, f32[2,128,512]{2,1,0:T(8,128)S(1)}, u32[]{:S(2)}, u32[]{:S(2)}) collective-permute-start(f32[2,128,512]{2,1,0:T(8,128)} %param.6), channel_id=1, source_target_pairs={{0,8},{8,16},{16,24},{24,32},{32,40},{40,48},{48,56},{56,64},{64,7... | collective-permute-start | bytes 1572872 | tf_op jit(solution)/shard_map/ppermute | solution.py:227
  3.5 5.7 %collective-permute-start.1 = (f32[2,128,512]{2,1,0:T(8,128)}, f32[2,128,512]{2,1,0:T(8,128)S(1)}, u32[]{:S(2)}, u32[]{:S(2)}) collective-permute-start(f32[2,128,512]{2,1,0:T(8,128)} %param.6), channel_id=1, source_target_pairs={{8,0},{16,8},{24,16},{32,24},{40,32},{48,40},{56,48},{64,56},{72,6... | collective-permute-start | bytes 1572872 | tf_op jit(solution)/shard_map/ppermute | solution.py:228
  11.6 7.5 %collective-permute-done = f32[2,128,512]{2,1,0:T(8,128)S(1)} collective-permute-done((f32[2,128,512]{2,1,0:T(8,128)}, f32[2,128,512]{2,1,0:T(8,128)S(1)}, u32[]{:S(2)}, u32[]{:S(2)}) %collective-permute-start) | collective-permute-done | bytes 524320 | tf_op jit(solution)/shard_map/ppermute | solution.py:227
  20.4 2.3 %pad_maximum_fusion.ext_ref = f32[2,384,512]{2,1,0:T(8,128)} fusion(f32[2,128,512]{2,1,0:T(8,128)S(1)} %collective-permute-done.1, f32[2,128,512]{2,1,0:T(8,128)} %param.6, f32[2,128,512]{2,1,0:T(8,128)S(1)} %collective-permute-done), kind=kLoop, calls=%fused_computation | loop fusion | flops 786432 | bytes 3145728 | tf_op jit(solution)/shard_map/concatenate | solution.py:229
  22.7 5.4 %shard_map.64 = (bf16[3,2,256,256]{3,2,1,0:T(8,128)(2,1)}, f32[3,2,256,256]{3,2,1,0:T(8,128)}, f32[3,256,256]{2,1,0:T(8,128)}) custom-call(s32[3]{0:T(128)} %roff.3, s32[3]{0:T(128)} %coff.3, s32[1]{0:T(128)S(6)} %copy.12.cnt, f32[2,384,512]{2,1,0:T(8,128)} %pad_maximum_fusion.ext_ref, f32[2,256,256]{2,1,0:T(8,128)} %bitcast.23, ...), custom_call_target="tpu_custom_call" | custom-call | flops 805306368 | bytes 8388608 | tf_op jit(solution)/shard_map/pallas_call | solution.py:150
  28.1 2.0 %collective-permute-start.2 = (f32[3,256,256]{2,1,0:T(8,128)}, f32[3,256,256]{2,1,0:T(8,128)S(1)}, u32[]{:S(2)}, u32[]{:S(2)}) collective-permute-start(f32[3,256,256]{2,1,0:T(8,128)} %get-tuple-element.12), channel_id=1, source_target_pairs={{0,1},{1,0},{2,3},{3,2},{4,5},{5,4},{6,7},{7,6},{8,9},{9,8},{10,11... | collective-permute-start | bytes 2359304 | tf_op jit(solution)/shard_map/ppermute | solution.py:32
  30.1 2.5 %collective-permute-done.2 = f32[3,256,256]{2,1,0:T(8,128)S(1)} collective-permute-done((f32[3,256,256]{2,1,0:T(8,128)}, f32[3,256,256]{2,1,0:T(8,128)S(1)}, u32[]{:S(2)}, u32[]{:S(2)}) %collective-permute-start.2) | collective-permute-done | bytes 786464 | tf_op jit(solution)/shard_map/ppermute | solution.py:32
  33.8 3.4 %collective-permute-start.3 = (f32[3,256,256]{2,1,0:T(8,128)S(1)}, f32[3,256,256]{2,1,0:T(8,128)S(1)}, u32[]{:S(2)}, u32[]{:S(2)}) collective-permute-start(f32[3,256,256]{2,1,0:T(8,128)S(1)} %add.125), channel_id=1, source_target_pairs={{0,2},{1,3},{2,0},{3,1},{4,6},{5,7},{6,4},{7,5},{8,10},{9,11},{10,... | collective-permute-start | bytes 2359304 | tf_op jit(solution)/shard_map/ppermute | solution.py:32
  37.3 1.9 %collective-permute-start.5 = (f32[256,256]{1,0:T(8,128)S(1)}, f32[256,256]{1,0:T(8,128)S(1)}, u32[]{:S(2)}, u32[]{:S(2)}) collective-permute-start(f32[256,256]{1,0:T(8,128)S(1)} %add_bitcast_fusion), channel_id=1, source_target_pairs={{0,1},{1,0},{2,3},{3,2},{4,5},{5,4},{6,7},{7,6},{8,9},{9,8},{10,11... | collective-permute-start | bytes 786440 | tf_op jit(solution)/shard_map/ppermute | solution.py:32
  39.2 16.1 %collective-permute-done.3 = f32[3,256,256]{2,1,0:T(8,128)S(1)} collective-permute-done((f32[3,256,256]{2,1,0:T(8,128)S(1)}, f32[3,256,256]{2,1,0:T(8,128)S(1)}, u32[]{:S(2)}, u32[]{:S(2)}) %collective-permute-start.3) | collective-permute-done | bytes 786464 | tf_op jit(solution)/shard_map/ppermute | solution.py:32
  55.4 4.9 %collective-permute-start.4 = (f32[3,256,256]{2,1,0:T(8,128)S(1)}, f32[3,256,256]{2,1,0:T(8,128)S(1)}, u32[]{:S(2)}, u32[]{:S(2)}) collective-permute-start(f32[3,256,256]{2,1,0:T(8,128)S(1)} %add.126), channel_id=1, source_target_pairs={{0,4},{1,5},{2,6},{3,7},{4,0},{5,1},{6,2},{7,3},{8,12},{9,13},{10,... | collective-permute-start | bytes 2359304 | tf_op jit(solution)/shard_map/ppermute | solution.py:32
  60.4 2.5 %collective-permute-start.6 = (f32[256,256]{1,0:T(8,128)S(1)}, f32[256,256]{1,0:T(8,128)S(1)}, u32[]{:S(2)}, u32[]{:S(2)}) collective-permute-start(f32[256,256]{1,0:T(8,128)S(1)} %fusion.9), channel_id=1, source_target_pairs={{0,2},{1,3},{2,0},{3,1},{4,6},{5,7},{6,4},{7,5},{8,10},{9,11},{10,... | collective-permute-start | bytes 786440 | tf_op jit(solution)/shard_map/ppermute | solution.py:32
  62.9 20.3 %collective-permute-done.6 = f32[256,256]{1,0:T(8,128)S(1)} collective-permute-done((f32[256,256]{1,0:T(8,128)S(1)}, f32[256,256]{1,0:T(8,128)S(1)}, u32[]{:S(2)}, u32[]{:S(2)}) %collective-permute-start.6) | collective-permute-done | bytes 262176 | tf_op jit(solution)/shard_map/ppermute | solution.py:32
  83.3 3.9 %collective-permute-start.7 = (f32[256,256]{1,0:T(8,128)S(1)}, f32[256,256]{1,0:T(8,128)S(1)}, u32[]{:S(2)}, u32[]{:S(2)}) collective-permute-start(f32[256,256]{1,0:T(8,128)S(1)} %add.131), channel_id=1, source_target_pairs={{0,4},{1,5},{2,6},{3,7},{4,0},{5,1},{6,2},{7,3},{8,12},{9,13},{10,... | collective-permute-start | bytes 786440 | tf_op jit(solution)/shard_map/ppermute | solution.py:32
  87.2 6.1 %collective-permute-done.7 = f32[256,256]{1,0:T(8,128)S(1)} collective-permute-done((f32[256,256]{1,0:T(8,128)S(1)}, f32[256,256]{1,0:T(8,128)S(1)}, u32[]{:S(2)}, u32[]{:S(2)}) %collective-permute-start.7) | collective-permute-done | bytes 262176 | tf_op jit(solution)/shard_map/ppermute | solution.py:32
  95.0 6.8 %shard_map.65 = (f32[2,384,512]{2,1,0:T(8,128)}, f32[384,512]{1,0:T(8,128)}) custom-call(s32[3]{0:T(128)} %roff.3, s32[3]{0:T(128)} %coff.3, s32[1]{0:T(128)S(6)} %copy.12.cnt, bf16[3,2,256,256]{3,2,1,0:T(8,128)(2,1)} %get-tuple-element.10.exit_ref, f32[3,2,256,256]{3,2,1,0:T(8,128)} %get-tuple-element.11.wave_ref, f32[3,256,256]{2,1,0:T(8,128)} %add.127.model_ref, ...), custom_call_target="tpu_custom_call" | custom-call | flops 805306368 | bytes 12582912 | tf_op jit(solution)/shard_map/pallas_call | solution.py:185
  103.1 2.9 %collective-permute-start.8 = (f32[2,128,512]{2,1,0:T(8,128)S(1)}, f32[2,128,512]{2,1,0:T(8,128)S(1)}, u32[]{:S(2)}, u32[]{:S(2)}) collective-permute-start(f32[2,128,512]{2,1,0:T(8,128)S(1)} %get-tuple-element.15), channel_id=1, source_target_pairs={{0,8},{8,16},{16,24},{24,32},{32,40},{40,48},{48,56},{56,64},{64,7... | collective-permute-start | bytes 1572872 | tf_op jit(solution)/shard_map/ppermute | solution.py:247
  106.0 7.4 %collective-permute-start.9 = (f32[2,128,512]{2,1,0:T(8,128)S(1)}, f32[2,128,512]{2,1,0:T(8,128)S(1)}, u32[]{:S(2)}, u32[]{:S(2)}) collective-permute-start(f32[2,128,512]{2,1,0:T(8,128)S(1)} %get-tuple-element.16), channel_id=1, source_target_pairs={{8,0},{16,8},{24,16},{32,24},{40,32},{48,40},{56,48},{64,56},{72,6... | collective-permute-start | bytes 1572872 | tf_op jit(solution)/shard_map/ppermute | solution.py:248
  113.4 7.6 %collective-permute-done.8 = f32[2,128,512]{2,1,0:T(8,128)S(1)} collective-permute-done((f32[2,128,512]{2,1,0:T(8,128)S(1)}, f32[2,128,512]{2,1,0:T(8,128)S(1)}, u32[]{:S(2)}, u32[]{:S(2)}) %collective-permute-start.8) | collective-permute-done | bytes 524320 | tf_op jit(solution)/shard_map/ppermute | solution.py:247
  127.0 3.3 %collective-permute-start.11 = (f32[2,2,16,512]{3,2,0,1:T(8,128)S(1)}, f32[2,2,16,512]{3,2,0,1:T(8,128)S(1)}, u32[]{:S(2)}, u32[]{:S(2)}) collective-permute-start(f32[2,2,16,512]{3,2,0,1:T(8,128)S(1)} %bitcast.27), channel_id=1, source_target_pairs={{0,2},{1,3},{2,0},{3,1},{4,6},{5,7},{6,4},{7,5},{8,10},{9,11},{10,... | collective-permute-start | bytes 393224 | tf_op jit(solution)/shard_map/ppermute | solution.py:49
  131.1 2.1 %collective-permute-start.13 = (f32[16,512]{1,0:T(8,128)S(1)}, f32[16,512]{1,0:T(8,128)S(1)}, u32[]{:S(2)}, u32[]{:S(2)}) collective-permute-start(f32[16,512]{1,0:T(8,128)S(1)} %get-tuple-element.17), channel_id=1, source_target_pairs={{0,8},{8,16},{16,24},{24,32},{32,40},{40,48},{48,56},{56,64},{64,7... | collective-permute-start | bytes 98312 | tf_op jit(solution)/shard_map/ppermute | solution.py:258
  133.3 7.5 %collective-permute-start.14 = (f32[16,512]{1,0:T(8,128)S(1)}, f32[16,512]{1,0:T(8,128)S(1)}, u32[]{:S(2)}, u32[]{:S(2)}) collective-permute-start(f32[16,512]{1,0:T(8,128)S(1)} %get-tuple-element.18), channel_id=1, source_target_pairs={{8,0},{16,8},{24,16},{32,24},{40,32},{48,40},{56,48},{64,56},{72,6... | collective-permute-start | bytes 98312 | tf_op jit(solution)/shard_map/ppermute | solution.py:259
  140.8 3.1 %collective-permute-start.12 = (f32[2,16,512]{2,1,0:T(8,128)S(1)}, f32[2,16,512]{2,1,0:T(8,128)S(1)}, u32[]{:S(2)}, u32[]{:S(2)}) collective-permute-start(f32[2,16,512]{2,1,0:T(8,128)S(1)} %dynamic-slice_bitcast_fusion.1), channel_id=1, source_target_pairs={{0,4},{1,5},{2,6},{3,7},{4,0},{5,1},{6,2},{7,3},{8,12},{9,13},{10,... | collective-permute-start | bytes 196616 | tf_op jit(solution)/shard_map/ppermute | solution.py:49
  144.7 3.8 %collective-permute-done.12 = f32[2,16,512]{2,1,0:T(8,128)S(1)} collective-permute-done((f32[2,16,512]{2,1,0:T(8,128)S(1)}, f32[2,16,512]{2,1,0:T(8,128)S(1)}, u32[]{:S(2)}, u32[]{:S(2)}) %collective-permute-start.12) | collective-permute-done | bytes 65568 | tf_op jit(solution)/shard_map/ppermute | solution.py:49
  (30 shorter events, 16.4 us)
Async XLA Ops:
  0.0 19.1 %collective-permute-start = (f32[2,128,512]{2,1,0:T(8,128)}, f32[2,128,512]{2,1,0:T(8,128)S(1)}, u32[]{:S(2)}, u32[]{:S(2)}) collective-permute-start(f32[2,128,512]{2,1,0:T(8,128)} %param.6), channel_id=1, source_target_pairs={{0,8},{8,16},{16,24},{24,32},{32,40},{40,48},{48,56},{56,64},{64,7... | collective-permute-start | bytes 1572872 | tf_op jit(solution)/shard_map/ppermute | solution.py:227
  3.5 16.9 %collective-permute-start.1 = (f32[2,128,512]{2,1,0:T(8,128)}, f32[2,128,512]{2,1,0:T(8,128)S(1)}, u32[]{:S(2)}, u32[]{:S(2)}) collective-permute-start(f32[2,128,512]{2,1,0:T(8,128)} %param.6), channel_id=1, source_target_pairs={{8,0},{16,8},{24,16},{32,24},{40,32},{48,40},{56,48},{64,56},{72,6... | collective-permute-start | bytes 1572872 | tf_op jit(solution)/shard_map/ppermute | solution.py:228
  28.1 9.2 %copy-start = (f32[2,1,256,256]{3,2,1,0:T(8,128)S(1)}, f32[2,1,256,256]{3,2,1,0:T(8,128)}, u32[]{:S(2)}) copy-start(f32[2,1,256,256]{3,2,1,0:T(8,128)} %param.7) | copy-start | bytes 1572868
  28.1 4.5 %collective-permute-start.2 = (f32[3,256,256]{2,1,0:T(8,128)}, f32[3,256,256]{2,1,0:T(8,128)S(1)}, u32[]{:S(2)}, u32[]{:S(2)}) collective-permute-start(f32[3,256,256]{2,1,0:T(8,128)} %get-tuple-element.12), channel_id=1, source_target_pairs={{0,1},{1,0},{2,3},{3,2},{4,5},{5,4},{6,7},{7,6},{8,9},{9,8},{10,11... | collective-permute-start | bytes 2359304 | tf_op jit(solution)/shard_map/ppermute | solution.py:32
  33.8 21.5 %collective-permute-start.3 = (f32[3,256,256]{2,1,0:T(8,128)S(1)}, f32[3,256,256]{2,1,0:T(8,128)S(1)}, u32[]{:S(2)}, u32[]{:S(2)}) collective-permute-start(f32[3,256,256]{2,1,0:T(8,128)S(1)} %add.125), channel_id=1, source_target_pairs={{0,2},{1,3},{2,0},{3,1},{4,6},{5,7},{6,4},{7,5},{8,10},{9,11},{10,... | collective-permute-start | bytes 2359304 | tf_op jit(solution)/shard_map/ppermute | solution.py:32
  37.3 23.1 %collective-permute-start.5 = (f32[256,256]{1,0:T(8,128)S(1)}, f32[256,256]{1,0:T(8,128)S(1)}, u32[]{:S(2)}, u32[]{:S(2)}) collective-permute-start(f32[256,256]{1,0:T(8,128)S(1)} %add_bitcast_fusion), channel_id=1, source_target_pairs={{0,1},{1,0},{2,3},{3,2},{4,5},{5,4},{6,7},{7,6},{8,9},{9,8},{10,11... | collective-permute-start | bytes 786440 | tf_op jit(solution)/shard_map/ppermute | solution.py:32
  55.4 38.6 %collective-permute-start.4 = (f32[3,256,256]{2,1,0:T(8,128)S(1)}, f32[3,256,256]{2,1,0:T(8,128)S(1)}, u32[]{:S(2)}, u32[]{:S(2)}) collective-permute-start(f32[3,256,256]{2,1,0:T(8,128)S(1)} %add.126), channel_id=1, source_target_pairs={{0,4},{1,5},{2,6},{3,7},{4,0},{5,1},{6,2},{7,3},{8,12},{9,13},{10,... | collective-permute-start | bytes 2359304 | tf_op jit(solution)/shard_map/ppermute | solution.py:32
  60.4 22.8 %collective-permute-start.6 = (f32[256,256]{1,0:T(8,128)S(1)}, f32[256,256]{1,0:T(8,128)S(1)}, u32[]{:S(2)}, u32[]{:S(2)}) collective-permute-start(f32[256,256]{1,0:T(8,128)S(1)} %fusion.9), channel_id=1, source_target_pairs={{0,2},{1,3},{2,0},{3,1},{4,6},{5,7},{6,4},{7,5},{8,10},{9,11},{10,... | collective-permute-start | bytes 786440 | tf_op jit(solution)/shard_map/ppermute | solution.py:32
  83.3 10.0 %collective-permute-start.7 = (f32[256,256]{1,0:T(8,128)S(1)}, f32[256,256]{1,0:T(8,128)S(1)}, u32[]{:S(2)}, u32[]{:S(2)}) collective-permute-start(f32[256,256]{1,0:T(8,128)S(1)} %add.131), channel_id=1, source_target_pairs={{0,4},{1,5},{2,6},{3,7},{4,0},{5,1},{6,2},{7,3},{8,12},{9,13},{10,... | collective-permute-start | bytes 786440 | tf_op jit(solution)/shard_map/ppermute | solution.py:32
  103.1 18.0 %collective-permute-start.8 = (f32[2,128,512]{2,1,0:T(8,128)S(1)}, f32[2,128,512]{2,1,0:T(8,128)S(1)}, u32[]{:S(2)}, u32[]{:S(2)}) collective-permute-start(f32[2,128,512]{2,1,0:T(8,128)S(1)} %get-tuple-element.15), channel_id=1, source_target_pairs={{0,8},{8,16},{16,24},{24,32},{32,40},{40,48},{48,56},{56,64},{64,7... | collective-permute-start | bytes 1572872 | tf_op jit(solution)/shard_map/ppermute | solution.py:247
  106.0 16.2 %collective-permute-start.9 = (f32[2,128,512]{2,1,0:T(8,128)S(1)}, f32[2,128,512]{2,1,0:T(8,128)S(1)}, u32[]{:S(2)}, u32[]{:S(2)}) collective-permute-start(f32[2,128,512]{2,1,0:T(8,128)S(1)} %get-tuple-element.16), channel_id=1, source_target_pairs={{8,0},{16,8},{24,16},{32,24},{40,32},{48,40},{56,48},{64,56},{72,6... | collective-permute-start | bytes 1572872 | tf_op jit(solution)/shard_map/ppermute | solution.py:248
  123.4 3.4 %collective-permute-start.10 = (f32[2,2,2,16,512]{4,3,2,1,0:T(8,128)S(1)}, f32[2,2,2,16,512]{4,3,2,1,0:T(8,128)S(1)}, u32[]{:S(2)}, u32[]{:S(2)}) collective-permute-start(f32[2,2,2,16,512]{4,3,2,1,0:T(8,128)S(1)} %dynamic-slice_bitcast_fusion), channel_id=1, source_target_pairs={{0,1},{1,0},{2,3},{3,2},{4,5},{5,4},{6,7},{7,6},{8,9},{9,8},{10,11... | collective-permute-start | bytes 786440 | tf_op jit(solution)/shard_map/ppermute | solution.py:49
  127.0 13.8 %collective-permute-start.11 = (f32[2,2,16,512]{3,2,0,1:T(8,128)S(1)}, f32[2,2,16,512]{3,2,0,1:T(8,128)S(1)}, u32[]{:S(2)}, u32[]{:S(2)}) collective-permute-start(f32[2,2,16,512]{3,2,0,1:T(8,128)S(1)} %bitcast.27), channel_id=1, source_target_pairs={{0,2},{1,3},{2,0},{3,1},{4,6},{5,7},{6,4},{7,5},{8,10},{9,11},{10,... | collective-permute-start | bytes 393224 | tf_op jit(solution)/shard_map/ppermute | solution.py:49
  131.1 12.8 %collective-permute-start.13 = (f32[16,512]{1,0:T(8,128)S(1)}, f32[16,512]{1,0:T(8,128)S(1)}, u32[]{:S(2)}, u32[]{:S(2)}) collective-permute-start(f32[16,512]{1,0:T(8,128)S(1)} %get-tuple-element.17), channel_id=1, source_target_pairs={{0,8},{8,16},{16,24},{24,32},{32,40},{40,48},{48,56},{56,64},{64,7... | collective-permute-start | bytes 98312 | tf_op jit(solution)/shard_map/ppermute | solution.py:258
  133.3 10.7 %collective-permute-start.14 = (f32[16,512]{1,0:T(8,128)S(1)}, f32[16,512]{1,0:T(8,128)S(1)}, u32[]{:S(2)}, u32[]{:S(2)}) collective-permute-start(f32[16,512]{1,0:T(8,128)S(1)} %get-tuple-element.18), channel_id=1, source_target_pairs={{8,0},{16,8},{24,16},{32,24},{40,32},{48,40},{56,48},{64,56},{72,6... | collective-permute-start | bytes 98312 | tf_op jit(solution)/shard_map/ppermute | solution.py:259
  140.8 7.7 %collective-permute-start.12 = (f32[2,16,512]{2,1,0:T(8,128)S(1)}, f32[2,16,512]{2,1,0:T(8,128)S(1)}, u32[]{:S(2)}, u32[]{:S(2)}) collective-permute-start(f32[2,16,512]{2,1,0:T(8,128)S(1)} %dynamic-slice_bitcast_fusion.1), channel_id=1, source_target_pairs={{0,4},{1,5},{2,6},{3,7},{4,0},{5,1},{6,2},{7,3},{8,12},{9,13},{10,... | collective-permute-start | bytes 196616 | tf_op jit(solution)/shard_map/ppermute | solution.py:49

commit v2 on v1

--- a/solution.py
+++ b/solution.py
@@ -25,28 +25,45 @@
     return [(i + 1, i) for i in range(size - 1)]
 
 
+def mode_pairs():
+    n = lax.axis_size("mode")
+    chips = n // 2
+    core = [(i, i ^ 1) for i in range(n)]
+    near = [(i, i ^ 2) for i in range(n)]
+    far = [(i, 2 * (chips - 1 - i // 2) + i % 2) for i in range(n)]
+    return core, near, far
+
+
 def allreduce_mode(x):
+    core_pairs, near, far = mode_pairs()
+    core = lax.axis_index("mode") % 2
+    parts = x.reshape(2, 2, -1, x.shape[-1])
+    keep = lax.dynamic_index_in_dim(parts, core, 0, keepdims=False)
+    send = lax.dynamic_index_in_dim(parts, 1 - core, 0, keepdims=False)
+    half = keep + lax.ppermute(send, "mode", core_pairs)
+    qa, qb = half[0], half[1]
+    qa = qa + lax.ppermute(qa, "mode", near)
+    qb = qb + lax.ppermute(qb, "mode", far)
+    qa = qa + lax.ppermute(qa, "mode", far)
+    qb = qb + lax.ppermute(qb, "mode", near)
+    half = jnp.stack([qa, qb])
+    other = lax.ppermute(half, "mode", core_pairs)
+    first = jnp.where(core == 0, half, other)
+    second = jnp.where(core == 0, other, half)
+    return jnp.stack([first, second]).reshape(x.shape)
+
+
+def reduce_scatter_mode(x):
+    core_pairs, near, far = mode_pairs()
     n = lax.axis_size("mode")
-    d = 1
-    while d < n:
-        x = x + lax.ppermute(x, "mode", [(i, i ^ d) for i in range(n)])
-        d *= 2
-    return x
-
-
-def reduce_scatter_mode(x):
-    n = lax.axis_size("mode")
-    k = n.bit_length() - 1
     m = lax.axis_index("mode")
     c, rows, w = x.shape
-    x = x.reshape((c,) + (2,) * k + (rows // n, w))
-    for i in range(k):
-        d = 1 << i
-        dim = k - i
+    x = x.reshape(c, 2, 2, 2, rows // n, w)
+    for pairs, dim, d in ((core_pairs, 3, 1), (far, 1, 4), (near, 1, 2)):
         bit = (m // d) % 2
         keep = lax.dynamic_index_in_dim(x, bit, axis=dim, keepdims=False)
         send = lax.dynamic_index_in_dim(x, 1 - bit, axis=dim, keepdims=False)
-        x = keep + lax.ppermute(send, "mode", [(j, j ^ d) for j in range(n)])
+        x = keep + lax.ppermute(send, "mode", pairs)
     return x.reshape(c, rows // n, w)
 
 
@@ -54,7 +71,7 @@
     return jnp.dot(a, b, preferred_element_type=jnp.float32)
 
 
-def forward_kernel(roff, coff, cnt, ext_ref, probe_ref, fr_ref, fi_ref, exit_ref, wave_ref, power_ref):
+def forward_kernel(roff, coff, cnt, ext_ref, probe_ref, fr_ref, fi_ref, ppt_ref, exit_ref, wave_ref, power_ref):
     j = pl.program_id(0)
     pat = probe_ref.shape[1]
     width = ext_ref.shape[2]
@@ -139,7 +156,7 @@
         illum_ref[pl.ds(base, span), :] += place(ppt_ref[...])
 
 
-def run_forward(ext, probe2, fr, fi, roff, coff, cnt):
+def run_forward(ext, probe2, fr, fi, ppt, roff, coff, cnt):
     slots = roff.shape[0]
     pat = probe2.shape[1]
     whole3 = lambda j, *_: (0, 0, 0)
@@ -157,6 +174,7 @@
                 pl.BlockSpec(probe2.shape, whole3),
                 pl.BlockSpec(fr.shape, whole2),
                 pl.BlockSpec(fi.shape, whole2),
+                pl.BlockSpec(ppt.shape, whole2),
             ],
             out_specs=[
                 pl.BlockSpec((1, 2, pat, pat), per4),
@@ -171,7 +189,7 @@
         ],
         compiler_params=pltpu.CompilerParams(dimension_semantics=("arbitrary",)),
         cost_estimate=pl.CostEstimate(flops=flops, transcendentals=0, bytes_accessed=8 * 1024 * 1024),
-    )(roff, coff, cnt, ext, probe2, fr, fi)
+    )(roff, coff, cnt, ext, probe2, fr, fi, ppt)
 
 
 def run_backward(exits, waves, model, measured, probe2, ppt, fr, fi, roff, coff, cnt, ext_rows, width):
@@ -233,7 +251,7 @@
     coff = col_offsets.astype(jnp.int32)
     cnt = tile_counts.astype(jnp.int32)
 
-    exits, waves, power = run_forward(ext, probe2, fr, fi, roff, coff, cnt)
+    exits, waves, power = run_forward(ext, probe2, fr, fi, probe_power, roff, coff, cnt)
     model = allreduce_mode(power)
     numer, illum = run_backward(
         exits, waves, model, measured, probe2, probe_power, fr, fi, roff, coff, cnt, ext_rows, width

time: 151 us -> 135 us (0.89)
  the two profiles are of different devices: /device:TPU:256 before, /device:TPU:384 now
where the time goes in v2:
time: 135 us; the launch traced here: 134 us
  starting transfers between devices  67.2 us (50%)
  waiting for transfers between devices  40.5 us (30%)
  Pallas kernels  12.3 us (9%)
  other arithmetic  9.8 us (7%)
  local copies, waits for them, and re-layouts  3.21 us (2%)
    ppermute x1, waiting for transfers between devices, local(): lax.ppermute(bottom, 'pos', neighbour_pairs(pos_count, 1))  10 us
    ppermute x2, waiting for transfers between devices, allreduce_mode(): qb = qb + lax.ppermute(qb, 'mode', far)  8.63 us
    ppermute x2, starting transfers between devices, allreduce_mode(): qa = qa + lax.ppermute(qa, 'mode', far)  8.01 us
    ppermute x1, starting transfers between devices, local(): lax.ppermute(illum_top, 'pos', neighbour_pairs(pos_count, -1))  7.71 us
    ppermute x2, starting transfers between devices, allreduce_mode(): qb = qb + lax.ppermute(qb, 'mode', far)  7.07 us
    ppermute x3, starting transfers between devices, reduce_scatter_mode(): x = keep + lax.ppermute(send, 'mode', pairs)  6.89 us
    pallas_call x1, Pallas kernels, run_backward(): pl.pallas_call(backward_kernel, grid_spec=pltpu.PrefetchScalarGridSpec(nu...  6.75 us
    ppermute x2, waiting for transfers between devices, allreduce_mode(): qb = qb + lax.ppermute(qb, 'mode', near)  6.69 us
  transfers between devices with their start and end apart: 21, of which 13 were waited for; matrix products, arithmetic and copies ran while one was open for 3% of the time, Pallas kernels for 0%

profile of v2, /device:TPU:384, one launch (start us, length us, event | category | flops | bytes accessed | tf_op | source)
XLA Modules:
  0.0 134.1 jit_solution(5868724612179890685)
XLA Ops:
  1.2 1.9 %collective-permute-start.2 = (f32[2,64,256]{2,1,0:T(8,128)S(1)}, f32[2,64,256]{2,1,0:T(8,128)S(1)}, u32[]{:S(2)}, u32[]{:S(2)}) collective-permute-start(f32[2,64,256]{2,1,0:T(8,128)S(1)} %dynamic-slice_bitcast_fusion.2), channel_id=1, source_target_pairs={{0,1},{1,0},{2,3},{3,2},{4,5},{5,4},{6,7},{7,6},{8,9},{9,8},{10,11... | collective-permute-start | bytes 393224 | tf_op jit(solution)/shard_map/ppermute | solution.py:43
  4.4 3.4 %collective-permute-start.3 = (f32[64,256]{1,0:T(8,128)S(1)}, f32[64,256]{1,0:T(8,128)S(1)}, u32[]{:S(2)}, u32[]{:S(2)}) collective-permute-start(f32[64,256]{1,0:T(8,128)S(1)} %get-tuple-element.31), channel_id=1, source_target_pairs={{0,2},{1,3},{2,0},{3,1},{4,6},{5,7},{6,4},{7,5},{8,10},{9,11},{10,... | collective-permute-start | bytes 196616 | tf_op jit(solution)/shard_map/ppermute | solution.py:45
  7.8 4.0 %collective-permute-start.5 = (f32[64,256]{1,0:T(8,128)S(1)}, f32[64,256]{1,0:T(8,128)S(1)}, u32[]{:S(2)}, u32[]{:S(2)}) collective-permute-start(f32[64,256]{1,0:T(8,128)S(1)} %get-tuple-element.32), channel_id=1, source_target_pairs={{0,6},{1,7},{2,4},{3,5},{4,2},{5,3},{6,0},{7,1},{8,14},{9,15},{10,... | collective-permute-start | bytes 196616 | tf_op jit(solution)/shard_map/ppermute | solution.py:46
  11.9 3.3 %collective-permute-done.5 = f32[64,256]{1,0:T(8,128)S(1)} collective-permute-done((f32[64,256]{1,0:T(8,128)S(1)}, f32[64,256]{1,0:T(8,128)S(1)}, u32[]{:S(2)}, u32[]{:S(2)}) %collective-permute-start.5) | collective-permute-done | bytes 65568 | tf_op jit(solution)/shard_map/ppermute | solution.py:46
  15.2 4.0 %collective-permute-start.4 = (f32[64,256]{1,0:T(8,128)S(1)}, f32[64,256]{1,0:T(8,128)S(1)}, u32[]{:S(2)}, u32[]{:S(2)}) collective-permute-start(f32[64,256]{1,0:T(8,128)S(1)} %get-tuple-element.29), channel_id=1, source_target_pairs={{0,6},{1,7},{2,4},{3,5},{4,2},{5,3},{6,0},{7,1},{8,14},{9,15},{10,... | collective-permute-start | bytes 196616 | tf_op jit(solution)/shard_map/ppermute | solution.py:47
  19.3 3.5 %collective-permute-start = (f32[2,128,512]{2,1,0:T(8,128)S(1)}, f32[2,128,512]{2,1,0:T(8,128)S(1)}, u32[]{:S(2)}, u32[]{:S(2)}) collective-permute-start(f32[2,128,512]{2,1,0:T(8,128)S(1)} %copy-done), channel_id=1, source_target_pairs={{0,8},{8,16},{16,24},{24,32},{32,40},{40,48},{48,56},{56,64},{64,7... | collective-permute-start | bytes 1572872 | tf_op jit(solution)/shard_map/ppermute | solution.py:245
  22.8 5.7 %collective-permute-start.1 = (f32[2,128,512]{2,1,0:T(8,128)S(1)}, f32[2,128,512]{2,1,0:T(8,128)S(1)}, u32[]{:S(2)}, u32[]{:S(2)}) collective-permute-start(f32[2,128,512]{2,1,0:T(8,128)S(1)} %copy-done), channel_id=1, source_target_pairs={{8,0},{16,8},{24,16},{32,24},{40,32},{48,40},{56,48},{64,56},{72,6... | collective-permute-start | bytes 1572872 | tf_op jit(solution)/shard_map/ppermute | solution.py:246
  30.4 4.2 %collective-permute-done.6 = f32[64,256]{1,0:T(8,128)S(1)} collective-permute-done((f32[64,256]{1,0:T(8,128)S(1)}, f32[64,256]{1,0:T(8,128)S(1)}, u32[]{:S(2)}, u32[]{:S(2)}) %collective-permute-start.6) | collective-permute-done | bytes 65568 | tf_op jit(solution)/shard_map/ppermute | solution.py:48
  41.0 5.5 %shard_map.64 = (bf16[3,2,256,256]{3,2,1,0:T(8,128)(2,1)}, f32[3,2,256,256]{3,2,1,0:T(8,128)}, f32[3,256,256]{2,1,0:T(8,128)}) custom-call(s32[3]{0:T(128)} %roff.3, s32[3]{0:T(128)} %coff.3, s32[1]{0:T(128)S(6)} %copy.12.cnt, f32[2,384,512]{2,1,0:T(8,128)} %pad_maximum_fusion.ext_ref, f32[2,256,256]{2,1,0:T(8,128)} %bitcast.64, ...), custom_call_target="tpu_custom_call" | custom-call | flops 805306368 | bytes 8388608 | tf_op jit(solution)/shard_map/pallas_call | solution.py:167
  47.5 2.4 %collective-permute-start.8 = (f32[2,192,256]{2,1,0:T(8,128)S(1)}, f32[2,192,256]{2,1,0:T(8,128)S(1)}, u32[]{:S(2)}, u32[]{:S(2)}) collective-permute-start(f32[2,192,256]{2,1,0:T(8,128)S(1)} %dynamic-slice_bitcast_fusion), channel_id=1, source_target_pairs={{0,1},{1,0},{2,3},{3,2},{4,5},{5,4},{6,7},{7,6},{8,9},{9,8},{10,11... | collective-permute-start | bytes 1179656 | tf_op jit(solution)/shard_map/ppermute | solution.py:43
  52.4 3.1 %collective-permute-start.11 = (f32[192,256]{1,0:T(8,128)S(1)}, f32[192,256]{1,0:T(8,128)S(1)}, u32[]{:S(2)}, u32[]{:S(2)}) collective-permute-start(f32[192,256]{1,0:T(8,128)S(1)} %get-tuple-element.24), channel_id=1, source_target_pairs={{0,6},{1,7},{2,4},{3,5},{4,2},{5,3},{6,0},{7,1},{8,14},{9,15},{10,... | collective-permute-start | bytes 589832 | tf_op jit(solution)/shard_map/ppermute | solution.py:46
  57.4 5.3 %collective-permute-done.11 = f32[192,256]{1,0:T(8,128)S(1)} collective-permute-done((f32[192,256]{1,0:T(8,128)S(1)}, f32[192,256]{1,0:T(8,128)S(1)}, u32[]{:S(2)}, u32[]{:S(2)}) %collective-permute-start.11) | collective-permute-done | bytes 196640 | tf_op jit(solution)/shard_map/ppermute | solution.py:46
  64.3 4.0 %collective-permute-start.10 = (f32[192,256]{1,0:T(8,128)S(1)}, f32[192,256]{1,0:T(8,128)S(1)}, u32[]{:S(2)}, u32[]{:S(2)}) collective-permute-start(f32[192,256]{1,0:T(8,128)S(1)} %get-tuple-element.21), channel_id=1, source_target_pairs={{0,6},{1,7},{2,4},{3,5},{4,2},{5,3},{6,0},{7,1},{8,14},{9,15},{10,... | collective-permute-start | bytes 589832 | tf_op jit(solution)/shard_map/ppermute | solution.py:47
  70.2 3.2 %collective-permute-done.10 = f32[192,256]{1,0:T(8,128)S(1)} collective-permute-done((f32[192,256]{1,0:T(8,128)S(1)}, f32[192,256]{1,0:T(8,128)S(1)}, u32[]{:S(2)}, u32[]{:S(2)}) %collective-permute-start.10) | collective-permute-done | bytes 196640 | tf_op jit(solution)/shard_map/ppermute | solution.py:47
  73.4 2.5 %collective-permute-done.12 = f32[192,256]{1,0:T(8,128)S(1)} collective-permute-done((f32[192,256]{1,0:T(8,128)S(1)}, f32[192,256]{1,0:T(8,128)S(1)}, u32[]{:S(2)}, u32[]{:S(2)}) %collective-permute-start.12) | collective-permute-done | bytes 196640 | tf_op jit(solution)/shard_map/ppermute | solution.py:48
  76.0 1.9 %collective-permute-start.13 = (f32[2,192,256]{2,1,0:T(8,128)S(1)}, f32[2,192,256]{2,1,0:T(8,128)S(1)}, u32[]{:S(2)}, u32[]{:S(2)}) collective-permute-start(f32[2,192,256]{2,1,0:T(8,128)S(1)} %pad_maximum_fusion.2), channel_id=1, source_target_pairs={{0,1},{1,0},{2,3},{3,2},{4,5},{5,4},{6,7},{7,6},{8,9},{9,8},{10,11... | collective-permute-start | bytes 1179656 | tf_op jit(solution)/shard_map/ppermute | solution.py:50
  80.6 6.8 %shard_map.65 = (f32[2,384,512]{2,1,0:T(8,128)}, f32[384,512]{1,0:T(8,128)}) custom-call(s32[3]{0:T(128)} %roff.3, s32[3]{0:T(128)} %coff.3, s32[1]{0:T(128)S(6)} %copy.12.cnt, bf16[3,2,256,256]{3,2,1,0:T(8,128)(2,1)} %get-tuple-element.10.exit_ref, f32[3,2,256,256]{3,2,1,0:T(8,128)} %get-tuple-element.11.wave_ref, f32[3,256,256]{2,1,0:T(8,128)} %bitcast.63, ...), custom_call_target="tpu_custom_call" | custom-call | flops 805306368 | bytes 12582912 | tf_op jit(solution)/shard_map/pallas_call | solution.py:203
  88.6 3.1 %collective-permute-start.14 = (f32[2,128,512]{2,1,0:T(8,128)S(1)}, f32[2,128,512]{2,1,0:T(8,128)S(1)}, u32[]{:S(2)}, u32[]{:S(2)}) collective-permute-start(f32[2,128,512]{2,1,0:T(8,128)S(1)} %get-tuple-element.15), channel_id=1, source_target_pairs={{0,8},{8,16},{16,24},{24,32},{32,40},{40,48},{48,56},{56,64},{64,7... | collective-permute-start | bytes 1572872 | tf_op jit(solution)/shard_map/ppermute | solution.py:265
  91.8 6.0 %collective-permute-start.15 = (f32[2,128,512]{2,1,0:T(8,128)S(1)}, f32[2,128,512]{2,1,0:T(8,128)S(1)}, u32[]{:S(2)}, u32[]{:S(2)}) collective-permute-start(f32[2,128,512]{2,1,0:T(8,128)S(1)} %get-tuple-element.16), channel_id=1, source_target_pairs={{8,0},{16,8},{24,16},{32,24},{40,32},{48,40},{56,48},{64,56},{72,6... | collective-permute-start | bytes 1572872 | tf_op jit(solution)/shard_map/ppermute | solution.py:266
  97.8 10.0 %collective-permute-done.14 = f32[2,128,512]{2,1,0:T(8,128)S(1)} collective-permute-done((f32[2,128,512]{2,1,0:T(8,128)S(1)}, f32[2,128,512]{2,1,0:T(8,128)S(1)}, u32[]{:S(2)}, u32[]{:S(2)}) %collective-permute-start.14) | collective-permute-done | bytes 524320 | tf_op jit(solution)/shard_map/ppermute | solution.py:265
  110.2 1.9 %collective-permute-start.16 = (f32[2,2,2,16,512]{4,3,2,1,0:T(8,128)S(1)}, f32[2,2,2,16,512]{4,3,2,1,0:T(8,128)S(1)}, u32[]{:S(2)}, u32[]{:S(2)}) collective-permute-start(f32[2,2,2,16,512]{4,3,2,1,0:T(8,128)S(1)} %dynamic-slice_bitcast_fusion.1), channel_id=1, source_target_pairs={{0,1},{1,0},{2,3},{3,2},{4,5},{5,4},{6,7},{7,6},{8,9},{9,8},{10,11... | collective-permute-start | bytes 786440 | tf_op jit(solution)/shard_map/ppermute | solution.py:66
  113.7 3.1 %collective-permute-start.17 = (f32[2,2,16,512]{3,2,0,1:T(8,128)S(1)}, f32[2,2,16,512]{3,2,0,1:T(8,128)S(1)}, u32[]{:S(2)}, u32[]{:S(2)}) collective-permute-start(f32[2,2,16,512]{3,2,0,1:T(8,128)S(1)} %bitcast.74), channel_id=1, source_target_pairs={{0,6},{1,7},{2,4},{3,5},{4,2},{5,3},{6,0},{7,1},{8,14},{9,15},{10,... | collective-permute-start | bytes 393224 | tf_op jit(solution)/shard_map/ppermute | solution.py:66
  119.5 7.7 %collective-permute-start.20 = (f32[16,512]{1,0:T(8,128)S(1)}, f32[16,512]{1,0:T(8,128)S(1)}, u32[]{:S(2)}, u32[]{:S(2)}) collective-permute-start(f32[16,512]{1,0:T(8,128)S(1)} %get-tuple-element.18), channel_id=1, source_target_pairs={{8,0},{16,8},{24,16},{32,24},{40,32},{48,40},{56,48},{64,56},{72,6... | collective-permute-start | bytes 98312 | tf_op jit(solution)/shard_map/ppermute | solution.py:277
  130.1 3.4 %collective-permute-done.18 = f32[2,16,512]{2,1,0:T(8,128)S(1)} collective-permute-done((f32[2,16,512]{2,1,0:T(8,128)S(1)}, f32[2,16,512]{2,1,0:T(8,128)S(1)}, u32[]{:S(2)}, u32[]{:S(2)}) %collective-permute-start.18) | collective-permute-done | bytes 65568 | tf_op jit(solution)/shard_map/ppermute | solution.py:66
  (54 shorter events, 33.1 us)
Async XLA Ops:
  0.0 19.3 %copy-start = (f32[2,128,512]{2,1,0:T(8,128)S(1)}, f32[2,128,512]{2,1,0:T(8,128)}, u32[]{:S(2)}) copy-start(f32[2,128,512]{2,1,0:T(8,128)} %param.6) | copy-start | bytes 1572868
  1.2 3.2 %collective-permute-start.2 = (f32[2,64,256]{2,1,0:T(8,128)S(1)}, f32[2,64,256]{2,1,0:T(8,128)S(1)}, u32[]{:S(2)}, u32[]{:S(2)}) collective-permute-start(f32[2,64,256]{2,1,0:T(8,128)S(1)} %dynamic-slice_bitcast_fusion.2), channel_id=1, source_target_pairs={{0,1},{1,0},{2,3},{3,2},{4,5},{5,4},{6,7},{7,6},{8,9},{9,8},{10,11... | collective-permute-start | bytes 393224 | tf_op jit(solution)/shard_map/ppermute | solution.py:43
  4.4 7.4 %collective-permute-start.3 = (f32[64,256]{1,0:T(8,128)S(1)}, f32[64,256]{1,0:T(8,128)S(1)}, u32[]{:S(2)}, u32[]{:S(2)}) collective-permute-start(f32[64,256]{1,0:T(8,128)S(1)} %get-tuple-element.31), channel_id=1, source_target_pairs={{0,2},{1,3},{2,0},{3,1},{4,6},{5,7},{6,4},{7,5},{8,10},{9,11},{10,... | collective-permute-start | bytes 196616 | tf_op jit(solution)/shard_map/ppermute | solution.py:45
  7.8 7.4 %collective-permute-start.5 = (f32[64,256]{1,0:T(8,128)S(1)}, f32[64,256]{1,0:T(8,128)S(1)}, u32[]{:S(2)}, u32[]{:S(2)}) collective-permute-start(f32[64,256]{1,0:T(8,128)S(1)} %get-tuple-element.32), channel_id=1, source_target_pairs={{0,6},{1,7},{2,4},{3,5},{4,2},{5,3},{6,0},{7,1},{8,14},{9,15},{10,... | collective-permute-start | bytes 196616 | tf_op jit(solution)/shard_map/ppermute | solution.py:46
  15.2 15.1 %collective-permute-start.4 = (f32[64,256]{1,0:T(8,128)S(1)}, f32[64,256]{1,0:T(8,128)S(1)}, u32[]{:S(2)}, u32[]{:S(2)}) collective-permute-start(f32[64,256]{1,0:T(8,128)S(1)} %get-tuple-element.29), channel_id=1, source_target_pairs={{0,6},{1,7},{2,4},{3,5},{4,2},{5,3},{6,0},{7,1},{8,14},{9,15},{10,... | collective-permute-start | bytes 196616 | tf_op jit(solution)/shard_map/ppermute | solution.py:47
  19.3 20.5 %collective-permute-start = (f32[2,128,512]{2,1,0:T(8,128)S(1)}, f32[2,128,512]{2,1,0:T(8,128)S(1)}, u32[]{:S(2)}, u32[]{:S(2)}) collective-permute-start(f32[2,128,512]{2,1,0:T(8,128)S(1)} %copy-done), channel_id=1, source_target_pairs={{0,8},{8,16},{16,24},{24,32},{32,40},{40,48},{48,56},{56,64},{64,7... | collective-permute-start | bytes 1572872 | tf_op jit(solution)/shard_map/ppermute | solution.py:245
  22.8 17.0 %collective-permute-start.1 = (f32[2,128,512]{2,1,0:T(8,128)S(1)}, f32[2,128,512]{2,1,0:T(8,128)S(1)}, u32[]{:S(2)}, u32[]{:S(2)}) collective-permute-start(f32[2,128,512]{2,1,0:T(8,128)S(1)} %copy-done), channel_id=1, source_target_pairs={{8,0},{16,8},{24,16},{32,24},{40,32},{48,40},{56,48},{64,56},{72,6... | collective-permute-start | bytes 1572872 | tf_op jit(solution)/shard_map/ppermute | solution.py:246
  28.4 6.2 %collective-permute-start.6 = (f32[64,256]{1,0:T(8,128)S(1)}, f32[64,256]{1,0:T(8,128)S(1)}, u32[]{:S(2)}, u32[]{:S(2)}) collective-permute-start(f32[64,256]{1,0:T(8,128)S(1)} %get-tuple-element.30), channel_id=1, source_target_pairs={{0,2},{1,3},{2,0},{3,1},{4,6},{5,7},{6,4},{7,5},{8,10},{9,11},{10,... | collective-permute-start | bytes 196616 | tf_op jit(solution)/shard_map/ppermute | solution.py:48
  34.6 4.3 %collective-permute-start.7 = (f32[2,64,256]{2,1,0:T(8,128)S(1)}, f32[2,64,256]{2,1,0:T(8,128)S(1)}, u32[]{:S(2)}, u32[]{:S(2)}) collective-permute-start(f32[2,64,256]{2,1,0:T(8,128)S(1)} %pad_maximum_fusion.4), channel_id=1, source_target_pairs={{0,1},{1,0},{2,3},{3,2},{4,5},{5,4},{6,7},{7,6},{8,9},{9,8},{10,11... | collective-permute-start | bytes 393224 | tf_op jit(solution)/shard_map/ppermute | solution.py:50
  47.5 3.7 %collective-permute-start.8 = (f32[2,192,256]{2,1,0:T(8,128)S(1)}, f32[2,192,256]{2,1,0:T(8,128)S(1)}, u32[]{:S(2)}, u32[]{:S(2)}) collective-permute-start(f32[2,192,256]{2,1,0:T(8,128)S(1)} %dynamic-slice_bitcast_fusion), channel_id=1, source_target_pairs={{0,1},{1,0},{2,3},{3,2},{4,5},{5,4},{6,7},{7,6},{8,9},{9,8},{10,11... | collective-permute-start | bytes 1179656 | tf_op jit(solution)/shard_map/ppermute | solution.py:43
  52.4 10.3 %collective-permute-start.11 = (f32[192,256]{1,0:T(8,128)S(1)}, f32[192,256]{1,0:T(8,128)S(1)}, u32[]{:S(2)}, u32[]{:S(2)}) collective-permute-start(f32[192,256]{1,0:T(8,128)S(1)} %get-tuple-element.24), channel_id=1, source_target_pairs={{0,6},{1,7},{2,4},{3,5},{4,2},{5,3},{6,0},{7,1},{8,14},{9,15},{10,... | collective-permute-start | bytes 589832 | tf_op jit(solution)/shard_map/ppermute | solution.py:46
  55.4 8.8 %collective-permute-start.9 = (f32[192,256]{1,0:T(8,128)S(1)}, f32[192,256]{1,0:T(8,128)S(1)}, u32[]{:S(2)}, u32[]{:S(2)}) collective-permute-start(f32[192,256]{1,0:T(8,128)S(1)} %get-tuple-element.23), channel_id=1, source_target_pairs={{0,2},{1,3},{2,0},{3,1},{4,6},{5,7},{6,4},{7,5},{8,10},{9,11},{10,... | collective-permute-start | bytes 589832 | tf_op jit(solution)/shard_map/ppermute | solution.py:45
  64.3 9.1 %collective-permute-start.10 = (f32[192,256]{1,0:T(8,128)S(1)}, f32[192,256]{1,0:T(8,128)S(1)}, u32[]{:S(2)}, u32[]{:S(2)}) collective-permute-start(f32[192,256]{1,0:T(8,128)S(1)} %get-tuple-element.21), channel_id=1, source_target_pairs={{0,6},{1,7},{2,4},{3,5},{4,2},{5,3},{6,0},{7,1},{8,14},{9,15},{10,... | collective-permute-start | bytes 589832 | tf_op jit(solution)/shard_map/ppermute | solution.py:47
  68.3 7.7 %collective-permute-start.12 = (f32[192,256]{1,0:T(8,128)S(1)}, f32[192,256]{1,0:T(8,128)S(1)}, u32[]{:S(2)}, u32[]{:S(2)}) collective-permute-start(f32[192,256]{1,0:T(8,128)S(1)} %get-tuple-element.22), channel_id=1, source_target_pairs={{0,2},{1,3},{2,0},{3,1},{4,6},{5,7},{6,4},{7,5},{8,10},{9,11},{10,... | collective-permute-start | bytes 589832 | tf_op jit(solution)/shard_map/ppermute | solution.py:48
  76.0 3.6 %collective-permute-start.13 = (f32[2,192,256]{2,1,0:T(8,128)S(1)}, f32[2,192,256]{2,1,0:T(8,128)S(1)}, u32[]{:S(2)}, u32[]{:S(2)}) collective-permute-start(f32[2,192,256]{2,1,0:T(8,128)S(1)} %pad_maximum_fusion.2), channel_id=1, source_target_pairs={{0,1},{1,0},{2,3},{3,2},{4,5},{5,4},{6,7},{7,6},{8,9},{9,8},{10,11... | collective-permute-start | bytes 1179656 | tf_op jit(solution)/shard_map/ppermute | solution.py:50
  88.6 19.2 %collective-permute-start.14 = (f32[2,128,512]{2,1,0:T(8,128)S(1)}, f32[2,128,512]{2,1,0:T(8,128)S(1)}, u32[]{:S(2)}, u32[]{:S(2)}) collective-permute-start(f32[2,128,512]{2,1,0:T(8,128)S(1)} %get-tuple-element.15), channel_id=1, source_target_pairs={{0,8},{8,16},{16,24},{24,32},{32,40},{40,48},{48,56},{56,64},{64,7... | collective-permute-start | bytes 1572872 | tf_op jit(solution)/shard_map/ppermute | solution.py:265
  91.8 17.2 %collective-permute-start.15 = (f32[2,128,512]{2,1,0:T(8,128)S(1)}, f32[2,128,512]{2,1,0:T(8,128)S(1)}, u32[]{:S(2)}, u32[]{:S(2)}) collective-permute-start(f32[2,128,512]{2,1,0:T(8,128)S(1)} %get-tuple-element.16), channel_id=1, source_target_pairs={{8,0},{16,8},{24,16},{32,24},{40,32},{48,40},{56,48},{64,56},{72,6... | collective-permute-start | bytes 1572872 | tf_op jit(solution)/shard_map/ppermute | solution.py:266
  110.2 3.4 %collective-permute-start.16 = (f32[2,2,2,16,512]{4,3,2,1,0:T(8,128)S(1)}, f32[2,2,2,16,512]{4,3,2,1,0:T(8,128)S(1)}, u32[]{:S(2)}, u32[]{:S(2)}) collective-permute-start(f32[2,2,2,16,512]{4,3,2,1,0:T(8,128)S(1)} %dynamic-slice_bitcast_fusion.1), channel_id=1, source_target_pairs={{0,1},{1,0},{2,3},{3,2},{4,5},{5,4},{6,7},{7,6},{8,9},{9,8},{10,11... | collective-permute-start | bytes 786440 | tf_op jit(solution)/shard_map/ppermute | solution.py:66
  113.7 13.5 %collective-permute-start.17 = (f32[2,2,16,512]{3,2,0,1:T(8,128)S(1)}, f32[2,2,16,512]{3,2,0,1:T(8,128)S(1)}, u32[]{:S(2)}, u32[]{:S(2)}) collective-permute-start(f32[2,2,16,512]{3,2,0,1:T(8,128)S(1)} %bitcast.74), channel_id=1, source_target_pairs={{0,6},{1,7},{2,4},{3,5},{4,2},{5,3},{6,0},{7,1},{8,14},{9,15},{10,... | collective-permute-start | bytes 393224 | tf_op jit(solution)/shard_map/ppermute | solution.py:66
  117.6 11.6 %collective-permute-start.19 = (f32[16,512]{1,0:T(8,128)S(1)}, f32[16,512]{1,0:T(8,128)S(1)}, u32[]{:S(2)}, u32[]{:S(2)}) collective-permute-start(f32[16,512]{1,0:T(8,128)S(1)} %get-tuple-element.17), channel_id=1, source_target_pairs={{0,8},{8,16},{16,24},{24,32},{32,40},{40,48},{48,56},{56,64},{64,7... | collective-permute-start | bytes 98312 | tf_op jit(solution)/shard_map/ppermute | solution.py:276
  119.5 9.7 %collective-permute-start.20 = (f32[16,512]{1,0:T(8,128)S(1)}, f32[16,512]{1,0:T(8,128)S(1)}, u32[]{:S(2)}, u32[]{:S(2)}) collective-permute-start(f32[16,512]{1,0:T(8,128)S(1)} %get-tuple-element.18), channel_id=1, source_target_pairs={{8,0},{16,8},{24,16},{32,24},{40,32},{48,40},{56,48},{64,56},{72,6... | collective-permute-start | bytes 98312 | tf_op jit(solution)/shard_map/ppermute | solution.py:277
  127.3 6.2 %collective-permute-start.18 = (f32[2,16,512]{2,1,0:T(8,128)S(1)}, f32[2,16,512]{2,1,0:T(8,128)S(1)}, u32[]{:S(2)}, u32[]{:S(2)}) collective-permute-start(f32[2,16,512]{2,1,0:T(8,128)S(1)} %dynamic-slice_bitcast_fusion.3), channel_id=1, source_target_pairs={{0,2},{1,3},{2,0},{3,1},{4,6},{5,7},{6,4},{7,5},{8,10},{9,11},{10,... | collective-permute-start | bytes 196616 | tf_op jit(solution)/shard_map/ppermute | solution.py:66

commit v3 on v2

--- a/solution.py
+++ b/solution.py
@@ -71,11 +71,22 @@
     return jnp.dot(a, b, preferred_element_type=jnp.float32)
 
 
-def forward_kernel(roff, coff, cnt, ext_ref, probe_ref, fr_ref, fi_ref, ppt_ref, exit_ref, wave_ref, power_ref):
+def forward_kernel(roff, coff, cnt, before_ref, own_ref, after_ref, probe_ref, fr_ref, fi_ref,
+                   exit_ref, wave_ref, power_ref, ext_ref):
     j = pl.program_id(0)
     pat = probe_ref.shape[1]
     width = ext_ref.shape[2]
+    band = own_ref.shape[1]
     live = j < cnt[0]
+
+    @pl.when(j == 0)
+    def _():
+        ext_ref[:, :band, :] = before_ref[...]
+        ext_ref[:, band : 2 * band, :] = own_ref[...]
+        ext_ref[:, 2 * band :, :] = after_ref[...]
+        p_re = probe_ref[0]
+        p_im = probe_ref[1]
+        power_ref[power_ref.shape[0] - 1] = p_re * p_re + p_im * p_im
 
     @pl.when(live)
     def _():
@@ -105,11 +116,11 @@
         exit_ref[0, 1] = e_im
         wave_ref[0, 0] = v_re
         wave_ref[0, 1] = v_im
-        power_ref[0] = v_re * v_re + v_im * v_im
+        power_ref[j] = v_re * v_re + v_im * v_im
 
     @pl.when(jnp.logical_not(live))
     def _():
-        power_ref[...] = jnp.zeros(power_ref.shape, jnp.float32)
+        power_ref[j] = jnp.zeros((pat, pat), jnp.float32)
 
 
 def backward_kernel(roff, coff, cnt, exit_ref, wave_ref, model_ref, meas_ref, probe_ref, ppt_ref,
@@ -153,46 +164,48 @@
 
         numer_ref[0, pl.ds(base, span), :] += place(n_re)
         numer_ref[1, pl.ds(base, span), :] += place(n_im)
-        illum_ref[pl.ds(base, span), :] += place(ppt_ref[...])
-
-
-def run_forward(ext, probe2, fr, fi, ppt, roff, coff, cnt):
+        illum_ref[pl.ds(base, span), :] += place(ppt_ref[0])
+
+
+def run_forward(before, own, after, probe2, fr, fi, roff, coff, cnt):
     slots = roff.shape[0]
     pat = probe2.shape[1]
     whole3 = lambda j, *_: (0, 0, 0)
     whole2 = lambda j, *_: (0, 0)
     per4 = lambda j, *_: (j, 0, 0, 0)
-    per3 = lambda j, *_: (j, 0, 0)
     flops = slots * 8 * 2 * pat ** 3
+    ext_shape = (2, 3 * own.shape[1], own.shape[2])
     return pl.pallas_call(
         forward_kernel,
         grid_spec=pltpu.PrefetchScalarGridSpec(
             num_scalar_prefetch=3,
             grid=(slots,),
             in_specs=[
-                pl.BlockSpec(ext.shape, whole3),
+                pl.BlockSpec(before.shape, whole3),
+                pl.BlockSpec(own.shape, whole3),
+                pl.BlockSpec(after.shape, whole3),
                 pl.BlockSpec(probe2.shape, whole3),
                 pl.BlockSpec(fr.shape, whole2),
                 pl.BlockSpec(fi.shape, whole2),
-                pl.BlockSpec(ppt.shape, whole2),
             ],
             out_specs=[
                 pl.BlockSpec((1, 2, pat, pat), per4),
                 pl.BlockSpec((1, 2, pat, pat), per4),
-                pl.BlockSpec((1, pat, pat), per3),
+                pl.BlockSpec((slots + 1, pat, pat), whole3),
             ],
+            scratch_shapes=[pltpu.VMEM(ext_shape, jnp.float32)],
         ),
         out_shape=[
             jax.ShapeDtypeStruct((slots, 2, pat, pat), jnp.bfloat16),
             jax.ShapeDtypeStruct((slots, 2, pat, pat), jnp.float32),
-            jax.ShapeDtypeStruct((slots, pat, pat), jnp.float32),
+            jax.ShapeDtypeStruct((slots + 1, pat, pat), jnp.float32),
         ],
         compiler_params=pltpu.CompilerParams(dimension_semantics=("arbitrary",)),
         cost_estimate=pl.CostEstimate(flops=flops, transcendentals=0, bytes_accessed=8 * 1024 * 1024),
-    )(roff, coff, cnt, ext, probe2, fr, fi, ppt)
-
-
-def run_backward(exits, waves, model, measured, probe2, ppt, fr, fi, roff, coff, cnt, ext_rows, width):
+    )(roff, coff, cnt, before, own, after, probe2, fr, fi)
+
+
+def run_backward(exits, waves, totals, measured, probe2, fr, fi, roff, coff, cnt, ext_rows, width):
     slots = roff.shape[0]
     pat = probe2.shape[1]
     whole3 = lambda j, *_: (0, 0, 0)
@@ -211,7 +224,7 @@
                 pl.BlockSpec((1, pat, pat), per3),
                 pl.BlockSpec((1, pat, pat), per3),
                 pl.BlockSpec(probe2.shape, whole3),
-                pl.BlockSpec(ppt.shape, whole2),
+                pl.BlockSpec((1, pat, pat), lambda j, *_: (slots, 0, 0)),
                 pl.BlockSpec(fr.shape, whole2),
                 pl.BlockSpec(fi.shape, whole2),
             ],
@@ -226,7 +239,7 @@
         ],
         compiler_params=pltpu.CompilerParams(dimension_semantics=("arbitrary",)),
         cost_estimate=pl.CostEstimate(flops=flops, transcendentals=0, bytes_accessed=12 * 1024 * 1024),
-    )(roff, coff, cnt, exits, waves, model, measured, probe2, ppt, fr, fi)
+    )(roff, coff, cnt, exits, waves, totals, measured, probe2, totals, fr, fi)
 
 
 def local(object_field, probe, measured, row_offsets, col_offsets, tile_counts):
@@ -240,45 +253,49 @@
     fr, fi = dft_tables(pattern)
     probe2 = probe[:, 0]
 
-    probe_power = allreduce_mode(probe2[0] * probe2[0] + probe2[1] * probe2[1])
-
     before = lax.ppermute(object_field, "pos", neighbour_pairs(pos_count, 1))
     after = lax.ppermute(object_field, "pos", neighbour_pairs(pos_count, -1))
-    ext = jnp.concatenate([before, object_field, after], axis=1)
-    ext_rows = ext.shape[1]
+    ext_rows = 3 * rows_tile
 
     roff = row_offsets.astype(jnp.int32)
     coff = col_offsets.astype(jnp.int32)
     cnt = tile_counts.astype(jnp.int32)
 
-    exits, waves, power = run_forward(ext, probe2, fr, fi, probe_power, roff, coff, cnt)
-    model = allreduce_mode(power)
+    exits, waves, power = run_forward(before, object_field, after, probe2, fr, fi, roff, coff, cnt)
+    totals = allreduce_mode(power)
     numer, illum = run_backward(
-        exits, waves, model, measured, probe2, probe_power, fr, fi, roff, coff, cnt, ext_rows, width
-    )
-
-    top = numer[:, :rows_tile]
-    mid = numer[:, rows_tile : 2 * rows_tile]
-    bottom = numer[:, 2 * rows_tile :]
-    tile_numer = (
-        mid
-        + lax.ppermute(bottom, "pos", neighbour_pairs(pos_count, 1))
-        + lax.ppermute(top, "pos", neighbour_pairs(pos_count, -1))
-    )
-    numer_rows = reduce_scatter_mode(tile_numer)
+        exits, waves, totals, measured, probe2, fr, fi, roff, coff, cnt, ext_rows, width
+    )
+
+    core_pairs, near, far = mode_pairs()
+    core = my_mode % 2
+    blocks = numer.reshape(2, 3, 2, 2, 2, share_rows, width)
+    keep = lax.dynamic_index_in_dim(blocks, core, axis=4, keepdims=False)
+    send = lax.dynamic_index_in_dim(blocks, 1 - core, axis=4, keepdims=False)
+    blocks = keep + lax.ppermute(send, "mode", core_pairs)
+    band_rows = 2 * 4 * share_rows
+    own_illum = lax.dynamic_index_in_dim(
+        illum.reshape(3, mode_count, share_rows, width), my_mode, axis=1, keepdims=False
+    )
+    to_next = jnp.concatenate([blocks[:, 2].reshape(band_rows, width), own_illum[2]], axis=0)
+    to_prev = jnp.concatenate([blocks[:, 0].reshape(band_rows, width), own_illum[0]], axis=0)
+    from_prev = lax.ppermute(to_next, "pos", neighbour_pairs(pos_count, 1))
+    from_next = lax.ppermute(to_prev, "pos", neighbour_pairs(pos_count, -1))
+    tile = (
+        blocks[:, 1]
+        + from_prev[:band_rows].reshape(blocks[:, 1].shape)
+        + from_next[:band_rows].reshape(blocks[:, 1].shape)
+    )
+    illum_rows = own_illum[1] + from_prev[band_rows:] + from_next[band_rows:]
+    for pairs, d in ((far, 4), (near, 2)):
+        bit = (my_mode // d) % 2
+        keep = lax.dynamic_index_in_dim(tile, bit, axis=1, keepdims=False)
+        send = lax.dynamic_index_in_dim(tile, 1 - bit, axis=1, keepdims=False)
+        tile = keep + lax.ppermute(send, "mode", pairs)
 
     start = my_mode * share_rows
-    illum_top = lax.dynamic_slice_in_dim(illum, start, share_rows, 0)
-    illum_mid = lax.dynamic_slice_in_dim(illum, rows_tile + start, share_rows, 0)
-    illum_bottom = lax.dynamic_slice_in_dim(illum, 2 * rows_tile + start, share_rows, 0)
-    illum_rows = (
-        illum_mid
-        + lax.ppermute(illum_bottom, "pos", neighbour_pairs(pos_count, 1))
-        + lax.ppermute(illum_top, "pos", neighbour_pairs(pos_count, -1))
-    )
-
     own_rows = lax.dynamic_slice_in_dim(object_field, start, share_rows, 1)
-    return own_rows + numer_rows / (illum_rows + 1.0)
+    return own_rows + tile / (illum_rows + 1.0)
 
 
 def solution(mesh):

time: 135 us -> 116 us (0.86)
  the two profiles are of different devices: /device:TPU:384 before, /device:TPU:120 now
where the time goes in v3:
time: 116 us
  waiting for transfers between devices  53.9 us (46%)
  starting transfers between devices  36.6 us (32%)
  Pallas kernels  13.2 us (11%)
  other arithmetic  6.71 us (6%)
  local copies, waits for them, and re-layouts  4.11 us (4%)
    ppermute x2, waiting for transfers between devices, local(): tile = keep + lax.ppermute(send, 'mode', pairs)  8.42 us
    ppermute x1, waiting for transfers between devices, local(): after = lax.ppermute(object_field, 'pos', neighbour_pairs(pos_count, -1))  7.33 us
    ppermute x1, waiting for transfers between devices, local(): before = lax.ppermute(object_field, 'pos', neighbour_pairs(pos_count, 1))  7.12 us
    pallas_call x1, Pallas kernels, run_backward(): pl.pallas_call(backward_kernel, grid_spec=pltpu.PrefetchScalarGridSpec(nu...  7.07 us
    ppermute x1, waiting for transfers between devices, local(): from_next = lax.ppermute(to_prev, 'pos', neighbour_pairs(pos_count, -1))  6.97 us
    pallas_call x1, Pallas kernels, run_forward(): pl.pallas_call(forward_kernel, grid_spec=pltpu.PrefetchScalarGridSpec(num...  6.17 us
    ppermute x1, waiting for transfers between devices, local(): from_prev = lax.ppermute(to_next, 'pos', neighbour_pairs(pos_count, 1))  5.02 us
    ppermute x2, starting transfers between devices, local(): tile = keep + lax.ppermute(send, 'mode', pairs)  4.97 us
  transfers between devices with their start and end apart: 13, of which 13 were waited for; matrix products, arithmetic and copies ran while one was open for 3% of the time, Pallas kernels for 0%

profile of v3, /device:TPU:120, one launch (start us, length us, event | category | flops | bytes accessed | tf_op | source)
XLA Modules:
  0.0 115.6 jit_solution(11584854270038935955)
XLA Ops:
  0.0 4.7 %collective-permute-start = (f32[2,128,512]{2,1,0:T(8,128)}, f32[2,128,512]{2,1,0:T(8,128)S(1)}, u32[]{:S(2)}, u32[]{:S(2)}) collective-permute-start(f32[2,128,512]{2,1,0:T(8,128)} %own_ref.1), channel_id=1, source_target_pairs={{0,8},{8,16},{16,24},{24,32},{32,40},{40,48},{48,56},{56,64},{64,7... | collective-permute-start | bytes 1572872 | tf_op jit(solution)/shard_map/ppermute | solution.py:256
  4.7 1.9 %collective-permute-start.1 = (f32[2,128,512]{2,1,0:T(8,128)}, f32[2,128,512]{2,1,0:T(8,128)S(1)}, u32[]{:S(2)}, u32[]{:S(2)}) collective-permute-start(f32[2,128,512]{2,1,0:T(8,128)} %own_ref.1), channel_id=1, source_target_pairs={{8,0},{16,8},{24,16},{32,24},{40,32},{48,40},{56,48},{64,56},{72,6... | collective-permute-start | bytes 1572872 | tf_op jit(solution)/shard_map/ppermute | solution.py:257
  9.0 7.1 %collective-permute-done.before_ref = f32[2,128,512]{2,1,0:T(8,128)S(1)} collective-permute-done((f32[2,128,512]{2,1,0:T(8,128)}, f32[2,128,512]{2,1,0:T(8,128)S(1)}, u32[]{:S(2)}, u32[]{:S(2)}) %collective-permute-start) | collective-permute-done | bytes 524320 | tf_op jit(solution)/shard_map/ppermute | solution.py:256
  16.2 7.3 %collective-permute-done.1.after_ref = f32[2,128,512]{2,1,0:T(8,128)S(1)} collective-permute-done((f32[2,128,512]{2,1,0:T(8,128)}, f32[2,128,512]{2,1,0:T(8,128)S(1)}, u32[]{:S(2)}, u32[]{:S(2)}) %collective-permute-start.1) | collective-permute-done | bytes 524320 | tf_op jit(solution)/shard_map/ppermute | solution.py:257
  24.3 6.2 %shard_map.64 = (bf16[3,2,256,256]{3,2,1,0:T(8,128)(2,1)}, f32[3,2,256,256]{3,2,1,0:T(8,128)}, f32[4,256,256]{2,1,0:T(8,128)}) custom-call(s32[3]{0:T(128)} %roff.3, s32[3]{0:T(128)} %coff.3, s32[1]{0:T(128)S(6)} %copy.13.cnt, f32[2,128,512]{2,1,0:T(8,128)} %copy-done.1, f32[2,128,512]{2,1,0:T(8,128)} %own_ref.1, f32[2,128,512]{2,1,0:T(8,128)} %copy-done.2, ...), custom_call_target="tpu_custom_call" | custom-call | flops 805306368 | bytes 8388608 | tf_op jit(solution)/shard_map/pallas_call | solution.py:178
  36.5 3.4 %collective-permute-start.3 = (f32[256,256]{1,0:T(8,128)S(1)}, f32[256,256]{1,0:T(8,128)S(1)}, u32[]{:S(2)}, u32[]{:S(2)}) collective-permute-start(f32[256,256]{1,0:T(8,128)S(1)} %get-tuple-element.23), channel_id=1, source_target_pairs={{0,2},{1,3},{2,0},{3,1},{4,6},{5,7},{6,4},{7,5},{8,10},{9,11},{10,... | collective-permute-start | bytes 786440 | tf_op jit(solution)/shard_map/ppermute | solution.py:45
  39.9 4.0 %collective-permute-start.5 = (f32[256,256]{1,0:T(8,128)S(1)}, f32[256,256]{1,0:T(8,128)S(1)}, u32[]{:S(2)}, u32[]{:S(2)}) collective-permute-start(f32[256,256]{1,0:T(8,128)S(1)} %get-tuple-element.24), channel_id=1, source_target_pairs={{0,6},{1,7},{2,4},{3,5},{4,2},{5,3},{6,0},{7,1},{8,14},{9,15},{10,... | collective-permute-start | bytes 786440 | tf_op jit(solution)/shard_map/ppermute | solution.py:46
  43.9 2.8 %collective-permute-done.3 = f32[256,256]{1,0:T(8,128)S(1)} collective-permute-done((f32[256,256]{1,0:T(8,128)S(1)}, f32[256,256]{1,0:T(8,128)S(1)}, u32[]{:S(2)}, u32[]{:S(2)}) %collective-permute-start.3) | collective-permute-done | bytes 262176 | tf_op jit(solution)/shard_map/ppermute | solution.py:45
  46.7 4.3 %collective-permute-done.5 = f32[256,256]{1,0:T(8,128)S(1)} collective-permute-done((f32[256,256]{1,0:T(8,128)S(1)}, f32[256,256]{1,0:T(8,128)S(1)}, u32[]{:S(2)}, u32[]{:S(2)}) %collective-permute-start.5) | collective-permute-done | bytes 262176 | tf_op jit(solution)/shard_map/ppermute | solution.py:46
  51.2 4.0 %collective-permute-start.4 = (f32[256,256]{1,0:T(8,128)S(1)}, f32[256,256]{1,0:T(8,128)S(1)}, u32[]{:S(2)}, u32[]{:S(2)}) collective-permute-start(f32[256,256]{1,0:T(8,128)S(1)} %get-tuple-element.21), channel_id=1, source_target_pairs={{0,6},{1,7},{2,4},{3,5},{4,2},{5,3},{6,0},{7,1},{8,14},{9,15},{10,... | collective-permute-start | bytes 786440 | tf_op jit(solution)/shard_map/ppermute | solution.py:47
  55.2 1.9 %collective-permute-start.6 = (f32[256,256]{1,0:T(8,128)S(1)}, f32[256,256]{1,0:T(8,128)S(1)}, u32[]{:S(2)}, u32[]{:S(2)}) collective-permute-start(f32[256,256]{1,0:T(8,128)S(1)} %get-tuple-element.22), channel_id=1, source_target_pairs={{0,2},{1,3},{2,0},{3,1},{4,6},{5,7},{6,4},{7,5},{8,10},{9,11},{10,... | collective-permute-start | bytes 786440 | tf_op jit(solution)/shard_map/ppermute | solution.py:48
  57.1 4.4 %collective-permute-done.4 = f32[256,256]{1,0:T(8,128)S(1)} collective-permute-done((f32[256,256]{1,0:T(8,128)S(1)}, f32[256,256]{1,0:T(8,128)S(1)}, u32[]{:S(2)}, u32[]{:S(2)}) %collective-permute-start.4) | collective-permute-done | bytes 262176 | tf_op jit(solution)/shard_map/ppermute | solution.py:47
  61.5 2.5 %collective-permute-done.6 = f32[256,256]{1,0:T(8,128)S(1)} collective-permute-done((f32[256,256]{1,0:T(8,128)S(1)}, f32[256,256]{1,0:T(8,128)S(1)}, u32[]{:S(2)}, u32[]{:S(2)}) %collective-permute-start.6) | collective-permute-done | bytes 262176 | tf_op jit(solution)/shard_map/ppermute | solution.py:48
  64.1 1.9 %collective-permute-start.7 = (f32[2,256,256]{2,1,0:T(8,128)S(1)}, f32[2,256,256]{2,1,0:T(8,128)S(1)}, u32[]{:S(2)}, u32[]{:S(2)}) collective-permute-start(f32[2,256,256]{2,1,0:T(8,128)S(1)} %pad_maximum_fusion.1), channel_id=1, source_target_pairs={{0,1},{1,0},{2,3},{3,2},{4,5},{5,4},{6,7},{7,6},{8,9},{9,8},{10,11... | collective-permute-start | bytes 1572872 | tf_op jit(solution)/shard_map/ppermute | solution.py:50
  69.0 7.1 %shard_map.65 = (f32[2,384,512]{2,1,0:T(8,128)}, f32[384,512]{1,0:T(8,128)}) custom-call(s32[3]{0:T(128)} %roff.3, s32[3]{0:T(128)} %coff.3, s32[1]{0:T(128)S(6)} %copy.13.cnt, bf16[3,2,256,256]{3,2,1,0:T(8,128)(2,1)} %get-tuple-element.10.exit_ref, f32[3,2,256,256]{3,2,1,0:T(8,128)} %get-tuple-element.11.wave_ref, f32[4,256,256]{2,1,0:T(8,128)} %bitcast.63, ...), custom_call_target="tpu_custom_call" | custom-call | flops 805306368 | bytes 12582912 | tf_op jit(solution)/shard_map/pallas_call | solution.py:216
  77.4 2.0 %collective-permute-start.8 = (f32[2,3,2,2,16,512]{5,4,3,2,1,0:T(8,128)S(1)}, f32[2,3,2,2,16,512]{5,4,3,2,1,0:T(8,128)S(1)}, u32[]{:S(2)}, u32[]{:S(2)}) collective-permute-start(f32[2,3,2,2,16,512]{5,4,3,2,1,0:T(8,128)S(1)} %dynamic-slice_bitcast_fusion), channel_id=1, source_target_pairs={{0,1},{1,0},{2,3},{3,2},{4,5},{5,4},{6,7},{7,6},{8,9},{9,8},{10,11... | collective-permute-start | bytes 2359304 | tf_op jit(solution)/shard_map/ppermute | solution.py:275
  81.8 3.9 %collective-permute-start.9 = (f32[144,512]{1,0:T(8,128)S(1)}, f32[144,512]{1,0:T(8,128)S(1)}, u32[]{:S(2)}, u32[]{:S(2)}) collective-permute-start(f32[144,512]{1,0:T(8,128)S(1)} %pad_maximum_fusion.2), channel_id=1, source_target_pairs={{0,8},{8,16},{16,24},{24,32},{32,40},{40,48},{48,56},{56,64},{64,7... | collective-permute-start | bytes 884744 | tf_op jit(solution)/shard_map/ppermute | solution.py:282
  85.8 1.9 %collective-permute-start.10 = (f32[144,512]{1,0:T(8,128)S(1)}, f32[144,512]{1,0:T(8,128)S(1)}, u32[]{:S(2)}, u32[]{:S(2)}) collective-permute-start(f32[144,512]{1,0:T(8,128)S(1)} %pad_maximum_fusion.3), channel_id=1, source_target_pairs={{8,0},{16,8},{24,16},{32,24},{40,32},{48,40},{56,48},{64,56},{72,6... | collective-permute-start | bytes 884744 | tf_op jit(solution)/shard_map/ppermute | solution.py:283
  87.7 5.0 %collective-permute-done.9 = f32[144,512]{1,0:T(8,128)S(1)} collective-permute-done((f32[144,512]{1,0:T(8,128)S(1)}, f32[144,512]{1,0:T(8,128)S(1)}, u32[]{:S(2)}, u32[]{:S(2)}) %collective-permute-start.9) | collective-permute-done | bytes 294944 | tf_op jit(solution)/shard_map/ppermute | solution.py:282
  92.8 7.0 %collective-permute-done.10 = f32[144,512]{1,0:T(8,128)S(1)} collective-permute-done((f32[144,512]{1,0:T(8,128)S(1)}, f32[144,512]{1,0:T(8,128)S(1)}, u32[]{:S(2)}, u32[]{:S(2)}) %collective-permute-start.10) | collective-permute-done | bytes 294944 | tf_op jit(solution)/shard_map/ppermute | solution.py:283
  99.9 3.1 %collective-permute-start.11 = (f32[2,2,16,512]{3,2,1,0:T(8,128)S(1)}, f32[2,2,16,512]{3,2,1,0:T(8,128)S(1)}, u32[]{:S(2)}, u32[]{:S(2)}) collective-permute-start(f32[2,2,16,512]{3,2,1,0:T(8,128)S(1)} %dynamic-slice_bitcast_fusion.2), channel_id=1, source_target_pairs={{0,6},{1,7},{2,4},{3,5},{4,2},{5,3},{6,0},{7,1},{8,14},{9,15},{10,... | collective-permute-start | bytes 393224 | tf_op jit(solution)/shard_map/ppermute | solution.py:294
  103.0 5.0 %collective-permute-done.11 = f32[2,2,16,512]{3,2,1,0:T(8,128)S(1)} collective-permute-done((f32[2,2,16,512]{3,2,1,0:T(8,128)S(1)}, f32[2,2,16,512]{3,2,1,0:T(8,128)S(1)}, u32[]{:S(2)}, u32[]{:S(2)}) %collective-permute-start.11) | collective-permute-done | bytes 131104 | tf_op jit(solution)/shard_map/ppermute | solution.py:294
  108.0 1.9 %collective-permute-start.12 = (f32[2,16,512]{2,1,0:T(8,128)S(1)}, f32[2,16,512]{2,1,0:T(8,128)S(1)}, u32[]{:S(2)}, u32[]{:S(2)}) collective-permute-start(f32[2,16,512]{2,1,0:T(8,128)S(1)} %dynamic-slice_bitcast_fusion.3), channel_id=1, source_target_pairs={{0,2},{1,3},{2,0},{3,1},{4,6},{5,7},{6,4},{7,5},{8,10},{9,11},{10,... | collective-permute-start | bytes 196616 | tf_op jit(solution)/shard_map/ppermute | solution.py:294
  110.7 3.5 %collective-permute-done.12 = f32[2,16,512]{2,1,0:T(8,128)S(1)} collective-permute-done((f32[2,16,512]{2,1,0:T(8,128)S(1)}, f32[2,16,512]{2,1,0:T(8,128)S(1)}, u32[]{:S(2)}, u32[]{:S(2)}) %collective-permute-start.12) | collective-permute-done | bytes 65568 | tf_op jit(solution)/shard_map/ppermute | solution.py:294
  (34 shorter events, 17.8 us)
Async XLA Ops:
  0.0 16.2 %collective-permute-start = (f32[2,128,512]{2,1,0:T(8,128)}, f32[2,128,512]{2,1,0:T(8,128)S(1)}, u32[]{:S(2)}, u32[]{:S(2)}) collective-permute-start(f32[2,128,512]{2,1,0:T(8,128)} %own_ref.1), channel_id=1, source_target_pairs={{0,8},{8,16},{16,24},{24,32},{32,40},{40,48},{48,56},{56,64},{64,7... | collective-permute-start | bytes 1572872 | tf_op jit(solution)/shard_map/ppermute | solution.py:256
  4.7 18.8 %collective-permute-start.1 = (f32[2,128,512]{2,1,0:T(8,128)}, f32[2,128,512]{2,1,0:T(8,128)S(1)}, u32[]{:S(2)}, u32[]{:S(2)}) collective-permute-start(f32[2,128,512]{2,1,0:T(8,128)} %own_ref.1), channel_id=1, source_target_pairs={{8,0},{16,8},{24,16},{32,24},{40,32},{48,40},{56,48},{64,56},{72,6... | collective-permute-start | bytes 1572872 | tf_op jit(solution)/shard_map/ppermute | solution.py:257
  16.2 7.3 %copy-start.1 = (f32[2,128,512]{2,1,0:T(8,128)}, f32[2,128,512]{2,1,0:T(8,128)S(1)}, u32[]{:S(2)}) copy-start(f32[2,128,512]{2,1,0:T(8,128)S(1)} %collective-permute-done.before_ref) | copy-start | bytes 1572868
  23.5 0.8 copy-start.2
  31.5 3.8 %collective-permute-start.2 = (f32[2,256,256]{2,1,0:T(8,128)S(1)}, f32[2,256,256]{2,1,0:T(8,128)S(1)}, u32[]{:S(2)}, u32[]{:S(2)}) collective-permute-start(f32[2,256,256]{2,1,0:T(8,128)S(1)} %dynamic-slice_bitcast_fusion.1), channel_id=1, source_target_pairs={{0,1},{1,0},{2,3},{3,2},{4,5},{5,4},{6,7},{7,6},{8,9},{9,8},{10,11... | collective-permute-start | bytes 1572872 | tf_op jit(solution)/shard_map/ppermute | solution.py:43
  36.5 10.2 %collective-permute-start.3 = (f32[256,256]{1,0:T(8,128)S(1)}, f32[256,256]{1,0:T(8,128)S(1)}, u32[]{:S(2)}, u32[]{:S(2)}) collective-permute-start(f32[256,256]{1,0:T(8,128)S(1)} %get-tuple-element.23), channel_id=1, source_target_pairs={{0,2},{1,3},{2,0},{3,1},{4,6},{5,7},{6,4},{7,5},{8,10},{9,11},{10,... | collective-permute-start | bytes 786440 | tf_op jit(solution)/shard_map/ppermute | solution.py:45
  39.9 11.2 %collective-permute-start.5 = (f32[256,256]{1,0:T(8,128)S(1)}, f32[256,256]{1,0:T(8,128)S(1)}, u32[]{:S(2)}, u32[]{:S(2)}) collective-permute-start(f32[256,256]{1,0:T(8,128)S(1)} %get-tuple-element.24), channel_id=1, source_target_pairs={{0,6},{1,7},{2,4},{3,5},{4,2},{5,3},{6,0},{7,1},{8,14},{9,15},{10,... | collective-permute-start | bytes 786440 | tf_op jit(solution)/shard_map/ppermute | solution.py:46
  51.2 10.3 %collective-permute-start.4 = (f32[256,256]{1,0:T(8,128)S(1)}, f32[256,256]{1,0:T(8,128)S(1)}, u32[]{:S(2)}, u32[]{:S(2)}) collective-permute-start(f32[256,256]{1,0:T(8,128)S(1)} %get-tuple-element.21), channel_id=1, source_target_pairs={{0,6},{1,7},{2,4},{3,5},{4,2},{5,3},{6,0},{7,1},{8,14},{9,15},{10,... | collective-permute-start | bytes 786440 | tf_op jit(solution)/shard_map/ppermute | solution.py:47
  55.2 8.8 %collective-permute-start.6 = (f32[256,256]{1,0:T(8,128)S(1)}, f32[256,256]{1,0:T(8,128)S(1)}, u32[]{:S(2)}, u32[]{:S(2)}) collective-permute-start(f32[256,256]{1,0:T(8,128)S(1)} %get-tuple-element.22), channel_id=1, source_target_pairs={{0,2},{1,3},{2,0},{3,1},{4,6},{5,7},{6,4},{7,5},{8,10},{9,11},{10,... | collective-permute-start | bytes 786440 | tf_op jit(solution)/shard_map/ppermute | solution.py:48
  64.1 3.8 %collective-permute-start.7 = (f32[2,256,256]{2,1,0:T(8,128)S(1)}, f32[2,256,256]{2,1,0:T(8,128)S(1)}, u32[]{:S(2)}, u32[]{:S(2)}) collective-permute-start(f32[2,256,256]{2,1,0:T(8,128)S(1)} %pad_maximum_fusion.1), channel_id=1, source_target_pairs={{0,1},{1,0},{2,3},{3,2},{4,5},{5,4},{6,7},{7,6},{8,9},{9,8},{10,11... | collective-permute-start | bytes 1572872 | tf_op jit(solution)/shard_map/ppermute | solution.py:50
  76.1 5.5 %copy-start = (f32[2,384,512]{2,1,0:T(8,128)S(1)}, f32[2,384,512]{2,1,0:T(8,128)}, u32[]{:S(2)}) copy-start(f32[2,384,512]{2,1,0:T(8,128)} %get-tuple-element.13) | copy-start | bytes 4718596
  77.4 4.2 %collective-permute-start.8 = (f32[2,3,2,2,16,512]{5,4,3,2,1,0:T(8,128)S(1)}, f32[2,3,2,2,16,512]{5,4,3,2,1,0:T(8,128)S(1)}, u32[]{:S(2)}, u32[]{:S(2)}) collective-permute-start(f32[2,3,2,2,16,512]{5,4,3,2,1,0:T(8,128)S(1)} %dynamic-slice_bitcast_fusion), channel_id=1, source_target_pairs={{0,1},{1,0},{2,3},{3,2},{4,5},{5,4},{6,7},{7,6},{8,9},{9,8},{10,11... | collective-permute-start | bytes 2359304 | tf_op jit(solution)/shard_map/ppermute | solution.py:275
  81.8 10.9 %collective-permute-start.9 = (f32[144,512]{1,0:T(8,128)S(1)}, f32[144,512]{1,0:T(8,128)S(1)}, u32[]{:S(2)}, u32[]{:S(2)}) collective-permute-start(f32[144,512]{1,0:T(8,128)S(1)} %pad_maximum_fusion.2), channel_id=1, source_target_pairs={{0,8},{8,16},{16,24},{24,32},{32,40},{40,48},{48,56},{56,64},{64,7... | collective-permute-start | bytes 884744 | tf_op jit(solution)/shard_map/ppermute | solution.py:282
  85.8 14.0 %collective-permute-start.10 = (f32[144,512]{1,0:T(8,128)S(1)}, f32[144,512]{1,0:T(8,128)S(1)}, u32[]{:S(2)}, u32[]{:S(2)}) collective-permute-start(f32[144,512]{1,0:T(8,128)S(1)} %pad_maximum_fusion.3), channel_id=1, source_target_pairs={{8,0},{16,8},{24,16},{32,24},{40,32},{48,40},{56,48},{64,56},{72,6... | collective-permute-start | bytes 884744 | tf_op jit(solution)/shard_map/ppermute | solution.py:283
  99.9 8.1 %collective-permute-start.11 = (f32[2,2,16,512]{3,2,1,0:T(8,128)S(1)}, f32[2,2,16,512]{3,2,1,0:T(8,128)S(1)}, u32[]{:S(2)}, u32[]{:S(2)}) collective-permute-start(f32[2,2,16,512]{3,2,1,0:T(8,128)S(1)} %dynamic-slice_bitcast_fusion.2), channel_id=1, source_target_pairs={{0,6},{1,7},{2,4},{3,5},{4,2},{5,3},{6,0},{7,1},{8,14},{9,15},{10,... | collective-permute-start | bytes 393224 | tf_op jit(solution)/shard_map/ppermute | solution.py:294
  108.0 6.2 %collective-permute-start.12 = (f32[2,16,512]{2,1,0:T(8,128)S(1)}, f32[2,16,512]{2,1,0:T(8,128)S(1)}, u32[]{:S(2)}, u32[]{:S(2)}) collective-permute-start(f32[2,16,512]{2,1,0:T(8,128)S(1)} %dynamic-slice_bitcast_fusion.3), channel_id=1, source_target_pairs={{0,2},{1,3},{2,0},{3,1},{4,6},{5,7},{6,4},{7,5},{8,10},{9,11},{10,... | collective-permute-start | bytes 196616 | tf_op jit(solution)/shard_map/ppermute | solution.py:294

commit v4 on v3

--- a/solution.py
+++ b/solution.py
@@ -35,22 +35,11 @@
 
 
 def allreduce_mode(x):
-    core_pairs, near, far = mode_pairs()
-    core = lax.axis_index("mode") % 2
-    parts = x.reshape(2, 2, -1, x.shape[-1])
-    keep = lax.dynamic_index_in_dim(parts, core, 0, keepdims=False)
-    send = lax.dynamic_index_in_dim(parts, 1 - core, 0, keepdims=False)
-    half = keep + lax.ppermute(send, "mode", core_pairs)
-    qa, qb = half[0], half[1]
-    qa = qa + lax.ppermute(qa, "mode", near)
-    qb = qb + lax.ppermute(qb, "mode", far)
-    qa = qa + lax.ppermute(qa, "mode", far)
-    qb = qb + lax.ppermute(qb, "mode", near)
-    half = jnp.stack([qa, qb])
-    other = lax.ppermute(half, "mode", core_pairs)
-    first = jnp.where(core == 0, half, other)
-    second = jnp.where(core == 0, other, half)
-    return jnp.stack([first, second]).reshape(x.shape)
+    n = lax.axis_size("mode")
+    chunks = x.reshape(n, -1, x.shape[-1])
+    mine = jnp.sum(lax.all_to_all(chunks, "mode", 0, 0), axis=0)
+    spread = jnp.broadcast_to(mine[None], chunks.shape)
+    return lax.all_to_all(spread, "mode", 0, 0).reshape(x.shape)
 
 
 def reduce_scatter_mode(x):
@@ -267,16 +256,12 @@
         exits, waves, totals, measured, probe2, fr, fi, roff, coff, cnt, ext_rows, width
     )
 
-    core_pairs, near, far = mode_pairs()
-    core = my_mode % 2
-    blocks = numer.reshape(2, 3, 2, 2, 2, share_rows, width)
-    keep = lax.dynamic_index_in_dim(blocks, core, axis=4, keepdims=False)
-    send = lax.dynamic_index_in_dim(blocks, 1 - core, axis=4, keepdims=False)
-    blocks = keep + lax.ppermute(send, "mode", core_pairs)
-    band_rows = 2 * 4 * share_rows
+    blocks = numer.reshape(2, 3, mode_count, share_rows, width)
+    blocks = jnp.sum(lax.all_to_all(blocks, "mode", 2, 2), axis=2)
     own_illum = lax.dynamic_index_in_dim(
         illum.reshape(3, mode_count, share_rows, width), my_mode, axis=1, keepdims=False
     )
+    band_rows = 2 * share_rows
     to_next = jnp.concatenate([blocks[:, 2].reshape(band_rows, width), own_illum[2]], axis=0)
     to_prev = jnp.concatenate([blocks[:, 0].reshape(band_rows, width), own_illum[0]], axis=0)
     from_prev = lax.ppermute(to_next, "pos", neighbour_pairs(pos_count, 1))
@@ -287,11 +272,6 @@
         + from_next[:band_rows].reshape(blocks[:, 1].shape)
     )
     illum_rows = own_illum[1] + from_prev[band_rows:] + from_next[band_rows:]
-    for pairs, d in ((far, 4), (near, 2)):
-        bit = (my_mode // d) % 2
-        keep = lax.dynamic_index_in_dim(tile, bit, axis=1, keepdims=False)
-        send = lax.dynamic_index_in_dim(tile, 1 - bit, axis=1, keepdims=False)
-        tile = keep + lax.ppermute(send, "mode", pairs)
 
     start = my_mode * share_rows
     own_rows = lax.dynamic_slice_in_dim(object_field, start, share_rows, 1)

time: 116 us -> 120 us (1.034)
  the two profiles are of different devices: /device:TPU:120 before, /device:TPU:376 now
where the time goes in v4:
time: 120 us
  waiting for transfers between devices  39.7 us (33%)
  blocking collectives  39.6 us (33%)
  Pallas kernels  15.6 us (13%)
  starting transfers between devices  15.3 us (13%)
  local copies, waits for them, and re-layouts  4.45 us (4%)
  other arithmetic  4.26 us (4%)
    all_to_all x1, waiting for transfers between devices, local(): blocks = jnp.sum(lax.all_to_all(blocks, 'mode', 2, 2), axis=2)  20.7 us
    all_to_all x1, blocking collectives, allreduce_mode(): mine = jnp.sum(lax.all_to_all(chunks, 'mode', 0, 0), axis=0)  20.4 us
    all_to_all x1, blocking collectives, allreduce_mode(): return lax.all_to_all(spread, 'mode', 0, 0).reshape(x.shape)  19.2 us
    pallas_call x1, Pallas kernels, run_backward(): pl.pallas_call(backward_kernel, grid_spec=pltpu.PrefetchScalarGridSpec(nu...  8.52 us
    ppermute x1, waiting for transfers between devices, local(): before = lax.ppermute(object_field, 'pos', neighbour_pairs(pos_count, 1))  7.5 us
    pallas_call x1, Pallas kernels, run_forward(): pl.pallas_call(forward_kernel, grid_spec=pltpu.PrefetchScalarGridSpec(num...  7.09 us
    ppermute x1, waiting for transfers between devices, local(): after = lax.ppermute(object_field, 'pos', neighbour_pairs(pos_count, -1))  5.63 us
    ppermute x1, waiting for transfers between devices, local(): from_next = lax.ppermute(to_prev, 'pos', neighbour_pairs(pos_count, -1))  5.26 us
  transfers between devices with their start and end apart: 5, of which 5 were waited for; matrix products, arithmetic and copies ran while one was open for 2% of the time, Pallas kernels for 0%

profile of v4, /device:TPU:376, one launch (start us, length us, event | category | flops | bytes accessed | tf_op | source)
XLA Modules:
  0.0 119.7 jit_solution(17411547157272124252)
XLA Ops:
  0.0 2.6 %collective-permute-start = (f32[2,128,512]{2,1,0:T(8,128)}, f32[2,128,512]{2,1,0:T(8,128)S(1)}, u32[]{:S(2)}, u32[]{:S(2)}) collective-permute-start(f32[2,128,512]{2,1,0:T(8,128)} %own_ref.1), channel_id=1, source_target_pairs={{0,8},{8,16},{16,24},{24,32},{32,40},{40,48},{48,56},{56,64},{64,7... | collective-permute-start | bytes 1572872 | tf_op jit(solution)/shard_map/ppermute | solution.py:245
  2.6 3.3 %collective-permute-start.1 = (f32[2,128,512]{2,1,0:T(8,128)}, f32[2,128,512]{2,1,0:T(8,128)S(1)}, u32[]{:S(2)}, u32[]{:S(2)}) collective-permute-start(f32[2,128,512]{2,1,0:T(8,128)} %own_ref.1), channel_id=1, source_target_pairs={{8,0},{16,8},{24,16},{32,24},{40,32},{48,40},{56,48},{64,56},{72,6... | collective-permute-start | bytes 1572872 | tf_op jit(solution)/shard_map/ppermute | solution.py:246
  6.5 1.8 %multiply_convert_fusion = (bf16[256,256]{1,0:T(8,128)(2,1)}, bf16[256,256]{1,0:T(8,128)(2,1)}) fusion(), kind=kLoop, calls=%fused_computation.6 | loop fusion | flops 1245184 | bytes 262144 | tf_op jit(solution)/shard_map/convert_element_type | solution.py:18
  8.3 7.5 %collective-permute-done.before_ref = f32[2,128,512]{2,1,0:T(8,128)S(1)} collective-permute-done((f32[2,128,512]{2,1,0:T(8,128)}, f32[2,128,512]{2,1,0:T(8,128)S(1)}, u32[]{:S(2)}, u32[]{:S(2)}) %collective-permute-start) | collective-permute-done | bytes 524320 | tf_op jit(solution)/shard_map/ppermute | solution.py:245
  15.8 5.6 %collective-permute-done.1.after_ref = f32[2,128,512]{2,1,0:T(8,128)S(1)} collective-permute-done((f32[2,128,512]{2,1,0:T(8,128)}, f32[2,128,512]{2,1,0:T(8,128)S(1)}, u32[]{:S(2)}, u32[]{:S(2)}) %collective-permute-start.1) | collective-permute-done | bytes 524320 | tf_op jit(solution)/shard_map/ppermute | solution.py:246
  21.4 0.0 copy-done
  21.4 0.8 copy-done.1
  22.2 7.1 %shard_map.64 = (bf16[3,2,256,256]{3,2,1,0:T(8,128)(2,1)}, f32[3,2,256,256]{3,2,1,0:T(8,128)}, f32[4,256,256]{2,1,0:T(8,128)}) custom-call(s32[3]{0:T(128)} %roff.3, s32[3]{0:T(128)} %coff.3, s32[1]{0:T(128)S(6)} %copy.13.cnt, f32[2,128,512]{2,1,0:T(8,128)} %copy-done, f32[2,128,512]{2,1,0:T(8,128)} %own_ref.1, f32[2,128,512]{2,1,0:T(8,128)} %copy-done.1, ...), custom_call_target="tpu_custom_call" | custom-call | flops 805306368 | bytes 8388608 | tf_op jit(solution)/shard_map/pallas_call | solution.py:167
  29.3 20.4 %all_to_all.15 = f32[8,128,256]{2,1,0:T(8,128)S(1)} all-to-all(f32[8,128,256]{2,1,0:T(8,128)} %bitcast.30), channel_id=1, replica_groups=mesh['pos'=64,'mode'=8] {'mode'}, dimensions={0} | all-to-all | bytes 2097152 | tf_op jit(solution)/shard_map/all_to_all | solution.py:40
  49.7 0.1 reduce_sum.18
  49.8 0.1 broadcast_in_dim.2
  49.8 19.2 %all_to_all.16 = f32[8,128,256]{2,1,0:T(8,128)} all-to-all(f32[8,128,256]{2,1,0:T(8,128)S(1)} %broadcast_in_dim.2), channel_id=1, replica_groups=mesh['pos'=64,'mode'=8] {'mode'}, dimensions={0} | all-to-all | bytes 2097152 | tf_op jit(solution)/shard_map/all_to_all | solution.py:42
  69.1 8.5 %shard_map.65 = (f32[2,384,512]{2,1,0:T(8,128)}, f32[384,512]{1,0:T(8,128)}) custom-call(s32[3]{0:T(128)} %roff.3, s32[3]{0:T(128)} %coff.3, s32[1]{0:T(128)S(6)} %copy.13.cnt, bf16[3,2,256,256]{3,2,1,0:T(8,128)(2,1)} %get-tuple-element.10.exit_ref, f32[3,2,256,256]{3,2,1,0:T(8,128)} %get-tuple-element.11.wave_ref, f32[4,256,256]{2,1,0:T(8,128)} %bitcast.27, ...), custom_call_target="tpu_custom_call" | custom-call | flops 805306368 | bytes 12582912 | tf_op jit(solution)/shard_map/pallas_call | solution.py:205
  77.6 2.8 %copy.7 = f32[2,3,8,16,512]{4,3,1,0,2:T(8,128)} copy(f32[2,3,8,16,512]{4,3,2,1,0:T(8,128)} %bitcast.29) | data formatting | bytes 3145728 | tf_op jit(solution)/shard_map/reshape | solution.py:259
  80.3 3.6 %all-to-all-start.2 = ((f32[2,3,8,16,512]{4,3,1,0,2:T(8,128)}), f32[2,3,8,16,512]{4,3,1,0,2:T(8,128)S(1)}, u32[]{:S(2)}, u32[]{:S(2)}) async-start(f32[2,3,8,16,512]{4,3,1,0,2:T(8,128)} %copy.7), calls=%async_computation.2 | async-start | bytes 3145728 | tf_op jit(solution)/shard_map/all_to_all | solution.py:260
  83.9 0.8 dynamic-slice_bitcast_fusion.2
  84.7 20.7 %all-to-all-done.2 = f32[2,3,8,16,512]{4,3,1,0,2:T(8,128)S(1)} async-done(((f32[2,3,8,16,512]{4,3,1,0,2:T(8,128)}), f32[2,3,8,16,512]{4,3,1,0,2:T(8,128)S(1)}, u32[]{:S(2)}, u32[]{:S(2)}) %all-to-all-start.2) | async-done | bytes 1572896 | tf_op jit(solution)/shard_map/all_to_all | solution.py:260
  105.4 0.1 reduce_sum.19
  105.6 1.9 %collective-permute-start.2 = (f32[48,512]{1,0:T(8,128)S(1)}, f32[48,512]{1,0:T(8,128)S(1)}, u32[]{:S(2)}, u32[]{:S(2)}) collective-permute-start(f32[48,512]{1,0:T(8,128)S(1)} %pad_maximum_fusion), channel_id=1, source_target_pairs={{0,8},{8,16},{16,24},{24,32},{32,40},{40,48},{48,56},{56,64},{64,7... | collective-permute-start | bytes 294920 | tf_op jit(solution)/shard_map/ppermute | solution.py:267
  107.6 3.9 %collective-permute-start.3 = (f32[48,512]{1,0:T(8,128)S(1)}, f32[48,512]{1,0:T(8,128)S(1)}, u32[]{:S(2)}, u32[]{:S(2)}) collective-permute-start(f32[48,512]{1,0:T(8,128)S(1)} %pad_maximum_fusion.1), channel_id=1, source_target_pairs={{8,0},{16,8},{24,16},{32,24},{40,32},{48,40},{56,48},{64,56},{72,6... | collective-permute-start | bytes 294920 | tf_op jit(solution)/shard_map/ppermute | solution.py:268
  111.5 0.6 collective-permute-done.2
  112.1 5.3 %collective-permute-done.3 = f32[48,512]{1,0:T(8,128)S(1)} collective-permute-done((f32[48,512]{1,0:T(8,128)S(1)}, f32[48,512]{1,0:T(8,128)S(1)}, u32[]{:S(2)}, u32[]{:S(2)}) %collective-permute-start.3) | collective-permute-done | bytes 98336 | tf_op jit(solution)/shard_map/ppermute | solution.py:268
  117.4 0.8 fusion.10
  118.2 1.5 %fusion.9 = f32[2,16,512]{2,1,0:T(8,128)} fusion(f32[2,16,512]{2,1,0:T(8,128)S(1)} %bitcast.36, f32[2,16,512]{2,1,0:T(8,128)S(1)} %bitcast.35, f32[2,3,16,512]{3,2,1,0:T(8,128)S(1)} %reduce_sum.19, f32[2,128,512]{2,1,0:T(8,128)} %own_ref.1, s32[]{:T(128)S(6)} %select_n.20, f32[16,512]{1,0:T(8,128)S(1)} %fusion.10), kind=kLoop, calls=%fused_computation.17 | loop fusion | flops 65536 | bytes 360452 | tf_op jit(solution)/shard_map/add | solution.py:278
  (7 shorter events, 0.0 us)
Async XLA Ops:
  0.0 15.8 %collective-permute-start = (f32[2,128,512]{2,1,0:T(8,128)}, f32[2,128,512]{2,1,0:T(8,128)S(1)}, u32[]{:S(2)}, u32[]{:S(2)}) collective-permute-start(f32[2,128,512]{2,1,0:T(8,128)} %own_ref.1), channel_id=1, source_target_pairs={{0,8},{8,16},{16,24},{24,32},{32,40},{40,48},{48,56},{56,64},{64,7... | collective-permute-start | bytes 1572872 | tf_op jit(solution)/shard_map/ppermute | solution.py:245
  2.6 18.8 %collective-permute-start.1 = (f32[2,128,512]{2,1,0:T(8,128)}, f32[2,128,512]{2,1,0:T(8,128)S(1)}, u32[]{:S(2)}, u32[]{:S(2)}) collective-permute-start(f32[2,128,512]{2,1,0:T(8,128)} %own_ref.1), channel_id=1, source_target_pairs={{8,0},{16,8},{24,16},{32,24},{40,32},{48,40},{56,48},{64,56},{72,6... | collective-permute-start | bytes 1572872 | tf_op jit(solution)/shard_map/ppermute | solution.py:246
  15.8 5.6 %copy-start = (f32[2,128,512]{2,1,0:T(8,128)}, f32[2,128,512]{2,1,0:T(8,128)S(1)}, u32[]{:S(2)}) copy-start(f32[2,128,512]{2,1,0:T(8,128)S(1)} %collective-permute-done.before_ref) | copy-start | bytes 1572868
  21.4 0.8 copy-start.1
  80.3 25.1 %all-to-all-start.2 = ((f32[2,3,8,16,512]{4,3,1,0,2:T(8,128)}), f32[2,3,8,16,512]{4,3,1,0,2:T(8,128)S(1)}, u32[]{:S(2)}, u32[]{:S(2)}) async-start(f32[2,3,8,16,512]{4,3,1,0,2:T(8,128)} %copy.7), calls=%async_computation.2 | async-start | bytes 3145728 | tf_op jit(solution)/shard_map/all_to_all | solution.py:260
  105.6 6.5 %collective-permute-start.2 = (f32[48,512]{1,0:T(8,128)S(1)}, f32[48,512]{1,0:T(8,128)S(1)}, u32[]{:S(2)}, u32[]{:S(2)}) collective-permute-start(f32[48,512]{1,0:T(8,128)S(1)} %pad_maximum_fusion), channel_id=1, source_target_pairs={{0,8},{8,16},{16,24},{24,32},{32,40},{40,48},{48,56},{56,64},{64,7... | collective-permute-start | bytes 294920 | tf_op jit(solution)/shard_map/ppermute | solution.py:267
  107.6 9.8 %collective-permute-start.3 = (f32[48,512]{1,0:T(8,128)S(1)}, f32[48,512]{1,0:T(8,128)S(1)}, u32[]{:S(2)}, u32[]{:S(2)}) collective-permute-start(f32[48,512]{1,0:T(8,128)S(1)} %pad_maximum_fusion.1), channel_id=1, source_target_pairs={{8,0},{16,8},{24,16},{32,24},{40,32},{48,40},{56,48},{64,56},{72,6... | collective-permute-start | bytes 294920 | tf_op jit(solution)/shard_map/ppermute | solution.py:268

commit v5 on v3

v5 whole, which is shorter than its diff:
```python
import math

import jax
import jax.numpy as jnp
from jax import lax
from jax.experimental import pallas as pl
from jax.experimental.pallas import tpu as pltpu
from jax.sharding import PartitionSpec as P


def dft_tables(pattern):
    counter = jnp.arange(pattern, dtype=jnp.int32)
    phases = counter[:, None] * counter[None, :] % pattern
    angles = phases.astype(jnp.float32) * (2.0 * math.pi / pattern)
    factor = 1.0 / math.sqrt(pattern)
    return (
        (jnp.cos(angles) * factor).astype(jnp.bfloat16),
        (-jnp.sin(angles) * factor).astype(jnp.bfloat16),
    )


def neighbour_pairs(size, step):
    if step > 0:
        return [(i, i + 1) for i in range(size - 1)]
    return [(i + 1, i) for i in range(size - 1)]


def mode_pairs():
    n = lax.axis_size("mode")
    chips = n // 2
    core = [(i, i ^ 1) for i in range(n)]
    near = [(i, i ^ 2) for i in range(n)]
    far = [(i, 2 * (chips - 1 - i // 2) + i % 2) for i in range(n)]
    return core, near, far


def allreduce_chips(x):
    _, near, far = mode_pairs()
    qa, qb = x[0], x[1]
    qa = qa + lax.ppermute(qa, "mode", near)
    qb = qb + lax.ppermute(qb, "mode", far)
    qa = qa + lax.ppermute(qa, "mode", far)
    qb = qb + lax.ppermute(qb, "mode", near)
    return jnp.stack([qa, qb])


def reduce_scatter_mode(x):
    core_pairs, near, far = mode_pairs()
    n = lax.axis_size("mode")
    m = lax.axis_index("mode")
    c, rows, w = x.shape
    x = x.reshape(c, 2, 2, 2, rows // n, w)
    for pairs, dim, d in ((core_pairs, 3, 1), (far, 1, 4), (near, 1, 2)):
        bit = (m // d) % 2
        keep = lax.dynamic_index_in_dim(x, bit, axis=dim, keepdims=False)
        send = lax.dynamic_index_in_dim(x, 1 - bit, axis=dim, keepdims=False)
        x = keep + lax.ppermute(send, "mode", pairs)
    return x.reshape(c, rows // n, w)


def _dot(a, b):
    return jnp.dot(a, b, preferred_element_type=jnp.float32)


def _window(ext_ref, k, r, c, pat):
    width = ext_ref.shape[2]
    base = pl.multiple_of((r // 8) * 8, 8)
    span = pat + 8
    down = (span - (r - base)) % span
    rows = pltpu.roll(ext_ref[k, pl.ds(base, span), :], down, 0)[:pat]
    return pltpu.roll(rows, (width - c) % width, 1)[:, :pat]


def _place(ref, a, r, c):
    pat = a.shape[0]
    width = ref.shape[-1]
    base = pl.multiple_of((r // 8) * 8, 8)
    span = pat + 8
    wide = pltpu.roll(jnp.concatenate([a, jnp.zeros((pat, width - pat), jnp.float32)], axis=1), c, 1)
    tall = jnp.concatenate([wide, jnp.zeros((span - pat, width), jnp.float32)], axis=0)
    ref[pl.ds(base, span), :] += pltpu.roll(tall, r - base, 0)


def forward_kernel(roff, coff, cnt, core, before_ref, own_ref, after_ref, pa_ref, pb_ref, fr_ref, fi_ref,
                   exit_ref, wave_ref, power_ref, ext_ref):
    i = pl.program_id(0)
    slots = roff.shape[0]
    pat = pa_ref.shape[1]
    band = own_ref.shape[1]
    g = core[0] + 2 * i
    gi = jnp.minimum(g, slots - 1)
    live = g < cnt[0]

    @pl.when(i == 0)
    def _():
        ext_ref[:, :band, :] = before_ref[...]
        ext_ref[:, band : 2 * band, :] = own_ref[...]
        ext_ref[:, 2 * band :, :] = after_ref[...]

    @pl.when(live)
    def _():
        r = roff[gi]
        c = coff[gi]
        obj_re = _window(ext_ref, 0, r, c, pat)
        obj_im = _window(ext_ref, 1, r, c, pat)
        fr = fr_ref[...]
        fi = fi_ref[...]
        total = None
        for k, p_ref in enumerate((pa_ref, pb_ref)):
            p_re = p_ref[0]
            p_im = p_ref[1]
            e_re = (p_re * obj_re - p_im * obj_im).astype(jnp.bfloat16)
            e_im = (p_re * obj_im + p_im * obj_re).astype(jnp.bfloat16)
            h_re = (_dot(fr, e_re) - _dot(fi, e_im)).astype(jnp.bfloat16)
            h_im = (_dot(fr, e_im) + _dot(fi, e_re)).astype(jnp.bfloat16)
            v_re = _dot(h_re, fr) - _dot(h_im, fi)
            v_im = _dot(h_re, fi) + _dot(h_im, fr)
            exit_ref[0, k, 0] = e_re
            exit_ref[0, k, 1] = e_im
            wave_ref[0, k, 0] = v_re
            wave_ref[0, k, 1] = v_im
            part = v_re * v_re + v_im * v_im
            total = part if total is None else total + part
        power_ref[i] = total

    @pl.when(g == slots)
    def _():
        total = None
        for p_ref in (pa_ref, pb_ref):
            p_re = p_ref[0]
            p_im = p_ref[1]
            part = p_re * p_re + p_im * p_im
            total = part if total is None else total + part
        power_ref[i] = total

    @pl.when(jnp.logical_and(jnp.logical_not(live), g != slots))
    def _():
        power_ref[i] = jnp.zeros((pat, pat), jnp.float32)


def backward_kernel(roff, coff, cnt, core, exit_ref, wave_ref, model_ref, meas_ref, pa_ref, pb_ref,
                    ppt_ref, fr_ref, fi_ref, numer_ref, illum_ref):
    i = pl.program_id(0)
    slots = roff.shape[0]
    g = core[0] + 2 * i
    gi = jnp.minimum(g, slots - 1)

    @pl.when(i == 0)
    def _():
        numer_ref[...] = jnp.zeros(numer_ref.shape, jnp.float32)
        illum_ref[...] = jnp.zeros(illum_ref.shape, jnp.float32)

    @pl.when(g < cnt[0])
    def _():
        r = roff[gi]
        c = coff[gi]
        scaling = jnp.sqrt(meas_ref[0]) / jnp.maximum(jnp.sqrt(model_ref[0]), 1.0)
        fr = fr_ref[...]
        fi = fi_ref[...]
        n_re = None
        n_im = None
        for k, p_ref in enumerate((pa_ref, pb_ref)):
            x_re = (scaling * wave_ref[0, k, 0]).astype(jnp.bfloat16)
            x_im = (scaling * wave_ref[0, k, 1]).astype(jnp.bfloat16)
            b_re = (_dot(fr, x_re) + _dot(fi, x_im)).astype(jnp.bfloat16)
            b_im = (_dot(fr, x_im) - _dot(fi, x_re)).astype(jnp.bfloat16)
            d_re = _dot(b_re, fr) + _dot(b_im, fi) - exit_ref[0, k, 0].astype(jnp.float32)
            d_im = _dot(b_im, fr) - _dot(b_re, fi) - exit_ref[0, k, 1].astype(jnp.float32)
            p_re = p_ref[0]
            p_im = p_ref[1]
            t_re = p_re * d_re + p_im * d_im
            t_im = p_re * d_im - p_im * d_re
            n_re = t_re if n_re is None else n_re + t_re
            n_im = t_im if n_im is None else n_im + t_im
        _place(numer_ref.at[0], n_re, r, c)
        _place(numer_ref.at[1], n_im, r, c)

    @pl.when(jnp.logical_and(core[0] == 1, i == pl.num_programs(0) - 1))
    def _():
        for slot in range(slots):
            @pl.when(slot < cnt[0])
            def _():
                _place(illum_ref, ppt_ref[0], roff[slot], coff[slot])


def run_forward(before, own, after, pa, pb, fr, fi, roff, coff, cnt, core):
    slots = roff.shape[0]
    local = (slots + 1) // 2
    pat = pa.shape[1]
    whole3 = lambda i, *_: (0, 0, 0)
    whole2 = lambda i, *_: (0, 0)
    per5 = lambda i, *_: (i, 0, 0, 0, 0)
    flops = local * 2 * 8 * 2 * pat ** 3
    ext_shape = (2, 3 * own.shape[1], own.shape[2])
    return pl.pallas_call(
        forward_kernel,
        grid_spec=pltpu.PrefetchScalarGridSpec(
            num_scalar_prefetch=4,
            grid=(local,),
            in_specs=[
                pl.BlockSpec(before.shape, whole3),
                pl.BlockSpec(own.shape, whole3),
                pl.BlockSpec(after.shape, whole3),
                pl.BlockSpec(pa.shape, whole3),
                pl.BlockSpec(pb.shape, whole3),
                pl.BlockSpec(fr.shape, whole2),
                pl.BlockSpec(fi.shape, whole2),
            ],
            out_specs=[
                pl.BlockSpec((1, 2, 2, pat, pat), per5),
                pl.BlockSpec((1, 2, 2, pat, pat), per5),
                pl.BlockSpec((local, pat, pat), whole3),
            ],
            scratch_shapes=[pltpu.VMEM(ext_shape, jnp.float32)],
        ),
        out_shape=[
            jax.ShapeDtypeStruct((local, 2, 2, pat, pat), jnp.bfloat16),
            jax.ShapeDtypeStruct((local, 2, 2, pat, pat), jnp.float32),
            jax.ShapeDtypeStruct((local, pat, pat), jnp.float32),
        ],
        compiler_params=pltpu.CompilerParams(dimension_semantics=("arbitrary",)),
        cost_estimate=pl.CostEstimate(flops=flops, transcendentals=0, bytes_accessed=10 * 1024 * 1024),
    )(roff, coff, cnt, core, before, own, after, pa, pb, fr, fi)


def run_backward(exits, waves, totals, measured, pa, pb, fr, fi, roff, coff, cnt, core, ext_rows, width):
    slots = roff.shape[0]
    local = (slots + 1) // 2
    pat = pa.shape[1]
    whole3 = lambda i, *_: (0, 0, 0)
    whole2 = lambda i, *_: (0, 0)
    per5 = lambda i, *_: (i, 0, 0, 0, 0)
    per3 = lambda i, *_: (i, 0, 0)
    slot_of = lambda i, roff, coff, cnt, core: (jnp.minimum(core[0] + 2 * i, slots - 1), 0, 0)
    flops = local * 2 * 8 * 2 * pat ** 3
    return pl.pallas_call(
        backward_kernel,
        grid_spec=pltpu.PrefetchScalarGridSpec(
            num_scalar_prefetch=4,
            grid=(local,),
            in_specs=[
                pl.BlockSpec((1, 2, 2, pat, pat), per5),
                pl.BlockSpec((1, 2, 2, pat, pat), per5),
                pl.BlockSpec((1, pat, pat), per3),
                pl.BlockSpec((1, pat, pat), slot_of),
                pl.BlockSpec(pa.shape, whole3),
                pl.BlockSpec(pb.shape, whole3),
                pl.BlockSpec((1, pat, pat), lambda i, *_: (local - 1, 0, 0)),
                pl.BlockSpec(fr.shape, whole2),
                pl.BlockSpec(fi.shape, whole2),
            ],
            out_specs=[
                pl.BlockSpec((2, ext_rows, width), whole3),
                pl.BlockSpec((ext_rows, width), whole2),
            ],
        ),
        out_shape=[
            jax.ShapeDtypeStruct((2, ext_rows, width), jnp.float32),
            jax.ShapeDtypeStruct((ext_rows, width), jnp.float32),
        ],
        compiler_params=pltpu.CompilerParams(dimension_semantics=("arbitrary",)),
        cost_estimate=pl.CostEstimate(flops=flops, transcendentals=0, bytes_accessed=14 * 1024 * 1024),
    )(roff, coff, cnt, core, exits, waves, totals, measured, pa, pb, totals, fr, fi)


def local(object_field, probe, measured, row_offsets, col_offsets, tile_counts):
    rows_tile = object_field.shape[1]
    width = object_field.shape[2]
    pos_count = lax.axis_size("pos")
    mode_count = lax.axis_size("mode")
    my_mode = lax.axis_index("mode")
    share_rows = rows_tile // mode_count
    pattern = probe.shape[2]
    fr, fi = dft_tables(pattern)
    probe2 = probe[:, 0]

    core_pairs, near, far = mode_pairs()
    core = my_mode % 2
    before = lax.ppermute(object_field, "pos", neighbour_pairs(pos_count, 1))
    after = lax.ppermute(object_field, "pos", neighbour_pairs(pos_count, -1))
    partner_probe = lax.ppermute(probe2, "mode", core_pairs)
    ext_rows = 3 * rows_tile

    roff = row_offsets.astype(jnp.int32)
    coff = col_offsets.astype(jnp.int32)
    cnt = tile_counts.astype(jnp.int32)
    core_arr = jnp.reshape(core, (1,)).astype(jnp.int32)

    exits, waves, power = run_forward(
        before, object_field, after, probe2, partner_probe, fr, fi, roff, coff, cnt, core_arr
    )
    totals = allreduce_chips(power)
    numer, illum = run_backward(
        exits, waves, totals, measured, probe2, partner_probe, fr, fi, roff, coff, cnt, core_arr,
        ext_rows, width
    )

    blocks = numer.reshape(2, 3, 2, 2, 2, share_rows, width)
    keep = lax.dynamic_index_in_dim(blocks, core, axis=4, keepdims=False)
    send = lax.dynamic_index_in_dim(blocks, 1 - core, axis=4, keepdims=False)
    illum_blocks = illum.reshape(3, mode_count, share_rows, width)
    partner = my_mode + 1 - 2 * core
    illum_partner = lax.dynamic_index_in_dim(illum_blocks, partner, axis=1, keepdims=False)
    numer_rows = send.size // width
    message = jnp.concatenate(
        [send.reshape(numer_rows, width), illum_partner.reshape(-1, width)], axis=0
    )
    got = lax.ppermute(message, "mode", core_pairs)
    blocks = keep + got[:numer_rows].reshape(keep.shape)
    own_illum = lax.dynamic_index_in_dim(illum_blocks, my_mode, axis=1, keepdims=False)
    own_illum = own_illum + got[numer_rows:].reshape(own_illum.shape)
    band_rows = 2 * 4 * share_rows
    to_next = jnp.concatenate([blocks[:, 2].reshape(band_rows, width), own_illum[2]], axis=0)
    to_prev = jnp.concatenate([blocks[:, 0].reshape(band_rows, width), own_illum[0]], axis=0)
    from_prev = lax.ppermute(to_next, "pos", neighbour_pairs(pos_count, 1))
    from_next = lax.ppermute(to_prev, "pos", neighbour_pairs(pos_count, -1))
    tile = (
        blocks[:, 1]
        + from_prev[:band_rows].reshape(blocks[:, 1].shape)
        + from_next[:band_rows].reshape(blocks[:, 1].shape)
    )
    illum_rows = own_illum[1] + from_prev[band_rows:] + from_next[band_rows:]
    for pairs, d in ((far, 4), (near, 2)):
        bit = (my_mode // d) % 2
        keep = lax.dynamic_index_in_dim(tile, bit, axis=1, keepdims=False)
        send = lax.dynamic_index_in_dim(tile, 1 - bit, axis=1, keepdims=False)
        tile = keep + lax.ppermute(send, "mode", pairs)

    start = my_mode * share_rows
    own_rows = lax.dynamic_slice_in_dim(object_field, start, share_rows, 1)
    return own_rows + tile / (illum_rows + 1.0)


def solution(mesh):
    in_specs = (
        P(None, "pos", None),
        P(None, "mode", None, None),
        P("pos", None, None),
        P("pos"),
        P("pos"),
        P("pos"),
    )
    out_specs = P(None, ("pos", "mode"), None)
    return jax.shard_map(local, mesh=mesh, in_specs=in_specs, out_specs=out_specs, check_vma=False)
```

time: 116 us -> 110 us (0.948)
  waiting for transfers between devices: 53.9 us -> 49.9 us
  starting transfers between devices: 36.6 us -> 34.6 us
    ppermute x7 -> x6, waiting for transfers between devices: 19.1 us -> 15.3 us  [the longest x1 4.33 us: allreduce_chips(): qb = qb + lax.ppermute(qb, 'mode', far)]
    dynamic_slice x0 -> x2, local copies, waits for them, and re-layouts: none -> 2.1 us  [the longest x1 1.19 us: local(): send = lax.dynamic_index_in_dim(blocks, 1 - core, axis=4, keepdims=False)]
    ppermute x7 -> x6, starting transfers between devices: 19.2 us -> 17.2 us  [the longest x1 4.01 us: allreduce_chips(): qb = qb + lax.ppermute(qb, 'mode', far)]
    ppermute x1, starting transfers between devices: 1.93 us -> 3.92 us  [local(): from_next = lax.ppermute(to_prev, 'pos', neighbour_pairs(pos_count, -1))]
    ppermute x1, starting transfers between devices: 3.91 us -> 1.92 us  [local(): from_prev = lax.ppermute(to_next, 'pos', neighbour_pairs(pos_count, 1))]
    ppermute x1, waiting for transfers between devices: 6.97 us -> 5.26 us  [local(): from_next = lax.ppermute(to_prev, 'pos', neighbour_pairs(pos_count, -1))]
    squeeze x3 -> x1, local copies, waits for them, and re-layouts: 2.43 us -> 1.07 us  [allreduce_chips(): qa, qb = (x[0], x[1])]
  transfers between devices with their start and end apart: 13 -> 12, of which waited for: 13 -> 11; matrix products, arithmetic and copies ran while one was open for 3% -> 2% of each run, Pallas kernels for 0% -> 0%
where the time goes in v5:
time: 110 us; the launch traced here: 109 us
  waiting for transfers between devices  49.9 us (45%)
  starting transfers between devices  34.6 us (31%)
  Pallas kernels  12.2 us (11%)
  other arithmetic  7.45 us (7%)
  local copies, waits for them, and re-layouts  4.13 us (4%)
    ppermute x2, waiting for transfers between devices, local(): tile = keep + lax.ppermute(send, 'mode', pairs)  9.19 us
    ppermute x1, waiting for transfers between devices, local(): before = lax.ppermute(object_field, 'pos', neighbour_pairs(pos_count, 1))  7.79 us
    ppermute x1, waiting for transfers between devices, local(): after = lax.ppermute(object_field, 'pos', neighbour_pairs(pos_count, -1))  7.33 us
    pallas_call x1, Pallas kernels, run_backward(): pl.pallas_call(backward_kernel, grid_spec=pltpu.PrefetchScalarGridSpec(nu...  6.29 us
    pallas_call x1, Pallas kernels, run_forward(): pl.pallas_call(forward_kernel, grid_spec=pltpu.PrefetchScalarGridSpec(num...  5.89 us
    ppermute x1, waiting for transfers between devices, local(): from_next = lax.ppermute(to_prev, 'pos', neighbour_pairs(pos_count, -1))  5.26 us
    ppermute x1, waiting for transfers between devices, local(): from_prev = lax.ppermute(to_next, 'pos', neighbour_pairs(pos_count, 1))  5.02 us
    ppermute x2, starting transfers between devices, local(): tile = keep + lax.ppermute(send, 'mode', pairs)  4.97 us
  transfers between devices with their start and end apart: 12, of which 11 were waited for; matrix products, arithmetic and copies ran while one was open for 2% of the time, Pallas kernels for 0%

profile of v5, /device:TPU:120, one launch (start us, length us, event | category | flops | bytes accessed | tf_op | source)
XLA Modules:
  0.0 109.2 jit_solution(9721092001178181071)
XLA Ops:
  0.0 1.9 %collective-permute-start.2 = (f32[2,256,256]{2,1,0:T(8,128)}, f32[2,256,256]{2,1,0:T(8,128)S(1)}, u32[]{:S(2)}, u32[]{:S(2)}) collective-permute-start(f32[2,256,256]{2,1,0:T(8,128)} %bitcast.64), channel_id=1, source_target_pairs={{0,1},{1,0},{2,3},{3,2},{4,5},{5,4},{6,7},{7,6},{8,9},{9,8},{10,11... | collective-permute-start | bytes 1572872 | tf_op jit(solution)/shard_map/ppermute | solution.py:281
  1.9 4.7 %collective-permute-start = (f32[2,128,512]{2,1,0:T(8,128)}, f32[2,128,512]{2,1,0:T(8,128)S(1)}, u32[]{:S(2)}, u32[]{:S(2)}) collective-permute-start(f32[2,128,512]{2,1,0:T(8,128)} %own_ref.1), channel_id=1, source_target_pairs={{0,8},{8,16},{16,24},{24,32},{32,40},{40,48},{48,56},{56,64},{64,7... | collective-permute-start | bytes 1572872 | tf_op jit(solution)/shard_map/ppermute | solution.py:279
  6.6 1.9 %collective-permute-start.1 = (f32[2,128,512]{2,1,0:T(8,128)}, f32[2,128,512]{2,1,0:T(8,128)S(1)}, u32[]{:S(2)}, u32[]{:S(2)}) collective-permute-start(f32[2,128,512]{2,1,0:T(8,128)} %own_ref.1), channel_id=1, source_target_pairs={{8,0},{16,8},{24,16},{32,24},{40,32},{48,40},{56,48},{64,56},{72,6... | collective-permute-start | bytes 1572872 | tf_op jit(solution)/shard_map/ppermute | solution.py:280
  11.0 7.8 %collective-permute-done.before_ref = f32[2,128,512]{2,1,0:T(8,128)S(1)} collective-permute-done((f32[2,128,512]{2,1,0:T(8,128)}, f32[2,128,512]{2,1,0:T(8,128)S(1)}, u32[]{:S(2)}, u32[]{:S(2)}) %collective-permute-start) | collective-permute-done | bytes 524320 | tf_op jit(solution)/shard_map/ppermute | solution.py:279
  18.8 7.3 %collective-permute-done.1.after_ref = f32[2,128,512]{2,1,0:T(8,128)S(1)} collective-permute-done((f32[2,128,512]{2,1,0:T(8,128)}, f32[2,128,512]{2,1,0:T(8,128)S(1)}, u32[]{:S(2)}, u32[]{:S(2)}) %collective-permute-start.1) | collective-permute-done | bytes 524320 | tf_op jit(solution)/shard_map/ppermute | solution.py:280
  26.9 5.9 %shard_map.64 = (bf16[2,2,2,256,256]{4,3,2,1,0:T(8,128)(2,1)}, f32[2,2,2,256,256]{4,3,2,1,0:T(8,128)}, f32[2,256,256]{2,1,0:T(8,128)}) custom-call(s32[3]{0:T(128)} %roff.3, s32[3]{0:T(128)} %coff.3, s32[1]{0:T(128)S(6)} %copy.12.cnt, s32[1]{0:T(128)} %bitcast.core, f32[2,128,512]{2,1,0:T(8,128)} %copy-done.2, f32[2,128,512]{2,1,0:T(8,128)} %own_ref.1, ...), custom_call_target="tpu_custom_call" | custom-call | flops 1073741824 | bytes 10485760 | tf_op jit(solution)/shard_map/pallas_call | solution.py:195
  33.9 3.4 %collective-permute-start.3 = (f32[256,256]{1,0:T(8,128)S(1)}, f32[256,256]{1,0:T(8,128)S(1)}, u32[]{:S(2)}, u32[]{:S(2)}) collective-permute-start(f32[256,256]{1,0:T(8,128)S(1)} %get-tuple-element.19), channel_id=1, source_target_pairs={{0,2},{1,3},{2,0},{3,1},{4,6},{5,7},{6,4},{7,5},{8,10},{9,11},{10,... | collective-permute-start | bytes 786440 | tf_op jit(solution)/shard_map/ppermute | solution.py:40
  37.3 4.0 %collective-permute-start.5 = (f32[256,256]{1,0:T(8,128)S(1)}, f32[256,256]{1,0:T(8,128)S(1)}, u32[]{:S(2)}, u32[]{:S(2)}) collective-permute-start(f32[256,256]{1,0:T(8,128)S(1)} %get-tuple-element.20), channel_id=1, source_target_pairs={{0,6},{1,7},{2,4},{3,5},{4,2},{5,3},{6,0},{7,1},{8,14},{9,15},{10,... | collective-permute-start | bytes 786440 | tf_op jit(solution)/shard_map/ppermute | solution.py:41
  41.3 2.1 %collective-permute-done.3 = f32[256,256]{1,0:T(8,128)S(1)} collective-permute-done((f32[256,256]{1,0:T(8,128)S(1)}, f32[256,256]{1,0:T(8,128)S(1)}, u32[]{:S(2)}, u32[]{:S(2)}) %collective-permute-start.3) | collective-permute-done | bytes 262176 | tf_op jit(solution)/shard_map/ppermute | solution.py:40
  43.4 4.3 %collective-permute-done.5 = f32[256,256]{1,0:T(8,128)S(1)} collective-permute-done((f32[256,256]{1,0:T(8,128)S(1)}, f32[256,256]{1,0:T(8,128)S(1)}, u32[]{:S(2)}, u32[]{:S(2)}) %collective-permute-start.5) | collective-permute-done | bytes 262176 | tf_op jit(solution)/shard_map/ppermute | solution.py:41
  48.8 4.0 %collective-permute-start.4 = (f32[256,256]{1,0:T(8,128)S(1)}, f32[256,256]{1,0:T(8,128)S(1)}, u32[]{:S(2)}, u32[]{:S(2)}) collective-permute-start(f32[256,256]{1,0:T(8,128)S(1)} %get-tuple-element.17), channel_id=1, source_target_pairs={{0,6},{1,7},{2,4},{3,5},{4,2},{5,3},{6,0},{7,1},{8,14},{9,15},{10,... | collective-permute-start | bytes 786440 | tf_op jit(solution)/shard_map/ppermute | solution.py:42
  52.8 1.9 %collective-permute-start.6 = (f32[256,256]{1,0:T(8,128)S(1)}, f32[256,256]{1,0:T(8,128)S(1)}, u32[]{:S(2)}, u32[]{:S(2)}) collective-permute-start(f32[256,256]{1,0:T(8,128)S(1)} %get-tuple-element.18), channel_id=1, source_target_pairs={{0,2},{1,3},{2,0},{3,1},{4,6},{5,7},{6,4},{7,5},{8,10},{9,11},{10,... | collective-permute-start | bytes 786440 | tf_op jit(solution)/shard_map/ppermute | solution.py:43
  54.7 3.6 %collective-permute-done.4 = f32[256,256]{1,0:T(8,128)S(1)} collective-permute-done((f32[256,256]{1,0:T(8,128)S(1)}, f32[256,256]{1,0:T(8,128)S(1)}, u32[]{:S(2)}, u32[]{:S(2)}) %collective-permute-start.4) | collective-permute-done | bytes 262176 | tf_op jit(solution)/shard_map/ppermute | solution.py:42
  58.3 2.7 %collective-permute-done.6 = f32[256,256]{1,0:T(8,128)S(1)} collective-permute-done((f32[256,256]{1,0:T(8,128)S(1)}, f32[256,256]{1,0:T(8,128)S(1)}, u32[]{:S(2)}, u32[]{:S(2)}) %collective-permute-start.6) | collective-permute-done | bytes 262176 | tf_op jit(solution)/shard_map/ppermute | solution.py:43
  62.0 6.3 %shard_map.65 = (f32[2,384,512]{2,1,0:T(8,128)}, f32[384,512]{1,0:T(8,128)}) custom-call(s32[3]{0:T(128)} %roff.3, s32[3]{0:T(128)} %coff.3, s32[1]{0:T(128)S(6)} %copy.12.cnt, s32[1]{0:T(128)} %bitcast.core, bf16[2,2,2,256,256]{4,3,2,1,0:T(8,128)(2,1)} %get-tuple-element.10.exit_ref, f32[2,2,2,256,256]{4,3,2,1,0:T(8,128)} %get-tuple-element.11.wave_ref, ...), custom_call_target="tpu_custom_call" | custom-call | flops 1073741824 | bytes 14680064 | tf_op jit(solution)/shard_map/pallas_call | solution.py:236
  73.3 2.6 %collective-permute-done.7 = f32[432,512]{1,0:T(8,128)S(1)} collective-permute-done((f32[432,512]{1,0:T(8,128)}, f32[432,512]{1,0:T(8,128)S(1)}, u32[]{:S(2)}, u32[]{:S(2)}) %collective-permute-start.7) | collective-permute-done | bytes 884768 | tf_op jit(solution)/shard_map/ppermute | solution.py:308
  77.1 1.9 %collective-permute-start.8 = (f32[144,512]{1,0:T(8,128)S(1)}, f32[144,512]{1,0:T(8,128)S(1)}, u32[]{:S(2)}, u32[]{:S(2)}) collective-permute-start(f32[144,512]{1,0:T(8,128)S(1)} %pad_maximum_fusion.2), channel_id=1, source_target_pairs={{0,8},{8,16},{16,24},{24,32},{32,40},{40,48},{48,56},{56,64},{64,7... | collective-permute-start | bytes 884744 | tf_op jit(solution)/shard_map/ppermute | solution.py:315
  79.1 3.9 %collective-permute-start.9 = (f32[144,512]{1,0:T(8,128)S(1)}, f32[144,512]{1,0:T(8,128)S(1)}, u32[]{:S(2)}, u32[]{:S(2)}) collective-permute-start(f32[144,512]{1,0:T(8,128)S(1)} %pad_maximum_fusion.3), channel_id=1, source_target_pairs={{8,0},{16,8},{24,16},{32,24},{40,32},{48,40},{56,48},{64,56},{72,6... | collective-permute-start | bytes 884744 | tf_op jit(solution)/shard_map/ppermute | solution.py:316
  83.0 5.0 %collective-permute-done.8 = f32[144,512]{1,0:T(8,128)S(1)} collective-permute-done((f32[144,512]{1,0:T(8,128)S(1)}, f32[144,512]{1,0:T(8,128)S(1)}, u32[]{:S(2)}, u32[]{:S(2)}) %collective-permute-start.8) | collective-permute-done | bytes 294944 | tf_op jit(solution)/shard_map/ppermute | solution.py:315
  88.1 5.3 %collective-permute-done.9 = f32[144,512]{1,0:T(8,128)S(1)} collective-permute-done((f32[144,512]{1,0:T(8,128)S(1)}, f32[144,512]{1,0:T(8,128)S(1)}, u32[]{:S(2)}, u32[]{:S(2)}) %collective-permute-start.9) | collective-permute-done | bytes 294944 | tf_op jit(solution)/shard_map/ppermute | solution.py:316
  93.5 3.0 %collective-permute-start.10 = (f32[2,2,16,512]{3,2,1,0:T(8,128)S(1)}, f32[2,2,16,512]{3,2,1,0:T(8,128)S(1)}, u32[]{:S(2)}, u32[]{:S(2)}) collective-permute-start(f32[2,2,16,512]{3,2,1,0:T(8,128)S(1)} %dynamic-slice_bitcast_fusion), channel_id=1, source_target_pairs={{0,6},{1,7},{2,4},{3,5},{4,2},{5,3},{6,0},{7,1},{8,14},{9,15},{10,... | collective-permute-start | bytes 393224 | tf_op jit(solution)/shard_map/ppermute | solution.py:327
  96.6 5.0 %collective-permute-done.10 = f32[2,2,16,512]{3,2,1,0:T(8,128)S(1)} collective-permute-done((f32[2,2,16,512]{3,2,1,0:T(8,128)S(1)}, f32[2,2,16,512]{3,2,1,0:T(8,128)S(1)}, u32[]{:S(2)}, u32[]{:S(2)}) %collective-permute-start.10) | collective-permute-done | bytes 131104 | tf_op jit(solution)/shard_map/ppermute | solution.py:327
  101.6 1.9 %collective-permute-start.11 = (f32[2,16,512]{2,1,0:T(8,128)S(1)}, f32[2,16,512]{2,1,0:T(8,128)S(1)}, u32[]{:S(2)}, u32[]{:S(2)}) collective-permute-start(f32[2,16,512]{2,1,0:T(8,128)S(1)} %dynamic-slice_bitcast_fusion.1), channel_id=1, source_target_pairs={{0,2},{1,3},{2,0},{3,1},{4,6},{5,7},{6,4},{7,5},{8,10},{9,11},{10,... | collective-permute-start | bytes 196616 | tf_op jit(solution)/shard_map/ppermute | solution.py:327
  103.5 4.2 %collective-permute-done.11 = f32[2,16,512]{2,1,0:T(8,128)S(1)} collective-permute-done((f32[2,16,512]{2,1,0:T(8,128)S(1)}, f32[2,16,512]{2,1,0:T(8,128)S(1)}, u32[]{:S(2)}, u32[]{:S(2)}) %collective-permute-start.11) | collective-permute-done | bytes 65568 | tf_op jit(solution)/shard_map/ppermute | solution.py:327
  (35 shorter events, 13.5 us)
Async XLA Ops:
  0.0 11.0 %collective-permute-start.2 = (f32[2,256,256]{2,1,0:T(8,128)}, f32[2,256,256]{2,1,0:T(8,128)S(1)}, u32[]{:S(2)}, u32[]{:S(2)}) collective-permute-start(f32[2,256,256]{2,1,0:T(8,128)} %bitcast.64), channel_id=1, source_target_pairs={{0,1},{1,0},{2,3},{3,2},{4,5},{5,4},{6,7},{7,6},{8,9},{9,8},{10,11... | collective-permute-start | bytes 1572872 | tf_op jit(solution)/shard_map/ppermute | solution.py:281
  1.9 16.8 %collective-permute-start = (f32[2,128,512]{2,1,0:T(8,128)}, f32[2,128,512]{2,1,0:T(8,128)S(1)}, u32[]{:S(2)}, u32[]{:S(2)}) collective-permute-start(f32[2,128,512]{2,1,0:T(8,128)} %own_ref.1), channel_id=1, source_target_pairs={{0,8},{8,16},{16,24},{24,32},{32,40},{40,48},{48,56},{56,64},{64,7... | collective-permute-start | bytes 1572872 | tf_op jit(solution)/shard_map/ppermute | solution.py:279
  6.6 19.5 %collective-permute-start.1 = (f32[2,128,512]{2,1,0:T(8,128)}, f32[2,128,512]{2,1,0:T(8,128)S(1)}, u32[]{:S(2)}, u32[]{:S(2)}) collective-permute-start(f32[2,128,512]{2,1,0:T(8,128)} %own_ref.1), channel_id=1, source_target_pairs={{8,0},{16,8},{24,16},{32,24},{40,32},{48,40},{56,48},{64,56},{72,6... | collective-permute-start | bytes 1572872 | tf_op jit(solution)/shard_map/ppermute | solution.py:280
  11.0 15.1 %copy-start.1 = (f32[2,256,256]{2,1,0:T(8,128)}, f32[2,256,256]{2,1,0:T(8,128)S(1)}, u32[]{:S(2)}) copy-start(f32[2,256,256]{2,1,0:T(8,128)S(1)} %collective-permute-done.2.pb_ref) | copy-start | bytes 1572868
  18.8 7.3 %copy-start.2 = (f32[2,128,512]{2,1,0:T(8,128)}, f32[2,128,512]{2,1,0:T(8,128)S(1)}, u32[]{:S(2)}) copy-start(f32[2,128,512]{2,1,0:T(8,128)S(1)} %collective-permute-done.before_ref) | copy-start | bytes 1572868
  26.1 0.8 copy-start.3
  33.9 9.5 %collective-permute-start.3 = (f32[256,256]{1,0:T(8,128)S(1)}, f32[256,256]{1,0:T(8,128)S(1)}, u32[]{:S(2)}, u32[]{:S(2)}) collective-permute-start(f32[256,256]{1,0:T(8,128)S(1)} %get-tuple-element.19), channel_id=1, source_target_pairs={{0,2},{1,3},{2,0},{3,1},{4,6},{5,7},{6,4},{7,5},{8,10},{9,11},{10,... | collective-permute-start | bytes 786440 | tf_op jit(solution)/shard_map/ppermute | solution.py:40
  37.3 10.4 %collective-permute-start.5 = (f32[256,256]{1,0:T(8,128)S(1)}, f32[256,256]{1,0:T(8,128)S(1)}, u32[]{:S(2)}, u32[]{:S(2)}) collective-permute-start(f32[256,256]{1,0:T(8,128)S(1)} %get-tuple-element.20), channel_id=1, source_target_pairs={{0,6},{1,7},{2,4},{3,5},{4,2},{5,3},{6,0},{7,1},{8,14},{9,15},{10,... | collective-permute-start | bytes 786440 | tf_op jit(solution)/shard_map/ppermute | solution.py:41
  48.8 9.5 %collective-permute-start.4 = (f32[256,256]{1,0:T(8,128)S(1)}, f32[256,256]{1,0:T(8,128)S(1)}, u32[]{:S(2)}, u32[]{:S(2)}) collective-permute-start(f32[256,256]{1,0:T(8,128)S(1)} %get-tuple-element.17), channel_id=1, source_target_pairs={{0,6},{1,7},{2,4},{3,5},{4,2},{5,3},{6,0},{7,1},{8,14},{9,15},{10,... | collective-permute-start | bytes 786440 | tf_op jit(solution)/shard_map/ppermute | solution.py:42
  52.8 8.3 %collective-permute-start.6 = (f32[256,256]{1,0:T(8,128)S(1)}, f32[256,256]{1,0:T(8,128)S(1)}, u32[]{:S(2)}, u32[]{:S(2)}) collective-permute-start(f32[256,256]{1,0:T(8,128)S(1)} %get-tuple-element.18), channel_id=1, source_target_pairs={{0,2},{1,3},{2,0},{3,1},{4,6},{5,7},{6,4},{7,5},{8,10},{9,11},{10,... | collective-permute-start | bytes 786440 | tf_op jit(solution)/shard_map/ppermute | solution.py:43
  70.4 5.6 %copy-start = (f32[2,384,512]{2,1,0:T(8,128)S(1)}, f32[2,384,512]{2,1,0:T(8,128)}, u32[]{:S(2)}) copy-start(f32[2,384,512]{2,1,0:T(8,128)} %get-tuple-element.13) | copy-start | bytes 4718596
  71.3 4.5 %collective-permute-start.7 = (f32[432,512]{1,0:T(8,128)}, f32[432,512]{1,0:T(8,128)S(1)}, u32[]{:S(2)}, u32[]{:S(2)}) collective-permute-start(f32[432,512]{1,0:T(8,128)} %pad_maximum_fusion), channel_id=1, source_target_pairs={{0,1},{1,0},{2,3},{3,2},{4,5},{5,4},{6,7},{7,6},{8,9},{9,8},{10,11... | collective-permute-start | bytes 2654216 | tf_op jit(solution)/shard_map/ppermute | solution.py:308
  77.1 10.9 %collective-permute-start.8 = (f32[144,512]{1,0:T(8,128)S(1)}, f32[144,512]{1,0:T(8,128)S(1)}, u32[]{:S(2)}, u32[]{:S(2)}) collective-permute-start(f32[144,512]{1,0:T(8,128)S(1)} %pad_maximum_fusion.2), channel_id=1, source_target_pairs={{0,8},{8,16},{16,24},{24,32},{32,40},{40,48},{48,56},{56,64},{64,7... | collective-permute-start | bytes 884744 | tf_op jit(solution)/shard_map/ppermute | solution.py:315
  79.1 14.3 %collective-permute-start.9 = (f32[144,512]{1,0:T(8,128)S(1)}, f32[144,512]{1,0:T(8,128)S(1)}, u32[]{:S(2)}, u32[]{:S(2)}) collective-permute-start(f32[144,512]{1,0:T(8,128)S(1)} %pad_maximum_fusion.3), channel_id=1, source_target_pairs={{8,0},{16,8},{24,16},{32,24},{40,32},{48,40},{56,48},{64,56},{72,6... | collective-permute-start | bytes 884744 | tf_op jit(solution)/shard_map/ppermute | solution.py:316
  93.5 8.1 %collective-permute-start.10 = (f32[2,2,16,512]{3,2,1,0:T(8,128)S(1)}, f32[2,2,16,512]{3,2,1,0:T(8,128)S(1)}, u32[]{:S(2)}, u32[]{:S(2)}) collective-permute-start(f32[2,2,16,512]{3,2,1,0:T(8,128)S(1)} %dynamic-slice_bitcast_fusion), channel_id=1, source_target_pairs={{0,6},{1,7},{2,4},{3,5},{4,2},{5,3},{6,0},{7,1},{8,14},{9,15},{10,... | collective-permute-start | bytes 393224 | tf_op jit(solution)/shard_map/ppermute | solution.py:327
  101.6 6.2 %collective-permute-start.11 = (f32[2,16,512]{2,1,0:T(8,128)S(1)}, f32[2,16,512]{2,1,0:T(8,128)S(1)}, u32[]{:S(2)}, u32[]{:S(2)}) collective-permute-start(f32[2,16,512]{2,1,0:T(8,128)S(1)} %dynamic-slice_bitcast_fusion.1), channel_id=1, source_target_pairs={{0,2},{1,3},{2,0},{3,1},{4,6},{5,7},{6,4},{7,5},{8,10},{9,11},{10,... | collective-permute-start | bytes 196616 | tf_op jit(solution)/shard_map/ppermute | solution.py:327

commit v6 on v5

--- a/solution.py
+++ b/solution.py
@@ -34,14 +34,13 @@
     return core, near, far
 
 
-def allreduce_chips(x):
+def allreduce_chips(qa, qb):
     _, near, far = mode_pairs()
-    qa, qb = x[0], x[1]
     qa = qa + lax.ppermute(qa, "mode", near)
     qb = qb + lax.ppermute(qb, "mode", far)
     qa = qa + lax.ppermute(qa, "mode", far)
     qb = qb + lax.ppermute(qb, "mode", near)
-    return jnp.stack([qa, qb])
+    return qa, qb
 
 
 def reduce_scatter_mode(x):
@@ -82,7 +81,7 @@
 
 
 def forward_kernel(roff, coff, cnt, core, before_ref, own_ref, after_ref, pa_ref, pb_ref, fr_ref, fi_ref,
-                   exit_ref, wave_ref, power_ref, ext_ref):
+                   exit_ref, wave_ref, power_a_ref, power_b_ref, ext_ref):
     i = pl.program_id(0)
     slots = roff.shape[0]
     pat = pa_ref.shape[1]
@@ -90,6 +89,15 @@
     g = core[0] + 2 * i
     gi = jnp.minimum(g, slots - 1)
     live = g < cnt[0]
+
+    def store_power(value):
+        @pl.when(i == 0)
+        def _():
+            power_a_ref[...] = value
+
+        @pl.when(i == 1)
+        def _():
+            power_b_ref[...] = value
 
     @pl.when(i == 0)
     def _():
@@ -121,7 +129,7 @@
             wave_ref[0, k, 1] = v_im
             part = v_re * v_re + v_im * v_im
             total = part if total is None else total + part
-        power_ref[i] = total
+        store_power(total)
 
     @pl.when(g == slots)
     def _():
@@ -131,16 +139,17 @@
             p_im = p_ref[1]
             part = p_re * p_re + p_im * p_im
             total = part if total is None else total + part
-        power_ref[i] = total
+        store_power(total)
 
     @pl.when(jnp.logical_and(jnp.logical_not(live), g != slots))
     def _():
-        power_ref[i] = jnp.zeros((pat, pat), jnp.float32)
-
-
-def backward_kernel(roff, coff, cnt, core, exit_ref, wave_ref, model_ref, meas_ref, pa_ref, pb_ref,
-                    ppt_ref, fr_ref, fi_ref, numer_ref, illum_ref):
+        store_power(jnp.zeros((pat, pat), jnp.float32))
+
+
+def backward_kernel(roff, coff, cnt, core, exit_ref, wave_ref, ma_ref, mb_ref, meas_ref, pa_ref, pb_ref,
+                    fr_ref, fi_ref, keep_ref, message_ref, own_illum_ref, numer_ref, illum_ref):
     i = pl.program_id(0)
+    last = pl.num_programs(0) - 1
     slots = roff.shape[0]
     g = core[0] + 2 * i
     gi = jnp.minimum(g, slots - 1)
@@ -154,7 +163,8 @@
     def _():
         r = roff[gi]
         c = coff[gi]
-        scaling = jnp.sqrt(meas_ref[0]) / jnp.maximum(jnp.sqrt(model_ref[0]), 1.0)
+        model = jnp.where(i == 0, ma_ref[...], mb_ref[...])
+        scaling = jnp.sqrt(meas_ref[0]) / jnp.maximum(jnp.sqrt(model), 1.0)
         fr = fr_ref[...]
         fi = fi_ref[...]
         n_re = None
@@ -175,12 +185,35 @@
         _place(numer_ref.at[0], n_re, r, c)
         _place(numer_ref.at[1], n_im, r, c)
 
-    @pl.when(jnp.logical_and(core[0] == 1, i == pl.num_programs(0) - 1))
+    @pl.when(jnp.logical_and(core[0] == 1, i == last))
     def _():
         for slot in range(slots):
             @pl.when(slot < cnt[0])
             def _():
-                _place(illum_ref, ppt_ref[0], roff[slot], coff[slot])
+                _place(illum_ref, mb_ref[...], roff[slot], coff[slot])
+
+    @pl.when(i == last)
+    def _():
+        side = core[0]
+        mode = core[1]
+        partner = mode + 1 - 2 * side
+        band = numer_ref.shape[1] // 3
+        share = band // 8
+        quads = 4
+        for ch in range(2):
+            for b in range(3):
+                for q in range(quads):
+                    dst = ((ch * 3 + b) * quads + q) * share
+                    kept = pl.multiple_of(b * band + (2 * q + side) * share, 8)
+                    sent = pl.multiple_of(b * band + (2 * q + 1 - side) * share, 8)
+                    keep_ref[dst : dst + share, :] = numer_ref[ch, pl.ds(kept, share), :]
+                    message_ref[dst : dst + share, :] = numer_ref[ch, pl.ds(sent, share), :]
+        top = 2 * 3 * quads * share
+        for b in range(3):
+            theirs = pl.multiple_of(b * band + partner * share, 8)
+            mine = pl.multiple_of(b * band + mode * share, 8)
+            message_ref[top + b * share : top + (b + 1) * share, :] = illum_ref[pl.ds(theirs, share), :]
+            own_illum_ref[b * share : (b + 1) * share, :] = illum_ref[pl.ds(mine, share), :]
 
 
 def run_forward(before, own, after, pa, pb, fr, fi, roff, coff, cnt, core):
@@ -209,28 +242,32 @@
             out_specs=[
                 pl.BlockSpec((1, 2, 2, pat, pat), per5),
                 pl.BlockSpec((1, 2, 2, pat, pat), per5),
-                pl.BlockSpec((local, pat, pat), whole3),
+                pl.BlockSpec((pat, pat), whole2),
+                pl.BlockSpec((pat, pat), whole2),
             ],
             scratch_shapes=[pltpu.VMEM(ext_shape, jnp.float32)],
         ),
         out_shape=[
             jax.ShapeDtypeStruct((local, 2, 2, pat, pat), jnp.bfloat16),
             jax.ShapeDtypeStruct((local, 2, 2, pat, pat), jnp.float32),
-            jax.ShapeDtypeStruct((local, pat, pat), jnp.float32),
+            jax.ShapeDtypeStruct((pat, pat), jnp.float32),
+            jax.ShapeDtypeStruct((pat, pat), jnp.float32),
         ],
         compiler_params=pltpu.CompilerParams(dimension_semantics=("arbitrary",)),
         cost_estimate=pl.CostEstimate(flops=flops, transcendentals=0, bytes_accessed=10 * 1024 * 1024),
     )(roff, coff, cnt, core, before, own, after, pa, pb, fr, fi)
 
 
-def run_backward(exits, waves, totals, measured, pa, pb, fr, fi, roff, coff, cnt, core, ext_rows, width):
+def run_backward(exits, waves, model_a, model_b, measured, pa, pb, fr, fi, roff, coff, cnt, ids,
+                 ext_rows, width):
     slots = roff.shape[0]
     local = (slots + 1) // 2
     pat = pa.shape[1]
+    share = ext_rows // 3 // 8
+    kept_rows = 2 * ext_rows // 2
     whole3 = lambda i, *_: (0, 0, 0)
     whole2 = lambda i, *_: (0, 0)
     per5 = lambda i, *_: (i, 0, 0, 0, 0)
-    per3 = lambda i, *_: (i, 0, 0)
     slot_of = lambda i, roff, coff, cnt, core: (jnp.minimum(core[0] + 2 * i, slots - 1), 0, 0)
     flops = local * 2 * 8 * 2 * pat ** 3
     return pl.pallas_call(
@@ -241,26 +278,32 @@
             in_specs=[
                 pl.BlockSpec((1, 2, 2, pat, pat), per5),
                 pl.BlockSpec((1, 2, 2, pat, pat), per5),
-                pl.BlockSpec((1, pat, pat), per3),
+                pl.BlockSpec((pat, pat), whole2),
+                pl.BlockSpec((pat, pat), whole2),
                 pl.BlockSpec((1, pat, pat), slot_of),
                 pl.BlockSpec(pa.shape, whole3),
                 pl.BlockSpec(pb.shape, whole3),
-                pl.BlockSpec((1, pat, pat), lambda i, *_: (local - 1, 0, 0)),
                 pl.BlockSpec(fr.shape, whole2),
                 pl.BlockSpec(fi.shape, whole2),
             ],
             out_specs=[
-                pl.BlockSpec((2, ext_rows, width), whole3),
-                pl.BlockSpec((ext_rows, width), whole2),
+                pl.BlockSpec((kept_rows, width), whole2),
+                pl.BlockSpec((kept_rows + 3 * share, width), whole2),
+                pl.BlockSpec((3 * share, width), whole2),
+            ],
+            scratch_shapes=[
+                pltpu.VMEM((2, ext_rows, width), jnp.float32),
+                pltpu.VMEM((ext_rows, width), jnp.float32),
             ],
         ),
         out_shape=[
-            jax.ShapeDtypeStruct((2, ext_rows, width), jnp.float32),
-            jax.ShapeDtypeStruct((ext_rows, width), jnp.float32),
+            jax.ShapeDtypeStruct((kept_rows, width), jnp.float32),
+            jax.ShapeDtypeStruct((kept_rows + 3 * share, width), jnp.float32),
+            jax.ShapeDtypeStruct((3 * share, width), jnp.float32),
         ],
         compiler_params=pltpu.CompilerParams(dimension_semantics=("arbitrary",)),
-        cost_estimate=pl.CostEstimate(flops=flops, transcendentals=0, bytes_accessed=14 * 1024 * 1024),
-    )(roff, coff, cnt, core, exits, waves, totals, measured, pa, pb, totals, fr, fi)
+        cost_estimate=pl.CostEstimate(flops=flops, transcendentals=0, bytes_accessed=12 * 1024 * 1024),
+    )(roff, coff, cnt, ids, exits, waves, model_a, model_b, measured, pa, pb, fr, fi)
 
 
 def local(object_field, probe, measured, row_offsets, col_offsets, tile_counts):
@@ -284,31 +327,22 @@
     roff = row_offsets.astype(jnp.int32)
     coff = col_offsets.astype(jnp.int32)
     cnt = tile_counts.astype(jnp.int32)
-    core_arr = jnp.reshape(core, (1,)).astype(jnp.int32)
-
-    exits, waves, power = run_forward(
-        before, object_field, after, probe2, partner_probe, fr, fi, roff, coff, cnt, core_arr
-    )
-    totals = allreduce_chips(power)
-    numer, illum = run_backward(
-        exits, waves, totals, measured, probe2, partner_probe, fr, fi, roff, coff, cnt, core_arr,
+    ids = jnp.stack([core, my_mode]).astype(jnp.int32)
+
+    exits, waves, power_a, power_b = run_forward(
+        before, object_field, after, probe2, partner_probe, fr, fi, roff, coff, cnt, ids
+    )
+    model_a, model_b = allreduce_chips(power_a, power_b)
+    kept, message, own_illum = run_backward(
+        exits, waves, model_a, model_b, measured, probe2, partner_probe, fr, fi, roff, coff, cnt, ids,
         ext_rows, width
     )
 
-    blocks = numer.reshape(2, 3, 2, 2, 2, share_rows, width)
-    keep = lax.dynamic_index_in_dim(blocks, core, axis=4, keepdims=False)
-    send = lax.dynamic_index_in_dim(blocks, 1 - core, axis=4, keepdims=False)
-    illum_blocks = illum.reshape(3, mode_count, share_rows, width)
-    partner = my_mode + 1 - 2 * core
-    illum_partner = lax.dynamic_index_in_dim(illum_blocks, partner, axis=1, keepdims=False)
-    numer_rows = send.size // width
-    message = jnp.concatenate(
-        [send.reshape(numer_rows, width), illum_partner.reshape(-1, width)], axis=0
-    )
     got = lax.ppermute(message, "mode", core_pairs)
-    blocks = keep + got[:numer_rows].reshape(keep.shape)
-    own_illum = lax.dynamic_index_in_dim(illum_blocks, my_mode, axis=1, keepdims=False)
-    own_illum = own_illum + got[numer_rows:].reshape(own_illum.shape)
+    numer_rows = kept.shape[0]
+    block_shape = (2, 3, 2, 2, share_rows, width)
+    blocks = kept.reshape(block_shape) + got[:numer_rows].reshape(block_shape)
+    own_illum = own_illum.reshape(3, share_rows, width) + got[numer_rows:].reshape(3, share_rows, width)
     band_rows = 2 * 4 * share_rows
     to_next = jnp.concatenate([blocks[:, 2].reshape(band_rows, width), own_illum[2]], axis=0)
     to_prev = jnp.concatenate([blocks[:, 0].reshape(band_rows, width), own_illum[0]], axis=0)

time: 110 us -> 104 us (0.945)
  the two profiles are of different devices: /device:TPU:120 before, /device:TPU:248 now
where the time goes in v6:
time: 104 us; the launch traced here: 103 us
  waiting for transfers between devices  46.6 us (45%)
  starting transfers between devices  33.2 us (32%)
  Pallas kernels  12.2 us (12%)
  other arithmetic  9.6 us (9%)
    ppermute x2, waiting for transfers between devices, local(): tile = keep + lax.ppermute(send, 'mode', pairs)  9.23 us
    ppermute x1, waiting for transfers between devices, local(): after = lax.ppermute(object_field, 'pos', neighbour_pairs(pos_count, -1))  7.33 us
    ppermute x1, waiting for transfers between devices, local(): before = lax.ppermute(object_field, 'pos', neighbour_pairs(pos_count, 1))  7.19 us
    pallas_call x1, Pallas kernels, run_backward(): pl.pallas_call(backward_kernel, grid_spec=pltpu.PrefetchScalarGridSpec(nu...  6.27 us
    pallas_call x1, Pallas kernels, run_forward(): pl.pallas_call(forward_kernel, grid_spec=pltpu.PrefetchScalarGridSpec(num...  5.92 us
    ppermute x1, waiting for transfers between devices, local(): from_next = lax.ppermute(to_prev, 'pos', neighbour_pairs(pos_count, -1))  5.26 us
    ppermute x1, waiting for transfers between devices, allreduce_chips(): qa = qa + lax.ppermute(qa, 'mode', far)  5.07 us
    ppermute x1, waiting for transfers between devices, local(): from_prev = lax.ppermute(to_next, 'pos', neighbour_pairs(pos_count, 1))  5.02 us
  transfers between devices with their start and end apart: 12, of which 11 were waited for; matrix products, arithmetic and copies ran while one was open for 5% of the time, Pallas kernels for 0%

profile of v6, /device:TPU:248, one launch (start us, length us, event | category | flops | bytes accessed | tf_op | source)
XLA Modules:
  0.0 103.5 jit_solution(10061648380454358027)
XLA Ops:
  0.0 1.9 %collective-permute-start.2 = (f32[2,256,256]{2,1,0:T(8,128)}, f32[2,256,256]{2,1,0:T(8,128)S(1)}, u32[]{:S(2)}, u32[]{:S(2)}) collective-permute-start(f32[2,256,256]{2,1,0:T(8,128)} %bitcast.35), channel_id=1, source_target_pairs={{0,1},{1,0},{2,3},{3,2},{4,5},{5,4},{6,7},{7,6},{8,9},{9,8},{10,11... | collective-permute-start | bytes 1572872 | tf_op jit(solution)/shard_map/ppermute | solution.py:324
  1.9 4.7 %collective-permute-start = (f32[2,128,512]{2,1,0:T(8,128)}, f32[2,128,512]{2,1,0:T(8,128)S(1)}, u32[]{:S(2)}, u32[]{:S(2)}) collective-permute-start(f32[2,128,512]{2,1,0:T(8,128)} %own_ref.1), channel_id=1, source_target_pairs={{0,8},{8,16},{16,24},{24,32},{32,40},{40,48},{48,56},{56,64},{64,7... | collective-permute-start | bytes 1572872 | tf_op jit(solution)/shard_map/ppermute | solution.py:322
  6.6 1.9 %collective-permute-start.1 = (f32[2,128,512]{2,1,0:T(8,128)}, f32[2,128,512]{2,1,0:T(8,128)S(1)}, u32[]{:S(2)}, u32[]{:S(2)}) collective-permute-start(f32[2,128,512]{2,1,0:T(8,128)} %own_ref.1), channel_id=1, source_target_pairs={{8,0},{16,8},{24,16},{32,24},{40,32},{48,40},{56,48},{64,56},{72,6... | collective-permute-start | bytes 1572872 | tf_op jit(solution)/shard_map/ppermute | solution.py:323
  9.8 1.7 %multiply_convert_fusion = (bf16[256,256]{1,0:T(8,128)(2,1)}, bf16[256,256]{1,0:T(8,128)(2,1)}) fusion(), kind=kLoop, calls=%fused_computation.12 | loop fusion | flops 1245184 | bytes 262144 | tf_op jit(solution)/shard_map/convert_element_type | solution.py:18
  11.6 7.2 %collective-permute-done.before_ref = f32[2,128,512]{2,1,0:T(8,128)S(1)} collective-permute-done((f32[2,128,512]{2,1,0:T(8,128)}, f32[2,128,512]{2,1,0:T(8,128)S(1)}, u32[]{:S(2)}, u32[]{:S(2)}) %collective-permute-start) | collective-permute-done | bytes 524320 | tf_op jit(solution)/shard_map/ppermute | solution.py:322
  18.8 7.3 %collective-permute-done.1.after_ref = f32[2,128,512]{2,1,0:T(8,128)S(1)} collective-permute-done((f32[2,128,512]{2,1,0:T(8,128)}, f32[2,128,512]{2,1,0:T(8,128)S(1)}, u32[]{:S(2)}, u32[]{:S(2)}) %collective-permute-start.1) | collective-permute-done | bytes 524320 | tf_op jit(solution)/shard_map/ppermute | solution.py:323
  26.9 5.9 %shard_map.64 = (bf16[2,2,2,256,256]{4,3,2,1,0:T(8,128)(2,1)}, f32[2,2,2,256,256]{4,3,2,1,0:T(8,128)}, f32[256,256]{1,0:T(8,128)}, f32[256,256]{1,0:T(8,128)}) custom-call(s32[3]{0:T(128)} %roff.3, s32[3]{0:T(128)} %coff.3, s32[1]{0:T(128)S(6)} %copy.25.cnt, s32[2]{0:T(128)} %pad_add_fusion.core, f32[2,128,512]{2,1,0:T(8,128)} %copy-done.1, ...), custom_call_target="tpu_custom_call" | custom-call | flops 1073741824 | bytes 10485760 | tf_op jit(solution)/shard_map/pallas_call | solution.py:228
  32.8 4.7 %collective-permute-start.5 = (f32[256,256]{1,0:T(8,128)}, f32[256,256]{1,0:T(8,128)S(1)}, u32[]{:S(2)}, u32[]{:S(2)}) collective-permute-start(f32[256,256]{1,0:T(8,128)} %get-tuple-element.15), channel_id=1, source_target_pairs={{0,6},{1,7},{2,4},{3,5},{4,2},{5,3},{6,0},{7,1},{8,14},{9,15},{10,... | collective-permute-start | bytes 786440 | tf_op jit(solution)/shard_map/ppermute | solution.py:40
  37.5 2.1 %collective-permute-start.3 = (f32[256,256]{1,0:T(8,128)}, f32[256,256]{1,0:T(8,128)S(1)}, u32[]{:S(2)}, u32[]{:S(2)}) collective-permute-start(f32[256,256]{1,0:T(8,128)} %get-tuple-element.14), channel_id=1, source_target_pairs={{0,2},{1,3},{2,0},{3,1},{4,6},{5,7},{6,4},{7,5},{8,10},{9,11},{10,... | collective-permute-start | bytes 786440 | tf_op jit(solution)/shard_map/ppermute | solution.py:39
  39.6 2.9 %collective-permute-done.5 = f32[256,256]{1,0:T(8,128)S(1)} collective-permute-done((f32[256,256]{1,0:T(8,128)}, f32[256,256]{1,0:T(8,128)S(1)}, u32[]{:S(2)}, u32[]{:S(2)}) %collective-permute-start.5) | collective-permute-done | bytes 262176 | tf_op jit(solution)/shard_map/ppermute | solution.py:40
  43.5 2.2 %collective-permute-start.6 = (f32[256,256]{1,0:T(8,128)S(1)}, f32[256,256]{1,0:T(8,128)S(1)}, u32[]{:S(2)}, u32[]{:S(2)}) collective-permute-start(f32[256,256]{1,0:T(8,128)S(1)} %add.97), channel_id=1, source_target_pairs={{0,2},{1,3},{2,0},{3,1},{4,6},{5,7},{6,4},{7,5},{8,10},{9,11},{10,... | collective-permute-start | bytes 786440 | tf_op jit(solution)/shard_map/ppermute | solution.py:42
  48.1 3.0 %collective-permute-start.4 = (f32[256,256]{1,0:T(8,128)S(1)}, f32[256,256]{1,0:T(8,128)S(1)}, u32[]{:S(2)}, u32[]{:S(2)}) collective-permute-start(f32[256,256]{1,0:T(8,128)S(1)} %add.95), channel_id=1, source_target_pairs={{0,6},{1,7},{2,4},{3,5},{4,2},{5,3},{6,0},{7,1},{8,14},{9,15},{10,... | collective-permute-start | bytes 786440 | tf_op jit(solution)/shard_map/ppermute | solution.py:41
  52.5 5.1 %collective-permute-done.4 = f32[256,256]{1,0:T(8,128)S(1)} collective-permute-done((f32[256,256]{1,0:T(8,128)S(1)}, f32[256,256]{1,0:T(8,128)S(1)}, u32[]{:S(2)}, u32[]{:S(2)}) %collective-permute-start.4) | collective-permute-done | bytes 262176 | tf_op jit(solution)/shard_map/ppermute | solution.py:41
  58.3 6.3 %shard_map.65 = (f32[384,512]{1,0:T(8,128)}, f32[432,512]{1,0:T(8,128)}, f32[48,512]{1,0:T(8,128)}) custom-call(s32[3]{0:T(128)} %roff.3, s32[3]{0:T(128)} %coff.3, s32[1]{0:T(128)S(6)} %copy.25.cnt, s32[2]{0:T(128)} %pad_add_fusion.core, bf16[2,2,2,256,256]{4,3,2,1,0:T(8,128)(2,1)} %get-tuple-element.12.exit_ref, ...), custom_call_target="tpu_custom_call" | custom-call | flops 1073741824 | bytes 12582912 | tf_op jit(solution)/shard_map/pallas_call | solution.py:273
  64.6 1.9 %collective-permute-start.7 = (f32[432,512]{1,0:T(8,128)}, f32[432,512]{1,0:T(8,128)S(1)}, u32[]{:S(2)}, u32[]{:S(2)}) collective-permute-start(f32[432,512]{1,0:T(8,128)} %get-tuple-element.17), channel_id=1, source_target_pairs={{0,1},{1,0},{2,3},{3,2},{4,5},{5,4},{6,7},{7,6},{8,9},{9,8},{10,11... | collective-permute-start | bytes 2654216 | tf_op jit(solution)/shard_map/ppermute | solution.py:341
  66.5 2.6 %collective-permute-done.7 = f32[432,512]{1,0:T(8,128)S(1)} collective-permute-done((f32[432,512]{1,0:T(8,128)}, f32[432,512]{1,0:T(8,128)S(1)}, u32[]{:S(2)}, u32[]{:S(2)}) %collective-permute-start.7) | collective-permute-done | bytes 884768 | tf_op jit(solution)/shard_map/ppermute | solution.py:341
  71.4 1.9 %collective-permute-start.8 = (f32[144,512]{1,0:T(8,128)S(1)}, f32[144,512]{1,0:T(8,128)S(1)}, u32[]{:S(2)}, u32[]{:S(2)}) collective-permute-start(f32[144,512]{1,0:T(8,128)S(1)} %pad_maximum_fusion), channel_id=1, source_target_pairs={{0,8},{8,16},{16,24},{24,32},{32,40},{40,48},{48,56},{56,64},{64,7... | collective-permute-start | bytes 884744 | tf_op jit(solution)/shard_map/ppermute | solution.py:349
  73.3 3.9 %collective-permute-start.9 = (f32[144,512]{1,0:T(8,128)S(1)}, f32[144,512]{1,0:T(8,128)S(1)}, u32[]{:S(2)}, u32[]{:S(2)}) collective-permute-start(f32[144,512]{1,0:T(8,128)S(1)} %pad_maximum_fusion.1), channel_id=1, source_target_pairs={{8,0},{16,8},{24,16},{32,24},{40,32},{48,40},{56,48},{64,56},{72,6... | collective-permute-start | bytes 884744 | tf_op jit(solution)/shard_map/ppermute | solution.py:350
  77.3 5.0 %collective-permute-done.8 = f32[144,512]{1,0:T(8,128)S(1)} collective-permute-done((f32[144,512]{1,0:T(8,128)S(1)}, f32[144,512]{1,0:T(8,128)S(1)}, u32[]{:S(2)}, u32[]{:S(2)}) %collective-permute-start.8) | collective-permute-done | bytes 294944 | tf_op jit(solution)/shard_map/ppermute | solution.py:349
  82.3 5.3 %collective-permute-done.9 = f32[144,512]{1,0:T(8,128)S(1)} collective-permute-done((f32[144,512]{1,0:T(8,128)S(1)}, f32[144,512]{1,0:T(8,128)S(1)}, u32[]{:S(2)}, u32[]{:S(2)}) %collective-permute-start.9) | collective-permute-done | bytes 294944 | tf_op jit(solution)/shard_map/ppermute | solution.py:350
  87.7 3.0 %collective-permute-start.10 = (f32[2,2,16,512]{3,2,1,0:T(8,128)S(1)}, f32[2,2,16,512]{3,2,1,0:T(8,128)S(1)}, u32[]{:S(2)}, u32[]{:S(2)}) collective-permute-start(f32[2,2,16,512]{3,2,1,0:T(8,128)S(1)} %dynamic-slice_bitcast_fusion), channel_id=1, source_target_pairs={{0,6},{1,7},{2,4},{3,5},{4,2},{5,3},{6,0},{7,1},{8,14},{9,15},{10,... | collective-permute-start | bytes 393224 | tf_op jit(solution)/shard_map/ppermute | solution.py:361
  90.8 5.0 %collective-permute-done.10 = f32[2,2,16,512]{3,2,1,0:T(8,128)S(1)} collective-permute-done((f32[2,2,16,512]{3,2,1,0:T(8,128)S(1)}, f32[2,2,16,512]{3,2,1,0:T(8,128)S(1)}, u32[]{:S(2)}, u32[]{:S(2)}) %collective-permute-start.10) | collective-permute-done | bytes 131104 | tf_op jit(solution)/shard_map/ppermute | solution.py:361
  95.8 1.9 %collective-permute-start.11 = (f32[2,16,512]{2,1,0:T(8,128)S(1)}, f32[2,16,512]{2,1,0:T(8,128)S(1)}, u32[]{:S(2)}, u32[]{:S(2)}) collective-permute-start(f32[2,16,512]{2,1,0:T(8,128)S(1)} %dynamic-slice_bitcast_fusion.1), channel_id=1, source_target_pairs={{0,2},{1,3},{2,0},{3,1},{4,6},{5,7},{6,4},{7,5},{8,10},{9,11},{10,... | collective-permute-start | bytes 196616 | tf_op jit(solution)/shard_map/ppermute | solution.py:361
  97.8 4.2 %collective-permute-done.11 = f32[2,16,512]{2,1,0:T(8,128)S(1)} collective-permute-done((f32[2,16,512]{2,1,0:T(8,128)S(1)}, f32[2,16,512]{2,1,0:T(8,128)S(1)}, u32[]{:S(2)}, u32[]{:S(2)}) %collective-permute-start.11) | collective-permute-done | bytes 65568 | tf_op jit(solution)/shard_map/ppermute | solution.py:361
  (28 shorter events, 10.9 us)
Async XLA Ops:
  0.0 11.6 %collective-permute-start.2 = (f32[2,256,256]{2,1,0:T(8,128)}, f32[2,256,256]{2,1,0:T(8,128)S(1)}, u32[]{:S(2)}, u32[]{:S(2)}) collective-permute-start(f32[2,256,256]{2,1,0:T(8,128)} %bitcast.35), channel_id=1, source_target_pairs={{0,1},{1,0},{2,3},{3,2},{4,5},{5,4},{6,7},{7,6},{8,9},{9,8},{10,11... | collective-permute-start | bytes 1572872 | tf_op jit(solution)/shard_map/ppermute | solution.py:324
  1.9 16.8 %collective-permute-start = (f32[2,128,512]{2,1,0:T(8,128)}, f32[2,128,512]{2,1,0:T(8,128)S(1)}, u32[]{:S(2)}, u32[]{:S(2)}) collective-permute-start(f32[2,128,512]{2,1,0:T(8,128)} %own_ref.1), channel_id=1, source_target_pairs={{0,8},{8,16},{16,24},{24,32},{32,40},{40,48},{48,56},{56,64},{64,7... | collective-permute-start | bytes 1572872 | tf_op jit(solution)/shard_map/ppermute | solution.py:322
  6.6 19.5 %collective-permute-start.1 = (f32[2,128,512]{2,1,0:T(8,128)}, f32[2,128,512]{2,1,0:T(8,128)S(1)}, u32[]{:S(2)}, u32[]{:S(2)}) collective-permute-start(f32[2,128,512]{2,1,0:T(8,128)} %own_ref.1), channel_id=1, source_target_pairs={{8,0},{16,8},{24,16},{32,24},{40,32},{48,40},{56,48},{64,56},{72,6... | collective-permute-start | bytes 1572872 | tf_op jit(solution)/shard_map/ppermute | solution.py:323
  11.6 14.5 %copy-start = (f32[2,256,256]{2,1,0:T(8,128)}, f32[2,256,256]{2,1,0:T(8,128)S(1)}, u32[]{:S(2)}) copy-start(f32[2,256,256]{2,1,0:T(8,128)S(1)} %collective-permute-done.2.pb_ref) | copy-start | bytes 1572868
  18.8 7.3 %copy-start.1 = (f32[2,128,512]{2,1,0:T(8,128)}, f32[2,128,512]{2,1,0:T(8,128)S(1)}, u32[]{:S(2)}) copy-start(f32[2,128,512]{2,1,0:T(8,128)S(1)} %collective-permute-done.before_ref) | copy-start | bytes 1572868
  26.1 0.8 copy-start.2
  32.8 9.7 %collective-permute-start.5 = (f32[256,256]{1,0:T(8,128)}, f32[256,256]{1,0:T(8,128)S(1)}, u32[]{:S(2)}, u32[]{:S(2)}) collective-permute-start(f32[256,256]{1,0:T(8,128)} %get-tuple-element.15), channel_id=1, source_target_pairs={{0,6},{1,7},{2,4},{3,5},{4,2},{5,3},{6,0},{7,1},{8,14},{9,15},{10,... | collective-permute-start | bytes 786440 | tf_op jit(solution)/shard_map/ppermute | solution.py:40
  37.5 9.6 %collective-permute-start.3 = (f32[256,256]{1,0:T(8,128)}, f32[256,256]{1,0:T(8,128)S(1)}, u32[]{:S(2)}, u32[]{:S(2)}) collective-permute-start(f32[256,256]{1,0:T(8,128)} %get-tuple-element.14), channel_id=1, source_target_pairs={{0,2},{1,3},{2,0},{3,1},{4,6},{5,7},{6,4},{7,5},{8,10},{9,11},{10,... | collective-permute-start | bytes 786440 | tf_op jit(solution)/shard_map/ppermute | solution.py:39
  43.5 8.3 %collective-permute-start.6 = (f32[256,256]{1,0:T(8,128)S(1)}, f32[256,256]{1,0:T(8,128)S(1)}, u32[]{:S(2)}, u32[]{:S(2)}) collective-permute-start(f32[256,256]{1,0:T(8,128)S(1)} %add.97), channel_id=1, source_target_pairs={{0,2},{1,3},{2,0},{3,1},{4,6},{5,7},{6,4},{7,5},{8,10},{9,11},{10,... | collective-permute-start | bytes 786440 | tf_op jit(solution)/shard_map/ppermute | solution.py:42
  48.1 9.5 %collective-permute-start.4 = (f32[256,256]{1,0:T(8,128)S(1)}, f32[256,256]{1,0:T(8,128)S(1)}, u32[]{:S(2)}, u32[]{:S(2)}) collective-permute-start(f32[256,256]{1,0:T(8,128)S(1)} %add.95), channel_id=1, source_target_pairs={{0,6},{1,7},{2,4},{3,5},{4,2},{5,3},{6,0},{7,1},{8,14},{9,15},{10,... | collective-permute-start | bytes 786440 | tf_op jit(solution)/shard_map/ppermute | solution.py:41
  64.6 4.5 %collective-permute-start.7 = (f32[432,512]{1,0:T(8,128)}, f32[432,512]{1,0:T(8,128)S(1)}, u32[]{:S(2)}, u32[]{:S(2)}) collective-permute-start(f32[432,512]{1,0:T(8,128)} %get-tuple-element.17), channel_id=1, source_target_pairs={{0,1},{1,0},{2,3},{3,2},{4,5},{5,4},{6,7},{7,6},{8,9},{9,8},{10,11... | collective-permute-start | bytes 2654216 | tf_op jit(solution)/shard_map/ppermute | solution.py:341
  71.4 10.9 %collective-permute-start.8 = (f32[144,512]{1,0:T(8,128)S(1)}, f32[144,512]{1,0:T(8,128)S(1)}, u32[]{:S(2)}, u32[]{:S(2)}) collective-permute-start(f32[144,512]{1,0:T(8,128)S(1)} %pad_maximum_fusion), channel_id=1, source_target_pairs={{0,8},{8,16},{16,24},{24,32},{32,40},{40,48},{48,56},{56,64},{64,7... | collective-permute-start | bytes 884744 | tf_op jit(solution)/shard_map/ppermute | solution.py:349
  73.3 14.3 %collective-permute-start.9 = (f32[144,512]{1,0:T(8,128)S(1)}, f32[144,512]{1,0:T(8,128)S(1)}, u32[]{:S(2)}, u32[]{:S(2)}) collective-permute-start(f32[144,512]{1,0:T(8,128)S(1)} %pad_maximum_fusion.1), channel_id=1, source_target_pairs={{8,0},{16,8},{24,16},{32,24},{40,32},{48,40},{56,48},{64,56},{72,6... | collective-permute-start | bytes 884744 | tf_op jit(solution)/shard_map/ppermute | solution.py:350
  87.7 8.1 %collective-permute-start.10 = (f32[2,2,16,512]{3,2,1,0:T(8,128)S(1)}, f32[2,2,16,512]{3,2,1,0:T(8,128)S(1)}, u32[]{:S(2)}, u32[]{:S(2)}) collective-permute-start(f32[2,2,16,512]{3,2,1,0:T(8,128)S(1)} %dynamic-slice_bitcast_fusion), channel_id=1, source_target_pairs={{0,6},{1,7},{2,4},{3,5},{4,2},{5,3},{6,0},{7,1},{8,14},{9,15},{10,... | collective-permute-start | bytes 393224 | tf_op jit(solution)/shard_map/ppermute | solution.py:361
  95.8 6.2 %collective-permute-start.11 = (f32[2,16,512]{2,1,0:T(8,128)S(1)}, f32[2,16,512]{2,1,0:T(8,128)S(1)}, u32[]{:S(2)}, u32[]{:S(2)}) collective-permute-start(f32[2,16,512]{2,1,0:T(8,128)S(1)} %dynamic-slice_bitcast_fusion.1), channel_id=1, source_target_pairs={{0,2},{1,3},{2,0},{3,1},{4,6},{5,7},{6,4},{7,5},{8,10},{9,11},{10,... | collective-permute-start | bytes 196616 | tf_op jit(solution)/shard_map/ppermute | solution.py:361

commit v7 on v6

--- a/solution.py
+++ b/solution.py
@@ -321,7 +321,8 @@
     core = my_mode % 2
     before = lax.ppermute(object_field, "pos", neighbour_pairs(pos_count, 1))
     after = lax.ppermute(object_field, "pos", neighbour_pairs(pos_count, -1))
-    partner_probe = lax.ppermute(probe2, "mode", core_pairs)
+    probe_late, before = lax.optimization_barrier((probe2, before))
+    partner_probe = lax.ppermute(probe_late, "mode", core_pairs)
     ext_rows = 3 * rows_tile
 
     roff = row_offsets.astype(jnp.int32)

time: 104 us -> 105 us (level)
  the two profiles are of different devices: /device:TPU:248 before, /device:TPU:120 now
where the time goes in v7:
time: 105 us; the launch traced here: 104 us
  waiting for transfers between devices  44 us (42%)
  starting transfers between devices  33.6 us (32%)
  Pallas kernels  14.9 us (14%)
  other arithmetic  9.6 us (9%)
  local copies, waits for them, and re-layouts  1.14 us (1%)
    ppermute x1, waiting for transfers between devices, local(): before = lax.ppermute(object_field, 'pos', neighbour_pairs(pos_count, 1))  9.55 us
    ppermute x2, waiting for transfers between devices, local(): tile = keep + lax.ppermute(send, 'mode', pairs)  8.45 us
    pallas_call x1, Pallas kernels, run_backward(): pl.pallas_call(backward_kernel, grid_spec=pltpu.PrefetchScalarGridSpec(nu...  7.94 us
    pallas_call x1, Pallas kernels, run_forward(): pl.pallas_call(forward_kernel, grid_spec=pltpu.PrefetchScalarGridSpec(num...  6.97 us
    ppermute x2, starting transfers between devices, local(): tile = keep + lax.ppermute(send, 'mode', pairs)  5.71 us
    ppermute x1, waiting for transfers between devices, allreduce_chips(): qa = qa + lax.ppermute(qa, 'mode', far)  5.45 us
    ppermute x1, waiting for transfers between devices, local(): from_next = lax.ppermute(to_prev, 'pos', neighbour_pairs(pos_count, -1))  5.26 us
    ppermute x1, waiting for transfers between devices, local(): from_prev = lax.ppermute(to_next, 'pos', neighbour_pairs(pos_count, 1))  5.02 us
  transfers between devices with their start and end apart: 12, of which 11 were waited for; matrix products, arithmetic and copies ran while one was open for 5% of the time, Pallas kernels for 0%

profile of v7, /device:TPU:120, one launch (start us, length us, event | category | flops | bytes accessed | tf_op | source)
XLA Modules:
  0.0 104.2 jit_solution(6345736201780391193)
XLA Ops:
  0.0 4.7 %collective-permute-start = (f32[2,128,512]{2,1,0:T(8,128)}, f32[2,128,512]{2,1,0:T(8,128)S(1)}, u32[]{:S(2)}, u32[]{:S(2)}) collective-permute-start(f32[2,128,512]{2,1,0:T(8,128)} %own_ref.1), channel_id=1, source_target_pairs={{0,8},{8,16},{16,24},{24,32},{32,40},{40,48},{48,56},{56,64},{64,7... | collective-permute-start | bytes 1572872 | tf_op jit(solution)/shard_map/ppermute | solution.py:322
  4.7 1.9 %collective-permute-start.1 = (f32[2,128,512]{2,1,0:T(8,128)}, f32[2,128,512]{2,1,0:T(8,128)S(1)}, u32[]{:S(2)}, u32[]{:S(2)}) collective-permute-start(f32[2,128,512]{2,1,0:T(8,128)} %own_ref.1), channel_id=1, source_target_pairs={{8,0},{16,8},{24,16},{32,24},{40,32},{48,40},{56,48},{64,56},{72,6... | collective-permute-start | bytes 1572872 | tf_op jit(solution)/shard_map/ppermute | solution.py:323
  6.6 9.5 %collective-permute-done.before_ref = f32[2,128,512]{2,1,0:T(8,128)S(1)} collective-permute-done((f32[2,128,512]{2,1,0:T(8,128)}, f32[2,128,512]{2,1,0:T(8,128)S(1)}, u32[]{:S(2)}, u32[]{:S(2)}) %collective-permute-start) | collective-permute-done | bytes 524320 | tf_op jit(solution)/shard_map/ppermute | solution.py:322
  16.2 1.9 %collective-permute-start.2 = (f32[2,256,256]{2,1,0:T(8,128)}, f32[2,256,256]{2,1,0:T(8,128)S(1)}, u32[]{:S(2)}, u32[]{:S(2)}) collective-permute-start(f32[2,256,256]{2,1,0:T(8,128)} %bitcast.35), channel_id=1, source_target_pairs={{0,1},{1,0},{2,3},{3,2},{4,5},{5,4},{6,7},{7,6},{8,9},{9,8},{10,11... | collective-permute-start | bytes 1572872 | tf_op jit(solution)/shard_map/ppermute | solution.py:325
  21.1 2.4 %collective-permute-done.1.after_ref = f32[2,128,512]{2,1,0:T(8,128)S(1)} collective-permute-done((f32[2,128,512]{2,1,0:T(8,128)}, f32[2,128,512]{2,1,0:T(8,128)S(1)}, u32[]{:S(2)}, u32[]{:S(2)}) %collective-permute-start.1) | collective-permute-done | bytes 524320 | tf_op jit(solution)/shard_map/ppermute | solution.py:323
  24.5 7.0 %shard_map.64 = (bf16[2,2,2,256,256]{4,3,2,1,0:T(8,128)(2,1)}, f32[2,2,2,256,256]{4,3,2,1,0:T(8,128)}, f32[256,256]{1,0:T(8,128)}, f32[256,256]{1,0:T(8,128)}) custom-call(s32[3]{0:T(128)} %roff.3, s32[3]{0:T(128)} %coff.3, s32[1]{0:T(128)S(6)} %copy.25.cnt, s32[2]{0:T(128)} %pad_add_fusion.core, f32[2,128,512]{2,1,0:T(8,128)} %copy-done.1, ...), custom_call_target="tpu_custom_call" | custom-call | flops 1073741824 | bytes 10485760 | tf_op jit(solution)/shard_map/pallas_call | solution.py:228
  31.5 4.7 %collective-permute-start.5 = (f32[256,256]{1,0:T(8,128)}, f32[256,256]{1,0:T(8,128)S(1)}, u32[]{:S(2)}, u32[]{:S(2)}) collective-permute-start(f32[256,256]{1,0:T(8,128)} %get-tuple-element.19), channel_id=1, source_target_pairs={{0,6},{1,7},{2,4},{3,5},{4,2},{5,3},{6,0},{7,1},{8,14},{9,15},{10,... | collective-permute-start | bytes 786440 | tf_op jit(solution)/shard_map/ppermute | solution.py:40
  36.2 2.1 %collective-permute-start.3 = (f32[256,256]{1,0:T(8,128)}, f32[256,256]{1,0:T(8,128)S(1)}, u32[]{:S(2)}, u32[]{:S(2)}) collective-permute-start(f32[256,256]{1,0:T(8,128)} %get-tuple-element.18), channel_id=1, source_target_pairs={{0,2},{1,3},{2,0},{3,1},{4,6},{5,7},{6,4},{7,5},{8,10},{9,11},{10,... | collective-permute-start | bytes 786440 | tf_op jit(solution)/shard_map/ppermute | solution.py:39
  38.3 2.9 %collective-permute-done.5 = f32[256,256]{1,0:T(8,128)S(1)} collective-permute-done((f32[256,256]{1,0:T(8,128)}, f32[256,256]{1,0:T(8,128)S(1)}, u32[]{:S(2)}, u32[]{:S(2)}) %collective-permute-start.5) | collective-permute-done | bytes 262176 | tf_op jit(solution)/shard_map/ppermute | solution.py:40
  42.2 2.2 %collective-permute-start.6 = (f32[256,256]{1,0:T(8,128)S(1)}, f32[256,256]{1,0:T(8,128)S(1)}, u32[]{:S(2)}, u32[]{:S(2)}) collective-permute-start(f32[256,256]{1,0:T(8,128)S(1)} %add.97), channel_id=1, source_target_pairs={{0,2},{1,3},{2,0},{3,1},{4,6},{5,7},{6,4},{7,5},{8,10},{9,11},{10,... | collective-permute-start | bytes 786440 | tf_op jit(solution)/shard_map/ppermute | solution.py:42
  44.4 1.8 %collective-permute-done.3 = f32[256,256]{1,0:T(8,128)S(1)} collective-permute-done((f32[256,256]{1,0:T(8,128)}, f32[256,256]{1,0:T(8,128)S(1)}, u32[]{:S(2)}, u32[]{:S(2)}) %collective-permute-start.3) | collective-permute-done | bytes 262176 | tf_op jit(solution)/shard_map/ppermute | solution.py:39
  47.1 2.6 %collective-permute-start.4 = (f32[256,256]{1,0:T(8,128)S(1)}, f32[256,256]{1,0:T(8,128)S(1)}, u32[]{:S(2)}, u32[]{:S(2)}) collective-permute-start(f32[256,256]{1,0:T(8,128)S(1)} %add.95), channel_id=1, source_target_pairs={{0,6},{1,7},{2,4},{3,5},{4,2},{5,3},{6,0},{7,1},{8,14},{9,15},{10,... | collective-permute-start | bytes 786440 | tf_op jit(solution)/shard_map/ppermute | solution.py:41
  51.2 5.4 %collective-permute-done.4 = f32[256,256]{1,0:T(8,128)S(1)} collective-permute-done((f32[256,256]{1,0:T(8,128)S(1)}, f32[256,256]{1,0:T(8,128)S(1)}, u32[]{:S(2)}, u32[]{:S(2)}) %collective-permute-start.4) | collective-permute-done | bytes 262176 | tf_op jit(solution)/shard_map/ppermute | solution.py:41
  57.4 7.9 %shard_map.65 = (f32[384,512]{1,0:T(8,128)}, f32[432,512]{1,0:T(8,128)}, f32[48,512]{1,0:T(8,128)}) custom-call(s32[3]{0:T(128)} %roff.3, s32[3]{0:T(128)} %coff.3, s32[1]{0:T(128)S(6)} %copy.25.cnt, s32[2]{0:T(128)} %pad_add_fusion.core, bf16[2,2,2,256,256]{4,3,2,1,0:T(8,128)(2,1)} %get-tuple-element.16.exit_ref, ...), custom_call_target="tpu_custom_call" | custom-call | flops 1073741824 | bytes 12582912 | tf_op jit(solution)/shard_map/pallas_call | solution.py:273
  65.3 1.9 %collective-permute-start.7 = (f32[432,512]{1,0:T(8,128)}, f32[432,512]{1,0:T(8,128)S(1)}, u32[]{:S(2)}, u32[]{:S(2)}) collective-permute-start(f32[432,512]{1,0:T(8,128)} %get-tuple-element.21), channel_id=1, source_target_pairs={{0,1},{1,0},{2,3},{3,2},{4,5},{5,4},{6,7},{7,6},{8,9},{9,8},{10,11... | collective-permute-start | bytes 2654216 | tf_op jit(solution)/shard_map/ppermute | solution.py:342
  67.2 2.6 %collective-permute-done.7 = f32[432,512]{1,0:T(8,128)S(1)} collective-permute-done((f32[432,512]{1,0:T(8,128)}, f32[432,512]{1,0:T(8,128)S(1)}, u32[]{:S(2)}, u32[]{:S(2)}) %collective-permute-start.7) | collective-permute-done | bytes 884768 | tf_op jit(solution)/shard_map/ppermute | solution.py:342
  72.1 1.9 %collective-permute-start.8 = (f32[144,512]{1,0:T(8,128)S(1)}, f32[144,512]{1,0:T(8,128)S(1)}, u32[]{:S(2)}, u32[]{:S(2)}) collective-permute-start(f32[144,512]{1,0:T(8,128)S(1)} %pad_maximum_fusion), channel_id=1, source_target_pairs={{0,8},{8,16},{16,24},{24,32},{32,40},{40,48},{48,56},{56,64},{64,7... | collective-permute-start | bytes 884744 | tf_op jit(solution)/shard_map/ppermute | solution.py:350
  74.1 3.9 %collective-permute-start.9 = (f32[144,512]{1,0:T(8,128)S(1)}, f32[144,512]{1,0:T(8,128)S(1)}, u32[]{:S(2)}, u32[]{:S(2)}) collective-permute-start(f32[144,512]{1,0:T(8,128)S(1)} %pad_maximum_fusion.1), channel_id=1, source_target_pairs={{8,0},{16,8},{24,16},{32,24},{40,32},{48,40},{56,48},{64,56},{72,6... | collective-permute-start | bytes 884744 | tf_op jit(solution)/shard_map/ppermute | solution.py:351
  78.0 5.0 %collective-permute-done.8 = f32[144,512]{1,0:T(8,128)S(1)} collective-permute-done((f32[144,512]{1,0:T(8,128)S(1)}, f32[144,512]{1,0:T(8,128)S(1)}, u32[]{:S(2)}, u32[]{:S(2)}) %collective-permute-start.8) | collective-permute-done | bytes 294944 | tf_op jit(solution)/shard_map/ppermute | solution.py:350
  83.1 5.3 %collective-permute-done.9 = f32[144,512]{1,0:T(8,128)S(1)} collective-permute-done((f32[144,512]{1,0:T(8,128)S(1)}, f32[144,512]{1,0:T(8,128)S(1)}, u32[]{:S(2)}, u32[]{:S(2)}) %collective-permute-start.9) | collective-permute-done | bytes 294944 | tf_op jit(solution)/shard_map/ppermute | solution.py:351
  88.4 3.8 %collective-permute-start.10 = (f32[2,2,16,512]{3,2,1,0:T(8,128)S(1)}, f32[2,2,16,512]{3,2,1,0:T(8,128)S(1)}, u32[]{:S(2)}, u32[]{:S(2)}) collective-permute-start(f32[2,2,16,512]{3,2,1,0:T(8,128)S(1)} %dynamic-slice_bitcast_fusion), channel_id=1, source_target_pairs={{0,6},{1,7},{2,4},{3,5},{4,2},{5,3},{6,0},{7,1},{8,14},{9,15},{10,... | collective-permute-start | bytes 393224 | tf_op jit(solution)/shard_map/ppermute | solution.py:362
  92.3 4.2 %collective-permute-done.10 = f32[2,2,16,512]{3,2,1,0:T(8,128)S(1)} collective-permute-done((f32[2,2,16,512]{3,2,1,0:T(8,128)S(1)}, f32[2,2,16,512]{3,2,1,0:T(8,128)S(1)}, u32[]{:S(2)}, u32[]{:S(2)}) %collective-permute-start.10) | collective-permute-done | bytes 131104 | tf_op jit(solution)/shard_map/ppermute | solution.py:362
  96.6 1.9 %collective-permute-start.11 = (f32[2,16,512]{2,1,0:T(8,128)S(1)}, f32[2,16,512]{2,1,0:T(8,128)S(1)}, u32[]{:S(2)}, u32[]{:S(2)}) collective-permute-start(f32[2,16,512]{2,1,0:T(8,128)S(1)} %dynamic-slice_bitcast_fusion.1), channel_id=1, source_target_pairs={{0,2},{1,3},{2,0},{3,1},{4,6},{5,7},{6,4},{7,5},{8,10},{9,11},{10,... | collective-permute-start | bytes 196616 | tf_op jit(solution)/shard_map/ppermute | solution.py:362
  98.5 4.2 %collective-permute-done.11 = f32[2,16,512]{2,1,0:T(8,128)S(1)} collective-permute-done((f32[2,16,512]{2,1,0:T(8,128)S(1)}, f32[2,16,512]{2,1,0:T(8,128)S(1)}, u32[]{:S(2)}, u32[]{:S(2)}) %collective-permute-start.11) | collective-permute-done | bytes 65568 | tf_op jit(solution)/shard_map/ppermute | solution.py:362
  (28 shorter events, 11.4 us)
Async XLA Ops:
  0.0 16.2 %collective-permute-start = (f32[2,128,512]{2,1,0:T(8,128)}, f32[2,128,512]{2,1,0:T(8,128)S(1)}, u32[]{:S(2)}, u32[]{:S(2)}) collective-permute-start(f32[2,128,512]{2,1,0:T(8,128)} %own_ref.1), channel_id=1, source_target_pairs={{0,8},{8,16},{16,24},{24,32},{32,40},{40,48},{48,56},{56,64},{64,7... | collective-permute-start | bytes 1572872 | tf_op jit(solution)/shard_map/ppermute | solution.py:322
  4.7 18.8 %collective-permute-start.1 = (f32[2,128,512]{2,1,0:T(8,128)}, f32[2,128,512]{2,1,0:T(8,128)S(1)}, u32[]{:S(2)}, u32[]{:S(2)}) collective-permute-start(f32[2,128,512]{2,1,0:T(8,128)} %own_ref.1), channel_id=1, source_target_pairs={{8,0},{16,8},{24,16},{32,24},{40,32},{48,40},{56,48},{64,56},{72,6... | collective-permute-start | bytes 1572872 | tf_op jit(solution)/shard_map/ppermute | solution.py:323
  16.2 7.3 %copy-start.1 = (f32[2,128,512]{2,1,0:T(8,128)}, f32[2,128,512]{2,1,0:T(8,128)S(1)}, u32[]{:S(2)}) copy-start(f32[2,128,512]{2,1,0:T(8,128)S(1)} %collective-permute-done.before_ref) | copy-start | bytes 1572868
  16.2 7.3 %collective-permute-start.2 = (f32[2,256,256]{2,1,0:T(8,128)}, f32[2,256,256]{2,1,0:T(8,128)S(1)}, u32[]{:S(2)}, u32[]{:S(2)}) collective-permute-start(f32[2,256,256]{2,1,0:T(8,128)} %bitcast.35), channel_id=1, source_target_pairs={{0,1},{1,0},{2,3},{3,2},{4,5},{5,4},{6,7},{7,6},{8,9},{9,8},{10,11... | collective-permute-start | bytes 1572872 | tf_op jit(solution)/shard_map/ppermute | solution.py:325
  23.5 0.8 copy-start.2
  23.5 1.0 copy-start
  31.5 9.7 %collective-permute-start.5 = (f32[256,256]{1,0:T(8,128)}, f32[256,256]{1,0:T(8,128)S(1)}, u32[]{:S(2)}, u32[]{:S(2)}) collective-permute-start(f32[256,256]{1,0:T(8,128)} %get-tuple-element.19), channel_id=1, source_target_pairs={{0,6},{1,7},{2,4},{3,5},{4,2},{5,3},{6,0},{7,1},{8,14},{9,15},{10,... | collective-permute-start | bytes 786440 | tf_op jit(solution)/shard_map/ppermute | solution.py:40
  36.2 10.0 %collective-permute-start.3 = (f32[256,256]{1,0:T(8,128)}, f32[256,256]{1,0:T(8,128)S(1)}, u32[]{:S(2)}, u32[]{:S(2)}) collective-permute-start(f32[256,256]{1,0:T(8,128)} %get-tuple-element.18), channel_id=1, source_target_pairs={{0,2},{1,3},{2,0},{3,1},{4,6},{5,7},{6,4},{7,5},{8,10},{9,11},{10,... | collective-permute-start | bytes 786440 | tf_op jit(solution)/shard_map/ppermute | solution.py:39
  42.2 8.3 %collective-permute-start.6 = (f32[256,256]{1,0:T(8,128)S(1)}, f32[256,256]{1,0:T(8,128)S(1)}, u32[]{:S(2)}, u32[]{:S(2)}) collective-permute-start(f32[256,256]{1,0:T(8,128)S(1)} %add.97), channel_id=1, source_target_pairs={{0,2},{1,3},{2,0},{3,1},{4,6},{5,7},{6,4},{7,5},{8,10},{9,11},{10,... | collective-permute-start | bytes 786440 | tf_op jit(solution)/shard_map/ppermute | solution.py:42
  47.1 9.5 %collective-permute-start.4 = (f32[256,256]{1,0:T(8,128)S(1)}, f32[256,256]{1,0:T(8,128)S(1)}, u32[]{:S(2)}, u32[]{:S(2)}) collective-permute-start(f32[256,256]{1,0:T(8,128)S(1)} %add.95), channel_id=1, source_target_pairs={{0,6},{1,7},{2,4},{3,5},{4,2},{5,3},{6,0},{7,1},{8,14},{9,15},{10,... | collective-permute-start | bytes 786440 | tf_op jit(solution)/shard_map/ppermute | solution.py:41
  65.3 4.5 %collective-permute-start.7 = (f32[432,512]{1,0:T(8,128)}, f32[432,512]{1,0:T(8,128)S(1)}, u32[]{:S(2)}, u32[]{:S(2)}) collective-permute-start(f32[432,512]{1,0:T(8,128)} %get-tuple-element.21), channel_id=1, source_target_pairs={{0,1},{1,0},{2,3},{3,2},{4,5},{5,4},{6,7},{7,6},{8,9},{9,8},{10,11... | collective-permute-start | bytes 2654216 | tf_op jit(solution)/shard_map/ppermute | solution.py:342
  72.1 10.9 %collective-permute-start.8 = (f32[144,512]{1,0:T(8,128)S(1)}, f32[144,512]{1,0:T(8,128)S(1)}, u32[]{:S(2)}, u32[]{:S(2)}) collective-permute-start(f32[144,512]{1,0:T(8,128)S(1)} %pad_maximum_fusion), channel_id=1, source_target_pairs={{0,8},{8,16},{16,24},{24,32},{32,40},{40,48},{48,56},{56,64},{64,7... | collective-permute-start | bytes 884744 | tf_op jit(solution)/shard_map/ppermute | solution.py:350
  74.1 14.3 %collective-permute-start.9 = (f32[144,512]{1,0:T(8,128)S(1)}, f32[144,512]{1,0:T(8,128)S(1)}, u32[]{:S(2)}, u32[]{:S(2)}) collective-permute-start(f32[144,512]{1,0:T(8,128)S(1)} %pad_maximum_fusion.1), channel_id=1, source_target_pairs={{8,0},{16,8},{24,16},{32,24},{40,32},{48,40},{56,48},{64,56},{72,6... | collective-permute-start | bytes 884744 | tf_op jit(solution)/shard_map/ppermute | solution.py:351
  88.4 8.1 %collective-permute-start.10 = (f32[2,2,16,512]{3,2,1,0:T(8,128)S(1)}, f32[2,2,16,512]{3,2,1,0:T(8,128)S(1)}, u32[]{:S(2)}, u32[]{:S(2)}) collective-permute-start(f32[2,2,16,512]{3,2,1,0:T(8,128)S(1)} %dynamic-slice_bitcast_fusion), channel_id=1, source_target_pairs={{0,6},{1,7},{2,4},{3,5},{4,2},{5,3},{6,0},{7,1},{8,14},{9,15},{10,... | collective-permute-start | bytes 393224 | tf_op jit(solution)/shard_map/ppermute | solution.py:362
  96.6 6.2 %collective-permute-start.11 = (f32[2,16,512]{2,1,0:T(8,128)S(1)}, f32[2,16,512]{2,1,0:T(8,128)S(1)}, u32[]{:S(2)}, u32[]{:S(2)}) collective-permute-start(f32[2,16,512]{2,1,0:T(8,128)S(1)} %dynamic-slice_bitcast_fusion.1), channel_id=1, source_target_pairs={{0,2},{1,3},{2,0},{3,1},{4,6},{5,7},{6,4},{7,5},{8,10},{9,11},{10,... | collective-permute-start | bytes 196616 | tf_op jit(solution)/shard_map/ppermute | solution.py:362

commit v8 on v6

--- a/solution.py
+++ b/solution.py
@@ -125,8 +125,8 @@
             v_im = _dot(h_re, fi) + _dot(h_im, fr)
             exit_ref[0, k, 0] = e_re
             exit_ref[0, k, 1] = e_im
-            wave_ref[0, k, 0] = v_re
-            wave_ref[0, k, 1] = v_im
+            wave_ref[0, k, 0] = h_re
+            wave_ref[0, k, 1] = h_im
             part = v_re * v_re + v_im * v_im
             total = part if total is None else total + part
         store_power(total)
@@ -170,8 +170,12 @@
         n_re = None
         n_im = None
         for k, p_ref in enumerate((pa_ref, pb_ref)):
-            x_re = (scaling * wave_ref[0, k, 0]).astype(jnp.bfloat16)
-            x_im = (scaling * wave_ref[0, k, 1]).astype(jnp.bfloat16)
+            h_re = wave_ref[0, k, 0]
+            h_im = wave_ref[0, k, 1]
+            v_re = _dot(h_re, fr) - _dot(h_im, fi)
+            v_im = _dot(h_re, fi) + _dot(h_im, fr)
+            x_re = (scaling * v_re).astype(jnp.bfloat16)
+            x_im = (scaling * v_im).astype(jnp.bfloat16)
             b_re = (_dot(fr, x_re) + _dot(fi, x_im)).astype(jnp.bfloat16)
             b_im = (_dot(fr, x_im) - _dot(fi, x_re)).astype(jnp.bfloat16)
             d_re = _dot(b_re, fr) + _dot(b_im, fi) - exit_ref[0, k, 0].astype(jnp.float32)
@@ -249,7 +253,7 @@
         ),
         out_shape=[
             jax.ShapeDtypeStruct((local, 2, 2, pat, pat), jnp.bfloat16),
-            jax.ShapeDtypeStruct((local, 2, 2, pat, pat), jnp.float32),
+            jax.ShapeDtypeStruct((local, 2, 2, pat, pat), jnp.bfloat16),
             jax.ShapeDtypeStruct((pat, pat), jnp.float32),
             jax.ShapeDtypeStruct((pat, pat), jnp.float32),
         ],

time: 104 us -> 106 us (1.019)
  the two profiles are of different devices: /device:TPU:248 before, /device:TPU:376 now
where the time goes in v8:
time: 106 us; the launch traced here: 105 us
  waiting for transfers between devices  44.6 us (42%)
  starting transfers between devices  32.6 us (31%)
  Pallas kernels  15.7 us (15%)
  other arithmetic  8.67 us (8%)
  local copies, waits for them, and re-layouts  2.56 us (2%)
    ppermute x2, waiting for transfers between devices, local(): tile = keep + lax.ppermute(send, 'mode', pairs)  9.26 us
    pallas_call x1, Pallas kernels, run_backward(): pl.pallas_call(backward_kernel, grid_spec=pltpu.PrefetchScalarGridSpec(nu...  8.98 us
    ppermute x1, waiting for transfers between devices, local(): before = lax.ppermute(object_field, 'pos', neighbour_pairs(pos_count, 1))  7.57 us
    pallas_call x1, Pallas kernels, run_forward(): pl.pallas_call(forward_kernel, grid_spec=pltpu.PrefetchScalarGridSpec(num...  6.74 us
    ppermute x1, waiting for transfers between devices, local(): after = lax.ppermute(object_field, 'pos', neighbour_pairs(pos_count, -1))  5.63 us
    ppermute x1, waiting for transfers between devices, local(): from_prev = lax.ppermute(to_next, 'pos', neighbour_pairs(pos_count, 1))  5.02 us
    ppermute x2, starting transfers between devices, local(): tile = keep + lax.ppermute(send, 'mode', pairs)  5.02 us
    ppermute x1, starting transfers between devices, allreduce_chips(): qb = qb + lax.ppermute(qb, 'mode', far)  4.67 us
  transfers between devices with their start and end apart: 12, of which 11 were waited for; matrix products, arithmetic and copies ran while one was open for 4% of the time, Pallas kernels for 0%

profile of v8, /device:TPU:376, one launch (start us, length us, event | category | flops | bytes accessed | tf_op | source)
XLA Modules:
  0.0 105.1 jit_solution(15212071210173246177)
XLA Ops:
  0.0 1.9 %collective-permute-start.2 = (f32[2,256,256]{2,1,0:T(8,128)}, f32[2,256,256]{2,1,0:T(8,128)S(1)}, u32[]{:S(2)}, u32[]{:S(2)}) collective-permute-start(f32[2,256,256]{2,1,0:T(8,128)} %bitcast.35), channel_id=1, source_target_pairs={{0,1},{1,0},{2,3},{3,2},{4,5},{5,4},{6,7},{7,6},{8,9},{9,8},{10,11... | collective-permute-start | bytes 1572872 | tf_op jit(solution)/shard_map/ppermute | solution.py:328
  1.9 2.6 %collective-permute-start = (f32[2,128,512]{2,1,0:T(8,128)}, f32[2,128,512]{2,1,0:T(8,128)S(1)}, u32[]{:S(2)}, u32[]{:S(2)}) collective-permute-start(f32[2,128,512]{2,1,0:T(8,128)} %own_ref.1), channel_id=1, source_target_pairs={{0,8},{8,16},{16,24},{24,32},{32,40},{40,48},{48,56},{56,64},{64,7... | collective-permute-start | bytes 1572872 | tf_op jit(solution)/shard_map/ppermute | solution.py:326
  4.5 3.3 %collective-permute-start.1 = (f32[2,128,512]{2,1,0:T(8,128)}, f32[2,128,512]{2,1,0:T(8,128)S(1)}, u32[]{:S(2)}, u32[]{:S(2)}) collective-permute-start(f32[2,128,512]{2,1,0:T(8,128)} %own_ref.1), channel_id=1, source_target_pairs={{8,0},{16,8},{24,16},{32,24},{40,32},{48,40},{56,48},{64,56},{72,6... | collective-permute-start | bytes 1572872 | tf_op jit(solution)/shard_map/ppermute | solution.py:327
  9.0 1.8 %multiply_convert_fusion = (bf16[256,256]{1,0:T(8,128)(2,1)}, bf16[256,256]{1,0:T(8,128)(2,1)}) fusion(), kind=kLoop, calls=%fused_computation.12 | loop fusion | flops 1245184 | bytes 262144 | tf_op jit(solution)/shard_map/convert_element_type | solution.py:18
  10.8 7.6 %collective-permute-done.before_ref = f32[2,128,512]{2,1,0:T(8,128)S(1)} collective-permute-done((f32[2,128,512]{2,1,0:T(8,128)}, f32[2,128,512]{2,1,0:T(8,128)S(1)}, u32[]{:S(2)}, u32[]{:S(2)}) %collective-permute-start) | collective-permute-done | bytes 524320 | tf_op jit(solution)/shard_map/ppermute | solution.py:326
  18.4 5.6 %collective-permute-done.1.after_ref = f32[2,128,512]{2,1,0:T(8,128)S(1)} collective-permute-done((f32[2,128,512]{2,1,0:T(8,128)}, f32[2,128,512]{2,1,0:T(8,128)S(1)}, u32[]{:S(2)}, u32[]{:S(2)}) %collective-permute-start.1) | collective-permute-done | bytes 524320 | tf_op jit(solution)/shard_map/ppermute | solution.py:327
  24.8 6.7 %shard_map.64 = (bf16[2,2,2,256,256]{4,3,2,1,0:T(8,128)(2,1)}, bf16[2,2,2,256,256]{4,3,2,1,0:T(8,128)(2,1)}, f32[256,256]{1,0:T(8,128)}, f32[256,256]{1,0:T(8,128)}) custom-call(s32[3]{0:T(128)} %roff.3, s32[3]{0:T(128)} %coff.3, s32[1]{0:T(128)S(6)} %copy.25.cnt, s32[2]{0:T(128)} %pad_add_fusion.core, f32[2,128,512]{2,1,0:T(8,128)} %copy-done.4, ...), custom_call_target="tpu_custom_call" | custom-call | flops 1073741824 | bytes 10485760 | tf_op jit(solution)/shard_map/pallas_call | solution.py:232
  31.5 4.7 %collective-permute-start.5 = (f32[256,256]{1,0:T(8,128)}, f32[256,256]{1,0:T(8,128)S(1)}, u32[]{:S(2)}, u32[]{:S(2)}) collective-permute-start(f32[256,256]{1,0:T(8,128)} %get-tuple-element.15), channel_id=1, source_target_pairs={{0,6},{1,7},{2,4},{3,5},{4,2},{5,3},{6,0},{7,1},{8,14},{9,15},{10,... | collective-permute-start | bytes 786440 | tf_op jit(solution)/shard_map/ppermute | solution.py:40
  36.2 2.3 %collective-permute-start.3 = (f32[256,256]{1,0:T(8,128)}, f32[256,256]{1,0:T(8,128)S(1)}, u32[]{:S(2)}, u32[]{:S(2)}) collective-permute-start(f32[256,256]{1,0:T(8,128)} %get-tuple-element.14), channel_id=1, source_target_pairs={{0,2},{1,3},{2,0},{3,1},{4,6},{5,7},{6,4},{7,5},{8,10},{9,11},{10,... | collective-permute-start | bytes 786440 | tf_op jit(solution)/shard_map/ppermute | solution.py:39
  38.5 2.7 %collective-permute-done.5 = f32[256,256]{1,0:T(8,128)S(1)} collective-permute-done((f32[256,256]{1,0:T(8,128)}, f32[256,256]{1,0:T(8,128)S(1)}, u32[]{:S(2)}, u32[]{:S(2)}) %collective-permute-start.5) | collective-permute-done | bytes 262176 | tf_op jit(solution)/shard_map/ppermute | solution.py:40
  42.2 2.2 %collective-permute-start.6 = (f32[256,256]{1,0:T(8,128)S(1)}, f32[256,256]{1,0:T(8,128)S(1)}, u32[]{:S(2)}, u32[]{:S(2)}) collective-permute-start(f32[256,256]{1,0:T(8,128)S(1)} %add.97), channel_id=1, source_target_pairs={{0,2},{1,3},{2,0},{3,1},{4,6},{5,7},{6,4},{7,5},{8,10},{9,11},{10,... | collective-permute-start | bytes 786440 | tf_op jit(solution)/shard_map/ppermute | solution.py:42
  45.9 3.0 %collective-permute-start.4 = (f32[256,256]{1,0:T(8,128)S(1)}, f32[256,256]{1,0:T(8,128)S(1)}, u32[]{:S(2)}, u32[]{:S(2)}) collective-permute-start(f32[256,256]{1,0:T(8,128)S(1)} %add.95), channel_id=1, source_target_pairs={{0,6},{1,7},{2,4},{3,5},{4,2},{5,3},{6,0},{7,1},{8,14},{9,15},{10,... | collective-permute-start | bytes 786440 | tf_op jit(solution)/shard_map/ppermute | solution.py:41
  51.2 4.1 %collective-permute-done.4 = f32[256,256]{1,0:T(8,128)S(1)} collective-permute-done((f32[256,256]{1,0:T(8,128)S(1)}, f32[256,256]{1,0:T(8,128)S(1)}, u32[]{:S(2)}, u32[]{:S(2)}) %collective-permute-start.4) | collective-permute-done | bytes 262176 | tf_op jit(solution)/shard_map/ppermute | solution.py:41
  56.1 9.0 %shard_map.65 = (f32[384,512]{1,0:T(8,128)}, f32[432,512]{1,0:T(8,128)}, f32[48,512]{1,0:T(8,128)}) custom-call(s32[3]{0:T(128)} %roff.3, s32[3]{0:T(128)} %coff.3, s32[1]{0:T(128)S(6)} %copy.25.cnt, s32[2]{0:T(128)} %pad_add_fusion.core, bf16[2,2,2,256,256]{4,3,2,1,0:T(8,128)(2,1)} %get-tuple-element.12.exit_ref, ...), custom_call_target="tpu_custom_call" | custom-call | flops 1073741824 | bytes 12582912 | tf_op jit(solution)/shard_map/pallas_call | solution.py:277
  65.1 1.9 %collective-permute-start.7 = (f32[432,512]{1,0:T(8,128)}, f32[432,512]{1,0:T(8,128)S(1)}, u32[]{:S(2)}, u32[]{:S(2)}) collective-permute-start(f32[432,512]{1,0:T(8,128)} %get-tuple-element.17), channel_id=1, source_target_pairs={{0,1},{1,0},{2,3},{3,2},{4,5},{5,4},{6,7},{7,6},{8,9},{9,8},{10,11... | collective-permute-start | bytes 2654216 | tf_op jit(solution)/shard_map/ppermute | solution.py:345
  67.0 2.6 %collective-permute-done.7 = f32[432,512]{1,0:T(8,128)S(1)} collective-permute-done((f32[432,512]{1,0:T(8,128)}, f32[432,512]{1,0:T(8,128)S(1)}, u32[]{:S(2)}, u32[]{:S(2)}) %collective-permute-start.7) | collective-permute-done | bytes 884768 | tf_op jit(solution)/shard_map/ppermute | solution.py:345
  71.9 1.9 %collective-permute-start.8 = (f32[144,512]{1,0:T(8,128)S(1)}, f32[144,512]{1,0:T(8,128)S(1)}, u32[]{:S(2)}, u32[]{:S(2)}) collective-permute-start(f32[144,512]{1,0:T(8,128)S(1)} %pad_maximum_fusion), channel_id=1, source_target_pairs={{0,8},{8,16},{16,24},{24,32},{32,40},{40,48},{48,56},{56,64},{64,7... | collective-permute-start | bytes 884744 | tf_op jit(solution)/shard_map/ppermute | solution.py:353
  73.9 3.9 %collective-permute-start.9 = (f32[144,512]{1,0:T(8,128)S(1)}, f32[144,512]{1,0:T(8,128)S(1)}, u32[]{:S(2)}, u32[]{:S(2)}) collective-permute-start(f32[144,512]{1,0:T(8,128)S(1)} %pad_maximum_fusion.1), channel_id=1, source_target_pairs={{8,0},{16,8},{24,16},{32,24},{40,32},{48,40},{56,48},{64,56},{72,6... | collective-permute-start | bytes 884744 | tf_op jit(solution)/shard_map/ppermute | solution.py:354
  77.9 5.0 %collective-permute-done.8 = f32[144,512]{1,0:T(8,128)S(1)} collective-permute-done((f32[144,512]{1,0:T(8,128)S(1)}, f32[144,512]{1,0:T(8,128)S(1)}, u32[]{:S(2)}, u32[]{:S(2)}) %collective-permute-start.8) | collective-permute-done | bytes 294944 | tf_op jit(solution)/shard_map/ppermute | solution.py:353
  83.6 4.6 %collective-permute-done.9 = f32[144,512]{1,0:T(8,128)S(1)} collective-permute-done((f32[144,512]{1,0:T(8,128)S(1)}, f32[144,512]{1,0:T(8,128)S(1)}, u32[]{:S(2)}, u32[]{:S(2)}) %collective-permute-start.9) | collective-permute-done | bytes 294944 | tf_op jit(solution)/shard_map/ppermute | solution.py:354
  89.2 3.1 %collective-permute-start.10 = (f32[2,2,16,512]{3,2,1,0:T(8,128)S(1)}, f32[2,2,16,512]{3,2,1,0:T(8,128)S(1)}, u32[]{:S(2)}, u32[]{:S(2)}) collective-permute-start(f32[2,2,16,512]{3,2,1,0:T(8,128)S(1)} %dynamic-slice_bitcast_fusion), channel_id=1, source_target_pairs={{0,6},{1,7},{2,4},{3,5},{4,2},{5,3},{6,0},{7,1},{8,14},{9,15},{10,... | collective-permute-start | bytes 393224 | tf_op jit(solution)/shard_map/ppermute | solution.py:365
  92.4 5.1 %collective-permute-done.10 = f32[2,2,16,512]{3,2,1,0:T(8,128)S(1)} collective-permute-done((f32[2,2,16,512]{3,2,1,0:T(8,128)S(1)}, f32[2,2,16,512]{3,2,1,0:T(8,128)S(1)}, u32[]{:S(2)}, u32[]{:S(2)}) %collective-permute-start.10) | collective-permute-done | bytes 131104 | tf_op jit(solution)/shard_map/ppermute | solution.py:365
  97.5 1.9 %collective-permute-start.11 = (f32[2,16,512]{2,1,0:T(8,128)S(1)}, f32[2,16,512]{2,1,0:T(8,128)S(1)}, u32[]{:S(2)}, u32[]{:S(2)}) collective-permute-start(f32[2,16,512]{2,1,0:T(8,128)S(1)} %dynamic-slice_bitcast_fusion.1), channel_id=1, source_target_pairs={{0,2},{1,3},{2,0},{3,1},{4,6},{5,7},{6,4},{7,5},{8,10},{9,11},{10,... | collective-permute-start | bytes 196616 | tf_op jit(solution)/shard_map/ppermute | solution.py:365
  99.4 4.2 %collective-permute-done.11 = f32[2,16,512]{2,1,0:T(8,128)S(1)} collective-permute-done((f32[2,16,512]{2,1,0:T(8,128)S(1)}, f32[2,16,512]{2,1,0:T(8,128)S(1)}, u32[]{:S(2)}, u32[]{:S(2)}) %collective-permute-start.11) | collective-permute-done | bytes 65568 | tf_op jit(solution)/shard_map/ppermute | solution.py:365
  (35 shorter events, 12.5 us)
Async XLA Ops:
  0.0 10.8 %collective-permute-start.2 = (f32[2,256,256]{2,1,0:T(8,128)}, f32[2,256,256]{2,1,0:T(8,128)S(1)}, u32[]{:S(2)}, u32[]{:S(2)}) collective-permute-start(f32[2,256,256]{2,1,0:T(8,128)} %bitcast.35), channel_id=1, source_target_pairs={{0,1},{1,0},{2,3},{3,2},{4,5},{5,4},{6,7},{7,6},{8,9},{9,8},{10,11... | collective-permute-start | bytes 1572872 | tf_op jit(solution)/shard_map/ppermute | solution.py:328
  1.9 16.4 %collective-permute-start = (f32[2,128,512]{2,1,0:T(8,128)}, f32[2,128,512]{2,1,0:T(8,128)S(1)}, u32[]{:S(2)}, u32[]{:S(2)}) collective-permute-start(f32[2,128,512]{2,1,0:T(8,128)} %own_ref.1), channel_id=1, source_target_pairs={{0,8},{8,16},{16,24},{24,32},{32,40},{40,48},{48,56},{56,64},{64,7... | collective-permute-start | bytes 1572872 | tf_op jit(solution)/shard_map/ppermute | solution.py:326
  4.5 19.5 %collective-permute-start.1 = (f32[2,128,512]{2,1,0:T(8,128)}, f32[2,128,512]{2,1,0:T(8,128)S(1)}, u32[]{:S(2)}, u32[]{:S(2)}) collective-permute-start(f32[2,128,512]{2,1,0:T(8,128)} %own_ref.1), channel_id=1, source_target_pairs={{8,0},{16,8},{24,16},{32,24},{40,32},{48,40},{56,48},{64,56},{72,6... | collective-permute-start | bytes 1572872 | tf_op jit(solution)/shard_map/ppermute | solution.py:327
  10.8 13.2 %copy-start.2 = (f32[2,256,256]{2,1,0:T(8,128)}, f32[2,256,256]{2,1,0:T(8,128)S(1)}, u32[]{:S(2)}) copy-start(f32[2,256,256]{2,1,0:T(8,128)S(1)} %collective-permute-done.2.pb_ref) | copy-start | bytes 1572868
  18.4 5.6 %copy-start.4 = (f32[2,128,512]{2,1,0:T(8,128)}, f32[2,128,512]{2,1,0:T(8,128)S(1)}, u32[]{:S(2)}) copy-start(f32[2,128,512]{2,1,0:T(8,128)S(1)} %collective-permute-done.before_ref) | copy-start | bytes 1572868
  24.0 0.8 copy-start.5
  31.5 9.7 %collective-permute-start.5 = (f32[256,256]{1,0:T(8,128)}, f32[256,256]{1,0:T(8,128)S(1)}, u32[]{:S(2)}, u32[]{:S(2)}) collective-permute-start(f32[256,256]{1,0:T(8,128)} %get-tuple-element.15), channel_id=1, source_target_pairs={{0,6},{1,7},{2,4},{3,5},{4,2},{5,3},{6,0},{7,1},{8,14},{9,15},{10,... | collective-permute-start | bytes 786440 | tf_op jit(solution)/shard_map/ppermute | solution.py:40
  36.2 9.7 %copy-start.3 = (f32[256,256]{1,0:T(8,128)S(1)}, f32[256,256]{1,0:T(8,128)}, u32[]{:S(2)}) copy-start(f32[256,256]{1,0:T(8,128)} %get-tuple-element.14) | copy-start | bytes 786436
  36.2 9.7 %collective-permute-start.3 = (f32[256,256]{1,0:T(8,128)}, f32[256,256]{1,0:T(8,128)S(1)}, u32[]{:S(2)}, u32[]{:S(2)}) collective-permute-start(f32[256,256]{1,0:T(8,128)} %get-tuple-element.14), channel_id=1, source_target_pairs={{0,2},{1,3},{2,0},{3,1},{4,6},{5,7},{6,4},{7,5},{8,10},{9,11},{10,... | collective-permute-start | bytes 786440 | tf_op jit(solution)/shard_map/ppermute | solution.py:39
  42.2 8.3 %collective-permute-start.6 = (f32[256,256]{1,0:T(8,128)S(1)}, f32[256,256]{1,0:T(8,128)S(1)}, u32[]{:S(2)}, u32[]{:S(2)}) collective-permute-start(f32[256,256]{1,0:T(8,128)S(1)} %add.97), channel_id=1, source_target_pairs={{0,2},{1,3},{2,0},{3,1},{4,6},{5,7},{6,4},{7,5},{8,10},{9,11},{10,... | collective-permute-start | bytes 786440 | tf_op jit(solution)/shard_map/ppermute | solution.py:42
  45.9 9.5 %collective-permute-start.4 = (f32[256,256]{1,0:T(8,128)S(1)}, f32[256,256]{1,0:T(8,128)S(1)}, u32[]{:S(2)}, u32[]{:S(2)}) collective-permute-start(f32[256,256]{1,0:T(8,128)S(1)} %add.95), channel_id=1, source_target_pairs={{0,6},{1,7},{2,4},{3,5},{4,2},{5,3},{6,0},{7,1},{8,14},{9,15},{10,... | collective-permute-start | bytes 786440 | tf_op jit(solution)/shard_map/ppermute | solution.py:41
  65.1 4.5 %collective-permute-start.7 = (f32[432,512]{1,0:T(8,128)}, f32[432,512]{1,0:T(8,128)S(1)}, u32[]{:S(2)}, u32[]{:S(2)}) collective-permute-start(f32[432,512]{1,0:T(8,128)} %get-tuple-element.17), channel_id=1, source_target_pairs={{0,1},{1,0},{2,3},{3,2},{4,5},{5,4},{6,7},{7,6},{8,9},{9,8},{10,11... | collective-permute-start | bytes 2654216 | tf_op jit(solution)/shard_map/ppermute | solution.py:345
  71.9 10.9 %collective-permute-start.8 = (f32[144,512]{1,0:T(8,128)S(1)}, f32[144,512]{1,0:T(8,128)S(1)}, u32[]{:S(2)}, u32[]{:S(2)}) collective-permute-start(f32[144,512]{1,0:T(8,128)S(1)} %pad_maximum_fusion), channel_id=1, source_target_pairs={{0,8},{8,16},{16,24},{24,32},{32,40},{40,48},{48,56},{56,64},{64,7... | collective-permute-start | bytes 884744 | tf_op jit(solution)/shard_map/ppermute | solution.py:353
  73.9 14.3 %collective-permute-start.9 = (f32[144,512]{1,0:T(8,128)S(1)}, f32[144,512]{1,0:T(8,128)S(1)}, u32[]{:S(2)}, u32[]{:S(2)}) collective-permute-start(f32[144,512]{1,0:T(8,128)S(1)} %pad_maximum_fusion.1), channel_id=1, source_target_pairs={{8,0},{16,8},{24,16},{32,24},{40,32},{48,40},{56,48},{64,56},{72,6... | collective-permute-start | bytes 884744 | tf_op jit(solution)/shard_map/ppermute | solution.py:354
  82.9 0.7 copy-start
  88.2 1.0 slice-start
  89.2 10.2 %copy-start.1 = (f32[144,512]{1,0:T(8,128)S(1)}, f32[144,512]{1,0:T(8,128)}, u32[]{:S(2)}) copy-start(f32[144,512]{1,0:T(8,128)} %copy-done) | copy-start | bytes 884740
  89.2 8.2 %collective-permute-start.10 = (f32[2,2,16,512]{3,2,1,0:T(8,128)S(1)}, f32[2,2,16,512]{3,2,1,0:T(8,128)S(1)}, u32[]{:S(2)}, u32[]{:S(2)}) collective-permute-start(f32[2,2,16,512]{3,2,1,0:T(8,128)S(1)} %dynamic-slice_bitcast_fusion), channel_id=1, source_target_pairs={{0,6},{1,7},{2,4},{3,5},{4,2},{5,3},{6,0},{7,1},{8,14},{9,15},{10,... | collective-permute-start | bytes 393224 | tf_op jit(solution)/shard_map/ppermute | solution.py:365
  97.5 6.2 %collective-permute-start.11 = (f32[2,16,512]{2,1,0:T(8,128)S(1)}, f32[2,16,512]{2,1,0:T(8,128)S(1)}, u32[]{:S(2)}, u32[]{:S(2)}) collective-permute-start(f32[2,16,512]{2,1,0:T(8,128)S(1)} %dynamic-slice_bitcast_fusion.1), channel_id=1, source_target_pairs={{0,2},{1,3},{2,0},{3,1},{4,6},{5,7},{6,4},{7,5},{8,10},{9,11},{10,... | collective-permute-start | bytes 196616 | tf_op jit(solution)/shard_map/ppermute | solution.py:365

commit v9 on v8

--- a/solution.py
+++ b/solution.py
@@ -358,11 +358,19 @@
         + from_next[:band_rows].reshape(blocks[:, 1].shape)
     )
     illum_rows = own_illum[1] + from_prev[band_rows:] + from_next[band_rows:]
-    for pairs, d in ((far, 4), (near, 2)):
-        bit = (my_mode // d) % 2
-        keep = lax.dynamic_index_in_dim(tile, bit, axis=1, keepdims=False)
-        send = lax.dynamic_index_in_dim(tile, 1 - bit, axis=1, keepdims=False)
-        tile = keep + lax.ppermute(send, "mode", pairs)
+    chip = my_mode // 2
+    hi = chip // 2
+    lo = chip % 2
+    across = [(i, i ^ 4) for i in range(mode_count)]
+
+    def block(a, b):
+        rows = lax.dynamic_index_in_dim(tile, a, axis=1, keepdims=False)
+        return lax.dynamic_index_in_dim(rows, b, axis=1, keepdims=False)
+
+    from_near = lax.ppermute(block(hi, 1 - lo), "mode", near)
+    from_far = lax.ppermute(block(1 - hi, 1 - lo), "mode", far)
+    from_across = lax.ppermute(block(1 - hi, lo), "mode", across)
+    tile = block(hi, lo) + from_near + from_far + from_across
 
     start = my_mode * share_rows
     own_rows = lax.dynamic_slice_in_dim(object_field, start, share_rows, 1)

time: 106 us -> 106 us (level)
  the two profiles are of different devices: /device:TPU:376 before, /device:TPU:248 now
where the time goes in v9:
time: 106 us
  starting transfers between devices  40.9 us (39%)
  waiting for transfers between devices  40.4 us (38%)
  Pallas kernels  12.2 us (12%)
  other arithmetic  7.8 us (7%)
  local copies, waits for them, and re-layouts  3.37 us (3%)
    ppermute x1, waiting for transfers between devices, local(): after = lax.ppermute(object_field, 'pos', neighbour_pairs(pos_count, -1))  7.33 us
    ppermute x1, waiting for transfers between devices, local(): before = lax.ppermute(object_field, 'pos', neighbour_pairs(pos_count, 1))  7.14 us
    ppermute x1, waiting for transfers between devices, local(): from_next = lax.ppermute(to_prev, 'pos', neighbour_pairs(pos_count, -1))  6.76 us
    pallas_call x1, Pallas kernels, run_backward(): pl.pallas_call(backward_kernel, grid_spec=pltpu.PrefetchScalarGridSpec(nu...  6.63 us
    pallas_call x1, Pallas kernels, run_forward(): pl.pallas_call(forward_kernel, grid_spec=pltpu.PrefetchScalarGridSpec(num...  5.54 us
    ppermute x1, starting transfers between devices, local(): from_prev = lax.ppermute(to_next, 'pos', neighbour_pairs(pos_count, 1))  5.18 us
    ppermute x1, starting transfers between devices, local(): before = lax.ppermute(object_field, 'pos', neighbour_pairs(pos_count, 1))  4.7 us
    ppermute x1, starting transfers between devices, allreduce_chips(): qb = qb + lax.ppermute(qb, 'mode', far)  4.67 us
  transfers between devices with their start and end apart: 13, of which 10 were waited for; matrix products, arithmetic and copies ran while one was open for 4% of the time, Pallas kernels for 0%

profile of v9, /device:TPU:248, one launch (start us, length us, event | category | flops | bytes accessed | tf_op | source)
XLA Modules:
  0.0 105.6 jit_solution(2543459688309103307)
XLA Ops:
  0.0 1.9 %collective-permute-start.2 = (f32[2,256,256]{2,1,0:T(8,128)}, f32[2,256,256]{2,1,0:T(8,128)S(1)}, u32[]{:S(2)}, u32[]{:S(2)}) collective-permute-start(f32[2,256,256]{2,1,0:T(8,128)} %bitcast.42), channel_id=1, source_target_pairs={{0,1},{1,0},{2,3},{3,2},{4,5},{5,4},{6,7},{7,6},{8,9},{9,8},{10,11... | collective-permute-start | bytes 1572872 | tf_op jit(solution)/shard_map/ppermute | solution.py:328
  1.9 4.7 %collective-permute-start = (f32[2,128,512]{2,1,0:T(8,128)}, f32[2,128,512]{2,1,0:T(8,128)S(1)}, u32[]{:S(2)}, u32[]{:S(2)}) collective-permute-start(f32[2,128,512]{2,1,0:T(8,128)} %own_ref.1), channel_id=1, source_target_pairs={{0,8},{8,16},{16,24},{24,32},{32,40},{40,48},{48,56},{56,64},{64,7... | collective-permute-start | bytes 1572872 | tf_op jit(solution)/shard_map/ppermute | solution.py:326
  6.6 1.9 %collective-permute-start.1 = (f32[2,128,512]{2,1,0:T(8,128)}, f32[2,128,512]{2,1,0:T(8,128)S(1)}, u32[]{:S(2)}, u32[]{:S(2)}) collective-permute-start(f32[2,128,512]{2,1,0:T(8,128)} %own_ref.1), channel_id=1, source_target_pairs={{8,0},{16,8},{24,16},{32,24},{40,32},{48,40},{56,48},{64,56},{72,6... | collective-permute-start | bytes 1572872 | tf_op jit(solution)/shard_map/ppermute | solution.py:327
  11.6 7.1 %collective-permute-done.before_ref = f32[2,128,512]{2,1,0:T(8,128)S(1)} collective-permute-done((f32[2,128,512]{2,1,0:T(8,128)}, f32[2,128,512]{2,1,0:T(8,128)S(1)}, u32[]{:S(2)}, u32[]{:S(2)}) %collective-permute-start) | collective-permute-done | bytes 524320 | tf_op jit(solution)/shard_map/ppermute | solution.py:326
  18.8 7.3 %collective-permute-done.1.after_ref = f32[2,128,512]{2,1,0:T(8,128)S(1)} collective-permute-done((f32[2,128,512]{2,1,0:T(8,128)}, f32[2,128,512]{2,1,0:T(8,128)S(1)}, u32[]{:S(2)}, u32[]{:S(2)}) %collective-permute-start.1) | collective-permute-done | bytes 524320 | tf_op jit(solution)/shard_map/ppermute | solution.py:327
  26.9 5.5 %shard_map.64 = (bf16[2,2,2,256,256]{4,3,2,1,0:T(8,128)(2,1)}, bf16[2,2,2,256,256]{4,3,2,1,0:T(8,128)(2,1)}, f32[256,256]{1,0:T(8,128)}, f32[256,256]{1,0:T(8,128)}) custom-call(s32[3]{0:T(128)} %roff.3, s32[3]{0:T(128)} %coff.3, s32[1]{0:T(128)S(6)} %copy.13.cnt, s32[2]{0:T(128)} %pad_add_fusion.core, f32[2,128,512]{2,1,0:T(8,128)} %copy-done.5, ...), custom_call_target="tpu_custom_call" | custom-call | flops 1073741824 | bytes 10485760 | tf_op jit(solution)/shard_map/pallas_call | solution.py:232
  32.4 4.7 %collective-permute-start.5 = (f32[256,256]{1,0:T(8,128)}, f32[256,256]{1,0:T(8,128)S(1)}, u32[]{:S(2)}, u32[]{:S(2)}) collective-permute-start(f32[256,256]{1,0:T(8,128)} %get-tuple-element.15), channel_id=1, source_target_pairs={{0,6},{1,7},{2,4},{3,5},{4,2},{5,3},{6,0},{7,1},{8,14},{9,15},{10,... | collective-permute-start | bytes 786440 | tf_op jit(solution)/shard_map/ppermute | solution.py:40
  37.1 2.3 %collective-permute-start.3 = (f32[256,256]{1,0:T(8,128)}, f32[256,256]{1,0:T(8,128)S(1)}, u32[]{:S(2)}, u32[]{:S(2)}) collective-permute-start(f32[256,256]{1,0:T(8,128)} %get-tuple-element.14), channel_id=1, source_target_pairs={{0,2},{1,3},{2,0},{3,1},{4,6},{5,7},{6,4},{7,5},{8,10},{9,11},{10,... | collective-permute-start | bytes 786440 | tf_op jit(solution)/shard_map/ppermute | solution.py:39
  39.4 4.0 %collective-permute-done.5 = f32[256,256]{1,0:T(8,128)S(1)} collective-permute-done((f32[256,256]{1,0:T(8,128)}, f32[256,256]{1,0:T(8,128)S(1)}, u32[]{:S(2)}, u32[]{:S(2)}) %collective-permute-start.5) | collective-permute-done | bytes 262176 | tf_op jit(solution)/shard_map/ppermute | solution.py:40
  44.3 2.2 %collective-permute-start.6 = (f32[256,256]{1,0:T(8,128)S(1)}, f32[256,256]{1,0:T(8,128)S(1)}, u32[]{:S(2)}, u32[]{:S(2)}) collective-permute-start(f32[256,256]{1,0:T(8,128)S(1)} %add.121), channel_id=1, source_target_pairs={{0,2},{1,3},{2,0},{3,1},{4,6},{5,7},{6,4},{7,5},{8,10},{9,11},{10,... | collective-permute-start | bytes 786440 | tf_op jit(solution)/shard_map/ppermute | solution.py:42
  46.7 4.3 %collective-permute-start.4 = (f32[256,256]{1,0:T(8,128)S(1)}, f32[256,256]{1,0:T(8,128)S(1)}, u32[]{:S(2)}, u32[]{:S(2)}) collective-permute-start(f32[256,256]{1,0:T(8,128)S(1)} %add.119), channel_id=1, source_target_pairs={{0,6},{1,7},{2,4},{3,5},{4,2},{5,3},{6,0},{7,1},{8,14},{9,15},{10,... | collective-permute-start | bytes 786440 | tf_op jit(solution)/shard_map/ppermute | solution.py:41
  51.0 1.9 %collective-permute-done.6 = f32[256,256]{1,0:T(8,128)S(1)} collective-permute-done((f32[256,256]{1,0:T(8,128)S(1)}, f32[256,256]{1,0:T(8,128)S(1)}, u32[]{:S(2)}, u32[]{:S(2)}) %collective-permute-start.6) | collective-permute-done | bytes 262176 | tf_op jit(solution)/shard_map/ppermute | solution.py:42
  53.7 2.6 %collective-permute-done.4 = f32[256,256]{1,0:T(8,128)S(1)} collective-permute-done((f32[256,256]{1,0:T(8,128)S(1)}, f32[256,256]{1,0:T(8,128)S(1)}, u32[]{:S(2)}, u32[]{:S(2)}) %collective-permute-start.4) | collective-permute-done | bytes 262176 | tf_op jit(solution)/shard_map/ppermute | solution.py:41
  57.0 6.6 %shard_map.65 = (f32[384,512]{1,0:T(8,128)}, f32[432,512]{1,0:T(8,128)}, f32[48,512]{1,0:T(8,128)}) custom-call(s32[3]{0:T(128)} %roff.3, s32[3]{0:T(128)} %coff.3, s32[1]{0:T(128)S(6)} %copy.13.cnt, s32[2]{0:T(128)} %pad_add_fusion.core, bf16[2,2,2,256,256]{4,3,2,1,0:T(8,128)(2,1)} %get-tuple-element.12.exit_ref, ...), custom_call_target="tpu_custom_call" | custom-call | flops 1073741824 | bytes 12582912 | tf_op jit(solution)/shard_map/pallas_call | solution.py:277
  63.6 1.9 %collective-permute-start.7 = (f32[432,512]{1,0:T(8,128)}, f32[432,512]{1,0:T(8,128)S(1)}, u32[]{:S(2)}, u32[]{:S(2)}) collective-permute-start(f32[432,512]{1,0:T(8,128)} %get-tuple-element.17), channel_id=1, source_target_pairs={{0,1},{1,0},{2,3},{3,2},{4,5},{5,4},{6,7},{7,6},{8,9},{9,8},{10,11... | collective-permute-start | bytes 2654216 | tf_op jit(solution)/shard_map/ppermute | solution.py:345
  65.5 2.6 %collective-permute-done.7 = f32[432,512]{1,0:T(8,128)S(1)} collective-permute-done((f32[432,512]{1,0:T(8,128)}, f32[432,512]{1,0:T(8,128)S(1)}, u32[]{:S(2)}, u32[]{:S(2)}) %collective-permute-start.7) | collective-permute-done | bytes 884768 | tf_op jit(solution)/shard_map/ppermute | solution.py:345
  70.3 5.2 %collective-permute-start.8 = (f32[144,512]{1,0:T(8,128)S(1)}, f32[144,512]{1,0:T(8,128)S(1)}, u32[]{:S(2)}, u32[]{:S(2)}) collective-permute-start(f32[144,512]{1,0:T(8,128)S(1)} %pad_maximum_fusion), channel_id=1, source_target_pairs={{0,8},{8,16},{16,24},{24,32},{32,40},{40,48},{48,56},{56,64},{64,7... | collective-permute-start | bytes 884744 | tf_op jit(solution)/shard_map/ppermute | solution.py:353
  75.6 1.9 %collective-permute-start.9 = (f32[144,512]{1,0:T(8,128)S(1)}, f32[144,512]{1,0:T(8,128)S(1)}, u32[]{:S(2)}, u32[]{:S(2)}) collective-permute-start(f32[144,512]{1,0:T(8,128)S(1)} %pad_maximum_fusion.1), channel_id=1, source_target_pairs={{8,0},{16,8},{24,16},{32,24},{40,32},{48,40},{56,48},{64,56},{72,6... | collective-permute-start | bytes 884744 | tf_op jit(solution)/shard_map/ppermute | solution.py:354
  77.6 4.5 %collective-permute-done.8 = f32[144,512]{1,0:T(8,128)S(1)} collective-permute-done((f32[144,512]{1,0:T(8,128)S(1)}, f32[144,512]{1,0:T(8,128)S(1)}, u32[]{:S(2)}, u32[]{:S(2)}) %collective-permute-start.8) | collective-permute-done | bytes 294944 | tf_op jit(solution)/shard_map/ppermute | solution.py:353
  82.8 6.8 %collective-permute-done.9 = f32[144,512]{1,0:T(8,128)S(1)} collective-permute-done((f32[144,512]{1,0:T(8,128)S(1)}, f32[144,512]{1,0:T(8,128)S(1)}, u32[]{:S(2)}, u32[]{:S(2)}) %collective-permute-start.9) | collective-permute-done | bytes 294944 | tf_op jit(solution)/shard_map/ppermute | solution.py:354
  90.6 2.1 %collective-permute-start.10 = (f32[2,16,512]{2,1,0:T(8,128)S(1)}, f32[2,16,512]{2,1,0:T(8,128)S(1)}, u32[]{:S(2)}, u32[]{:S(2)}) collective-permute-start(f32[2,16,512]{2,1,0:T(8,128)S(1)} %get-tuple-element.21), channel_id=1, source_target_pairs={{0,2},{1,3},{2,0},{3,1},{4,6},{5,7},{6,4},{7,5},{8,10},{9,11},{10,... | collective-permute-start | bytes 196616 | tf_op jit(solution)/shard_map/ppermute | solution.py:370
  92.7 3.8 %collective-permute-start.11 = (f32[2,16,512]{2,1,0:T(8,128)S(1)}, f32[2,16,512]{2,1,0:T(8,128)S(1)}, u32[]{:S(2)}, u32[]{:S(2)}) collective-permute-start(f32[2,16,512]{2,1,0:T(8,128)S(1)} %get-tuple-element.23), channel_id=1, source_target_pairs={{0,6},{1,7},{2,4},{3,5},{4,2},{5,3},{6,0},{7,1},{8,14},{9,15},{10,... | collective-permute-start | bytes 196616 | tf_op jit(solution)/shard_map/ppermute | solution.py:371
  96.5 4.1 %collective-permute-start.12 = (f32[2,16,512]{2,1,0:T(8,128)S(1)}, f32[2,16,512]{2,1,0:T(8,128)S(1)}, u32[]{:S(2)}, u32[]{:S(2)}) collective-permute-start(f32[2,16,512]{2,1,0:T(8,128)S(1)} %get-tuple-element.22), channel_id=1, source_target_pairs={{0,4},{1,5},{2,6},{3,7},{4,0},{5,1},{6,2},{7,3},{8,12},{9,13},{10,... | collective-permute-start | bytes 196616 | tf_op jit(solution)/shard_map/ppermute | solution.py:372
  100.6 3.5 %collective-permute-done.12 = f32[2,16,512]{2,1,0:T(8,128)S(1)} collective-permute-done((f32[2,16,512]{2,1,0:T(8,128)S(1)}, f32[2,16,512]{2,1,0:T(8,128)S(1)}, u32[]{:S(2)}, u32[]{:S(2)}) %collective-permute-start.12) | collective-permute-done | bytes 65568 | tf_op jit(solution)/shard_map/ppermute | solution.py:372
  (37 shorter events, 11.3 us)
Async XLA Ops:
  0.0 11.6 %collective-permute-start.2 = (f32[2,256,256]{2,1,0:T(8,128)}, f32[2,256,256]{2,1,0:T(8,128)S(1)}, u32[]{:S(2)}, u32[]{:S(2)}) collective-permute-start(f32[2,256,256]{2,1,0:T(8,128)} %bitcast.42), channel_id=1, source_target_pairs={{0,1},{1,0},{2,3},{3,2},{4,5},{5,4},{6,7},{7,6},{8,9},{9,8},{10,11... | collective-permute-start | bytes 1572872 | tf_op jit(solution)/shard_map/ppermute | solution.py:328
  1.9 16.8 %collective-permute-start = (f32[2,128,512]{2,1,0:T(8,128)}, f32[2,128,512]{2,1,0:T(8,128)S(1)}, u32[]{:S(2)}, u32[]{:S(2)}) collective-permute-start(f32[2,128,512]{2,1,0:T(8,128)} %own_ref.1), channel_id=1, source_target_pairs={{0,8},{8,16},{16,24},{24,32},{32,40},{40,48},{48,56},{56,64},{64,7... | collective-permute-start | bytes 1572872 | tf_op jit(solution)/shard_map/ppermute | solution.py:326
  6.6 19.5 %collective-permute-start.1 = (f32[2,128,512]{2,1,0:T(8,128)}, f32[2,128,512]{2,1,0:T(8,128)S(1)}, u32[]{:S(2)}, u32[]{:S(2)}) collective-permute-start(f32[2,128,512]{2,1,0:T(8,128)} %own_ref.1), channel_id=1, source_target_pairs={{8,0},{16,8},{24,16},{32,24},{40,32},{48,40},{56,48},{64,56},{72,6... | collective-permute-start | bytes 1572872 | tf_op jit(solution)/shard_map/ppermute | solution.py:327
  11.6 14.5 %copy-start.2 = (f32[2,256,256]{2,1,0:T(8,128)}, f32[2,256,256]{2,1,0:T(8,128)S(1)}, u32[]{:S(2)}) copy-start(f32[2,256,256]{2,1,0:T(8,128)S(1)} %collective-permute-done.2.pb_ref) | copy-start | bytes 1572868
  18.8 7.3 %copy-start.5 = (f32[2,128,512]{2,1,0:T(8,128)}, f32[2,128,512]{2,1,0:T(8,128)S(1)}, u32[]{:S(2)}) copy-start(f32[2,128,512]{2,1,0:T(8,128)S(1)} %collective-permute-done.before_ref) | copy-start | bytes 1572868
  26.1 0.8 copy-start.6
  32.4 10.9 %collective-permute-start.5 = (f32[256,256]{1,0:T(8,128)}, f32[256,256]{1,0:T(8,128)S(1)}, u32[]{:S(2)}, u32[]{:S(2)}) collective-permute-start(f32[256,256]{1,0:T(8,128)} %get-tuple-element.15), channel_id=1, source_target_pairs={{0,6},{1,7},{2,4},{3,5},{4,2},{5,3},{6,0},{7,1},{8,14},{9,15},{10,... | collective-permute-start | bytes 786440 | tf_op jit(solution)/shard_map/ppermute | solution.py:40
  37.1 9.6 %copy-start.3 = (f32[256,256]{1,0:T(8,128)S(1)}, f32[256,256]{1,0:T(8,128)}, u32[]{:S(2)}) copy-start(f32[256,256]{1,0:T(8,128)} %get-tuple-element.14) | copy-start | bytes 786436
  37.1 9.6 %collective-permute-start.3 = (f32[256,256]{1,0:T(8,128)}, f32[256,256]{1,0:T(8,128)S(1)}, u32[]{:S(2)}, u32[]{:S(2)}) collective-permute-start(f32[256,256]{1,0:T(8,128)} %get-tuple-element.14), channel_id=1, source_target_pairs={{0,2},{1,3},{2,0},{3,1},{4,6},{5,7},{6,4},{7,5},{8,10},{9,11},{10,... | collective-permute-start | bytes 786440 | tf_op jit(solution)/shard_map/ppermute | solution.py:39
  44.3 8.6 %collective-permute-start.6 = (f32[256,256]{1,0:T(8,128)S(1)}, f32[256,256]{1,0:T(8,128)S(1)}, u32[]{:S(2)}, u32[]{:S(2)}) collective-permute-start(f32[256,256]{1,0:T(8,128)S(1)} %add.121), channel_id=1, source_target_pairs={{0,2},{1,3},{2,0},{3,1},{4,6},{5,7},{6,4},{7,5},{8,10},{9,11},{10,... | collective-permute-start | bytes 786440 | tf_op jit(solution)/shard_map/ppermute | solution.py:42
  46.7 9.5 %collective-permute-start.4 = (f32[256,256]{1,0:T(8,128)S(1)}, f32[256,256]{1,0:T(8,128)S(1)}, u32[]{:S(2)}, u32[]{:S(2)}) collective-permute-start(f32[256,256]{1,0:T(8,128)S(1)} %add.119), channel_id=1, source_target_pairs={{0,6},{1,7},{2,4},{3,5},{4,2},{5,3},{6,0},{7,1},{8,14},{9,15},{10,... | collective-permute-start | bytes 786440 | tf_op jit(solution)/shard_map/ppermute | solution.py:41
  63.6 4.5 %collective-permute-start.7 = (f32[432,512]{1,0:T(8,128)}, f32[432,512]{1,0:T(8,128)S(1)}, u32[]{:S(2)}, u32[]{:S(2)}) collective-permute-start(f32[432,512]{1,0:T(8,128)} %get-tuple-element.17), channel_id=1, source_target_pairs={{0,1},{1,0},{2,3},{3,2},{4,5},{5,4},{6,7},{7,6},{8,9},{9,8},{10,11... | collective-permute-start | bytes 2654216 | tf_op jit(solution)/shard_map/ppermute | solution.py:345
  69.4 0.9 copy-start.4
  70.3 11.7 %collective-permute-start.8 = (f32[144,512]{1,0:T(8,128)S(1)}, f32[144,512]{1,0:T(8,128)S(1)}, u32[]{:S(2)}, u32[]{:S(2)}) collective-permute-start(f32[144,512]{1,0:T(8,128)S(1)} %pad_maximum_fusion), channel_id=1, source_target_pairs={{0,8},{8,16},{16,24},{24,32},{32,40},{40,48},{48,56},{56,64},{64,7... | collective-permute-start | bytes 884744 | tf_op jit(solution)/shard_map/ppermute | solution.py:353
  75.6 14.0 %collective-permute-start.9 = (f32[144,512]{1,0:T(8,128)S(1)}, f32[144,512]{1,0:T(8,128)S(1)}, u32[]{:S(2)}, u32[]{:S(2)}) collective-permute-start(f32[144,512]{1,0:T(8,128)S(1)} %pad_maximum_fusion.1), channel_id=1, source_target_pairs={{8,0},{16,8},{24,16},{32,24},{40,32},{48,40},{56,48},{64,56},{72,6... | collective-permute-start | bytes 884744 | tf_op jit(solution)/shard_map/ppermute | solution.py:354
  82.1 0.7 copy-start
  89.5 1.0 slice-start
  90.6 10.0 %copy-start.1 = (f32[144,512]{1,0:T(8,128)S(1)}, f32[144,512]{1,0:T(8,128)}, u32[]{:S(2)}) copy-start(f32[144,512]{1,0:T(8,128)} %copy-done) | copy-start | bytes 884740
  90.6 10.0 %collective-permute-start.10 = (f32[2,16,512]{2,1,0:T(8,128)S(1)}, f32[2,16,512]{2,1,0:T(8,128)S(1)}, u32[]{:S(2)}, u32[]{:S(2)}) collective-permute-start(f32[2,16,512]{2,1,0:T(8,128)S(1)} %get-tuple-element.21), channel_id=1, source_target_pairs={{0,2},{1,3},{2,0},{3,1},{4,6},{5,7},{6,4},{7,5},{8,10},{9,11},{10,... | collective-permute-start | bytes 196616 | tf_op jit(solution)/shard_map/ppermute | solution.py:370
  92.7 8.0 %collective-permute-start.11 = (f32[2,16,512]{2,1,0:T(8,128)S(1)}, f32[2,16,512]{2,1,0:T(8,128)S(1)}, u32[]{:S(2)}, u32[]{:S(2)}) collective-permute-start(f32[2,16,512]{2,1,0:T(8,128)S(1)} %get-tuple-element.23), channel_id=1, source_target_pairs={{0,6},{1,7},{2,4},{3,5},{4,2},{5,3},{6,0},{7,1},{8,14},{9,15},{10,... | collective-permute-start | bytes 196616 | tf_op jit(solution)/shard_map/ppermute | solution.py:371
  96.5 7.7 %collective-permute-start.12 = (f32[2,16,512]{2,1,0:T(8,128)S(1)}, f32[2,16,512]{2,1,0:T(8,128)S(1)}, u32[]{:S(2)}, u32[]{:S(2)}) collective-permute-start(f32[2,16,512]{2,1,0:T(8,128)S(1)} %get-tuple-element.22), channel_id=1, source_target_pairs={{0,4},{1,5},{2,6},{3,7},{4,0},{5,1},{6,2},{7,3},{8,12},{9,13},{10,... | collective-permute-start | bytes 196616 | tf_op jit(solution)/shard_map/ppermute | solution.py:372
